TPU v7x, 512 devices: a whole 4x8x8 slice. The times are simulated.
512 devices in a mesh: ctx: 32 (over y_lo, z, core), tp: 16 (over x, y_hi).
Axes of the slice: x: 4, y: 8 (y_hi: 4, y_lo: 2; y = y_hi * 2 + y_lo), z: 8, core: 2. Of those that a mesh axis runs over, the one named last changes fastest.
Arguments:
- query: bfloat16 [8192, 4096], P('ctx', 'tp'), may hold values from 0.049804688 to 2
- key_feat: bfloat16 [8192, 4096], P('ctx', 'tp'), may hold values from 0.049804688 to 2
- value: bfloat16 [8192, 4096], P('ctx', 'tp'), may hold values from -36 to 36
- grad_out: bfloat16 [8192, 4096], P('ctx', 'tp'), may hold values from -6 to 6
- w_out: bfloat16 [4096, 4096], P('tp', 'ctx'), may hold values from -0.09375 to 0.09375
Outputs:
- grad_query: bfloat16 [8192, 4096], P('ctx', 'tp')
- grad_key: bfloat16 [8192, 4096], P('ctx', 'tp')
- grad_value: bfloat16 [8192, 4096], P('ctx', 'tp')
All inputs are finite; a program needn't handle non-finite values.
Results may differ from a plain program's by a relative error of at most 0.0059.
Values may be sent and summed in bfloat16 or wider, within the bound.
No kernel may reach another device: no remote copies, remote signals or barrier semaphores. Data moves between devices by JAX's collectives and lax.ppermute only.
A program may use at most 64 MiB of HBM per device.

v0:
```python
import jax
import jax.numpy as jnp
from jax import lax
from jax.sharding import PartitionSpec as P

E = 128


epsilon = 1e-06
highest = lax.Precision.HIGHEST


def prefix(value, axis, join, neutral, backward):
    count, mine = (lax.axis_size(axis), lax.axis_index(axis))
    pieces = lax.all_gather(value, axis)
    if backward:
        pieces = pieces[::-1]
        mine = count - 1 - mine
    subtotal = jnp.full_like(value, 0) + jnp.asarray(neutral, value.dtype)

    def lap(position, subtotal):
        longer = join(subtotal, pieces[position])
        return jnp.where(position < mine, longer, subtotal)

    return lax.fori_loop(0, count - 1, lap, subtotal)


def add_states(earlier, later):
    return earlier + later


def local(query, key_feat, value, grad_out, w_out):
    tok_rows = query.shape[0]
    feat_width = query.shape[1]
    head_count = feat_width // E
    full_rows = lax.all_gather(grad_out, "tp", axis=1, tiled=True)
    grad_z = lax.dot_general(
        full_rows,
        lax.all_gather(w_out, "ctx", axis=1, tiled=True),
        (((1,), (1,)), ((), ())),
        preferred_element_type=jnp.float32,
    )
    query_heads = query.reshape(tok_rows, head_count, E)
    key_heads = key_feat.reshape(tok_rows, head_count, E)
    value_heads = value.reshape(tok_rows, head_count, E)
    gradz_heads = grad_z.reshape(tok_rows, head_count, E)
    query_wide = query_heads.astype(jnp.float32)
    key_wide = key_heads.astype(jnp.float32)
    value_wide = value_heads.astype(jnp.float32)
    causal = (
        lax.broadcasted_iota(jnp.int32, (tok_rows, tok_rows), 0)
        >= lax.broadcasted_iota(jnp.int32, (tok_rows, tok_rows), 1)
    )[None]
    scores = jnp.einsum("thd,shd->hts", query_heads, key_heads, preferred_element_type=jnp.float32)
    weights = jnp.where(causal, scores, 0.0)
    local_state = jnp.einsum(
        "shd,she->hde", key_heads, value_heads, preferred_element_type=jnp.float32
    )
    empty_state = jnp.zeros_like(local_state)
    state_in = prefix(local_state, "ctx", add_states, empty_state, False)
    attended = jnp.einsum("hts,she->the", weights, value_wide, precision=highest)
    attended = attended + jnp.einsum("thd,hde->the", query_wide, state_in, precision=highest)
    inv_rms = lax.rsqrt(jnp.mean(attended * attended, axis=-1, keepdims=True) + epsilon)
    normed = attended * inv_rms
    grad_att = (
        inv_rms * (gradz_heads - normed * jnp.mean(gradz_heads * normed, axis=-1, keepdims=True))
    ).astype(jnp.bfloat16)
    grad_wide = grad_att.astype(jnp.float32)
    grad_weights = jnp.where(
        causal,
        jnp.einsum("the,she->hts", grad_att, value_heads, preferred_element_type=jnp.float32),
        0.0,
    )
    grad_query = jnp.einsum("hts,shd->thd", grad_weights, key_wide, precision=highest)
    grad_query = grad_query + jnp.einsum("the,hde->thd", grad_wide, state_in, precision=highest)
    local_adjoint = jnp.einsum(
        "thd,the->hde", query_heads, grad_att, preferred_element_type=jnp.float32
    )
    adjoint = prefix(local_adjoint, "ctx", add_states, empty_state, True)
    grad_key = jnp.einsum("hts,thd->shd", grad_weights, query_wide, precision=highest)
    grad_key = grad_key + jnp.einsum("she,hde->shd", value_wide, adjoint, precision=highest)
    grad_value = jnp.einsum("hts,the->she", weights, grad_wide, precision=highest)
    grad_value = grad_value + jnp.einsum("shd,hde->she", key_wide, adjoint, precision=highest)
    return (
        grad_query.reshape(tok_rows, feat_width).astype(jnp.bfloat16),
        grad_key.reshape(tok_rows, feat_width).astype(jnp.bfloat16),
        grad_value.reshape(tok_rows, feat_width).astype(jnp.bfloat16),
    )


def solution(mesh):
    return jax.shard_map(
        local,
        mesh=mesh,
        in_specs=(P("ctx", "tp"), P("ctx", "tp"), P("ctx", "tp"), P("ctx", "tp"), P("tp", "ctx")),
        out_specs=(P("ctx", "tp"), P("ctx", "tp"), P("ctx", "tp")),
        check_vma=False,
    )
```

profile of v0, /device:TPU:1, one launch (start us, length us, event | category | flops | bytes accessed | tf_op | source)
XLA Modules:
  0.0 341.3 jit_solution(11616398118935155709)
XLA Ops:
  7.2 1.1 copy.95
  10.8 1.2 convolution_select_fusion.1
  12.0 74.3 %all-gather.11.cloned.1.call-done = f32[64,128,128]{2,1,0:T(8,128)} async-done(((f32[2,128,128]{2,1,0:T(8,128)}), f32[64,128,128]{2,1,0:T(8,128)}) %all-gather.11.cloned.1.call-update) | async-done | bytes 4194320 | tf_op jit(solution)/shard_map/all_gather | solution.py:15
  86.3 30.2 %while.28 = (s32[]{:T(128)}, f32[2,128,128]{2,1,0:T(8,128)S(1)}, s32[]{:T(128)}, f32[32,2,128,128]{3,2,1,0:T(8,128)}, s32[]{:T(128)}, /*index=5*/s32[]{:T(128)}) while((s32[]{:T(128)}, f32[2,128,128]{2,1,0:T(8,128)S(1)}, s32[]{:T(128)}, f32[32,2,128,128]{3,2,1,0:T(8,128)}, s32[]{:T(128)}, /*index=5*/s32[]{:T(128)}) %tuple.81), condition=%wide.region_1.2_spmd.clone, body=%wide.region_0.1_spmd.clone.sunk | while | flops 98308 | bytes 393317 | solution.py:25
  87.2 0.9 add_select_fusion.4
  88.2 0.9 add_select_fusion.4
  89.2 0.9 add_select_fusion.4
  90.2 0.9 add_select_fusion.4
  91.1 0.9 add_select_fusion.4
  92.1 0.9 add_select_fusion.4
  93.1 0.9 add_select_fusion.4
  94.1 0.9 add_select_fusion.4
  95.0 0.9 add_select_fusion.4
  96.0 0.9 add_select_fusion.4
  97.0 0.9 add_select_fusion.4
  98.0 0.9 add_select_fusion.4
  98.9 0.9 add_select_fusion.4
  99.9 0.9 add_select_fusion.4
  100.9 0.9 add_select_fusion.4
  101.8 0.9 add_select_fusion.4
  102.8 1.0 add_select_fusion.4
  103.8 1.0 add_select_fusion.4
  104.8 0.9 add_select_fusion.4
  105.7 0.9 add_select_fusion.4
  106.7 0.9 add_select_fusion.4
  107.7 0.9 add_select_fusion.4
  108.7 0.9 add_select_fusion.4
  109.6 1.0 add_select_fusion.4
  110.6 1.0 add_select_fusion.4
  111.6 0.9 add_select_fusion.4
  112.6 0.9 add_select_fusion.4
  113.5 0.9 add_select_fusion.4
  114.5 1.0 add_select_fusion.4
  115.5 0.9 add_select_fusion.4
  117.3 36.0 %all-gather.7.cloned.1.call-done = bf16[256,4096]{1,0:T(8,128)(2,1)} async-done(((bf16[256,256]{1,0:T(8,128)(2,1)}), bf16[256,4096]{1,0:T(8,128)(2,1)}) %all-gather.7.cloned.1.call-update) | async-done | bytes 2097168 | tf_op jit(solution)/shard_map/all_gather | solution.py:36
  153.3 72.8 %all-gather.9.cloned.1.call-done = bf16[256,4096]{1,0:T(8,128)(2,1)} async-done(((bf16[256,128]{1,0:T(8,128)(2,1)}), bf16[256,4096]{1,0:T(8,128)(2,1)}) %all-gather.9.cloned.1.call-update) | async-done | bytes 2097168 | tf_op jit(solution)/shard_map/all_gather | solution.py:39
  226.1 3.0 multiply_reduce_fusion
  232.2 65.2 %all-gather.13.cloned.1.call-done = f32[64,128,128]{2,1,0:T(8,128)} async-done(((f32[2,128,128]{2,1,0:T(8,128)}), f32[64,128,128]{2,1,0:T(8,128)}) %all-gather.13.cloned.1.call-update) | async-done | bytes 4194320 | tf_op jit(solution)/shard_map/all_gather | solution.py:15
  297.4 4.7 %rev.3 = f32[32,2,128,128]{3,2,1,0:T(8,128)} reverse(f32[32,2,128,128]{3,2,1,0:T(8,128)} %bitcast.117), dimensions={0} | reverse | bytes 8388608 | tf_op jit(solution)/shard_map/rev | solution.py:17
  302.1 30.2 %while.29 = (s32[]{:T(128)}, f32[2,128,128]{2,1,0:T(8,128)S(1)}, s32[]{:T(128)}, f32[32,2,128,128]{3,2,1,0:T(8,128)}, s32[]{:T(128)}, /*index=5*/s32[]{:T(128)}) while((s32[]{:T(128)}, f32[2,128,128]{2,1,0:T(8,128)S(1)}, s32[]{:T(128)}, f32[32,2,128,128]{3,2,1,0:T(8,128)}, s32[]{:T(128)}, /*index=5*/s32[]{:T(128)}) %tuple.70), condition=%wide.region_5.6_spmd.clone, body=%wide.region_4.5_spmd.clone.sunk | while | flops 98308 | bytes 393317 | solution.py:25
  302.1 1.0 add_select_fusion.5
  303.1 0.9 add_select_fusion.5
  304.1 0.9 add_select_fusion.5
  305.0 0.9 add_select_fusion.5
  306.0 0.9 add_select_fusion.5
  307.0 0.9 add_select_fusion.5
  307.9 0.9 add_select_fusion.5
  308.9 0.9 add_select_fusion.5
  (59 shorter events, 31.5 us)
Async XLA Ops:
  7.2 1.1 copy-start
  7.2 109.3 %copy-start.1 = (bf16[256,256]{1,0:T(8,128)(2,1)S(1)}, bf16[256,256]{1,0:T(8,128)(2,1)}, u32[]{:S(2)}) copy-start(bf16[256,256]{1,0:T(8,128)(2,1)} %param.9) | copy-start | bytes 393220
  7.2 79.1 %all-gather.11.cloned.1.call-start = ((), (), s32[]{:S(2)}) async-start(), calls=%async_computation.2 | async-start | bytes 4325376 | tf_op jit(solution)/shard_map/all_gather | solution.py:15
  9.2 144.1 %all-gather.7.cloned.1.call-start = ((), (), s32[]{:S(2)}) async-start(), calls=%async_computation | async-start | bytes 2228224 | tf_op jit(solution)/shard_map/all_gather | solution.py:36
  9.9 216.1 %all-gather.9.cloned.1.call-start = ((), (), s32[]{:S(2)}) async-start(), calls=%async_computation.1 | async-start | bytes 2162688 | tf_op jit(solution)/shard_map/all_gather | solution.py:39
  10.7 286.8 %all-gather.13.cloned.1.call-start = ((), (), s32[]{:S(2)}) async-start(), calls=%async_computation.3 | async-start | bytes 4325376 | tf_op jit(solution)/shard_map/all_gather | solution.py:15
  302.1 30.5 %copy-start.2 = (bf16[256,256]{1,0:T(8,128)(2,1)S(1)}, bf16[256,256]{1,0:T(8,128)(2,1)}, u32[]{:S(2)}) copy-start(bf16[256,256]{1,0:T(8,128)(2,1)} %param.10) | copy-start | bytes 393220
Sparse Core Ops, SparseCore 0:
  10.7 75.5 all-gather.10
  89.3 63.9 all-gather.6
  155.3 70.6 all-gather.8
  230.2 67.1 all-gather.12
where the time goes:
time: 343 us; the launch traced here: 341 us
  waiting for transfers between devices  250 us (73%)
  other arithmetic  59 us (17%)
  between operations  13.9 us (4%)
  local copies, waits for them, and re-layouts  8.78 us (3%)
  matrix products  8.2 us (2%)
    all_gather x2, waiting for transfers between devices, prefix(): pieces = lax.all_gather(value, axis)  140 us
    all_gather x1, waiting for transfers between devices, local(): lax.all_gather(w_out, 'ctx', axis=1, tiled=True)  72.8 us
    select_n x62, other arithmetic, lap(): return jnp.where(position < mine, longer, subtotal)  58.9 us
    all_gather x1, waiting for transfers between devices, local(): full_rows = lax.all_gather(grad_out, 'tp', axis=1, tiled=True)  36 us
  transfers between devices with their start and end apart: 4, of which 4 were waited for; matrix products, arithmetic and copies ran while one was open for 10% of the time, Pallas kernels for 0%

commit v1 on v0

--- a/solution.py
+++ b/solution.py
@@ -1,6 +1,7 @@
 import jax
 import jax.numpy as jnp
 from jax import lax
+from jax.sharding import Mesh
 from jax.sharding import PartitionSpec as P
 
 E = 128
@@ -9,34 +10,54 @@
 epsilon = 1e-06
 highest = lax.Precision.HIGHEST
 
-
-def prefix(value, axis, join, neutral, backward):
-    count, mine = (lax.axis_size(axis), lax.axis_index(axis))
-    pieces = lax.all_gather(value, axis)
-    if backward:
-        pieces = pieces[::-1]
-        mine = count - 1 - mine
-    subtotal = jnp.full_like(value, 0) + jnp.asarray(neutral, value.dtype)
-
-    def lap(position, subtotal):
-        longer = join(subtotal, pieces[position])
-        return jnp.where(position < mine, longer, subtotal)
-
-    return lax.fori_loop(0, count - 1, lap, subtotal)
+CTX = ("ylo", "z", "core")
+TP = ("x", "yhi")
+CHIPS = ("ylo", "z")
 
 
-def add_states(earlier, later):
-    return earlier + later
+def swap_cores(value):
+    return lax.ppermute(value, "core", [(0, 1), (1, 0)])
+
+
+def ctx_scan(local_state, backward):
+    core = lax.axis_index("core")
+    other = swap_cores(local_state)
+    first = jnp.where(core == 0, local_state, other)
+    second = jnp.where(core == 0, other, local_state)
+    chip_total = first + second
+    if backward:
+        within = jnp.where(core == 0, other, jnp.zeros_like(other))
+    else:
+        within = jnp.where(core == 1, other, jnp.zeros_like(other))
+    half = lax.dynamic_index_in_dim(chip_total, core, 0, keepdims=False)
+    chips = lax.axis_size("ylo") * lax.axis_size("z")
+    window = half
+    below = jnp.zeros_like(half)
+    distance = 1
+    while distance < chips:
+        if backward:
+            pairs = [(q, q - distance) for q in range(distance, chips)]
+        else:
+            pairs = [(q, q + distance) for q in range(chips - distance)]
+        arrived = lax.ppermute(window, CHIPS, pairs)
+        below = below + arrived
+        if distance * 2 < chips:
+            window = window + arrived
+        distance *= 2
+    other_half = swap_cores(below)
+    head0 = jnp.where(core == 0, below, other_half)
+    head1 = jnp.where(core == 0, other_half, below)
+    return jnp.stack([head0, head1]) + within
 
 
 def local(query, key_feat, value, grad_out, w_out):
     tok_rows = query.shape[0]
     feat_width = query.shape[1]
     head_count = feat_width // E
-    full_rows = lax.all_gather(grad_out, "tp", axis=1, tiled=True)
+    full_rows = lax.all_gather(grad_out, TP, axis=1, tiled=True)
     grad_z = lax.dot_general(
         full_rows,
-        lax.all_gather(w_out, "ctx", axis=1, tiled=True),
+        lax.all_gather(w_out, CTX, axis=1, tiled=True),
         (((1,), (1,)), ((), ())),
         preferred_element_type=jnp.float32,
     )
@@ -56,8 +77,7 @@
     local_state = jnp.einsum(
         "shd,she->hde", key_heads, value_heads, preferred_element_type=jnp.float32
     )
-    empty_state = jnp.zeros_like(local_state)
-    state_in = prefix(local_state, "ctx", add_states, empty_state, False)
+    state_in = ctx_scan(local_state, False)
     attended = jnp.einsum("hts,she->the", weights, value_wide, precision=highest)
     attended = attended + jnp.einsum("thd,hde->the", query_wide, state_in, precision=highest)
     inv_rms = lax.rsqrt(jnp.mean(attended * attended, axis=-1, keepdims=True) + epsilon)
@@ -76,7 +96,7 @@
     local_adjoint = jnp.einsum(
         "thd,the->hde", query_heads, grad_att, preferred_element_type=jnp.float32
     )
-    adjoint = prefix(local_adjoint, "ctx", add_states, empty_state, True)
+    adjoint = ctx_scan(local_adjoint, True)
     grad_key = jnp.einsum("hts,thd->shd", grad_weights, query_wide, precision=highest)
     grad_key = grad_key + jnp.einsum("she,hde->shd", value_wide, adjoint, precision=highest)
     grad_value = jnp.einsum("hts,the->she", weights, grad_wide, precision=highest)
@@ -89,10 +109,16 @@
 
 
 def solution(mesh):
+    ctx_size, tp_size = mesh.devices.shape
+    chips_y = 2
+    fine = Mesh(
+        mesh.devices.reshape(chips_y, ctx_size // (2 * chips_y), 2, tp_size // 4, 4),
+        CTX + TP,
+    )
     return jax.shard_map(
         local,
-        mesh=mesh,
-        in_specs=(P("ctx", "tp"), P("ctx", "tp"), P("ctx", "tp"), P("ctx", "tp"), P("tp", "ctx")),
-        out_specs=(P("ctx", "tp"), P("ctx", "tp"), P("ctx", "tp")),
+        mesh=fine,
+        in_specs=(P(CTX, TP), P(CTX, TP), P(CTX, TP), P(CTX, TP), P(TP, CTX)),
+        out_specs=(P(CTX, TP), P(CTX, TP), P(CTX, TP)),
         check_vma=False,
     )

time: 343 us -> 203 us (0.59)
  waiting for transfers between devices: 250 us -> 122 us
  other arithmetic: 59 us -> 0.21 us
  starting transfers between devices: 0.16 us -> 54.3 us
  local copies, waits for them, and re-layouts: 8.78 us -> 3.31 us
    all_gather x4 -> x2, waiting for transfers between devices: 248 us -> 95.5 us  [the longest x1 72.8 us: local(): lax.all_gather(w_out, CTX, axis=1, tiled=True)]
    select_n x62 -> x0, other arithmetic: 58.9 us -> none  [lap(): return jnp.where(position < mine, longer, subtotal)]
    ppermute x0 -> x12, starting transfers between devices: none -> 54.2 us  [the longest x8 30.6 us: ctx_scan(): arrived = lax.ppermute(window, CHIPS, pairs)]
    ppermute x0 -> x12, waiting for transfers between devices: none -> 24.8 us  [the longest x8 22.4 us: ctx_scan(): arrived = lax.ppermute(window, CHIPS, pairs)]
    rev x1 -> x0, local copies, waits for them, and re-layouts: 4.66 us -> none  [prefix(): pieces = pieces[::-1]]
  transfers between devices with their start and end apart: 4 -> 14, of which waited for: 4 -> 13; matrix products, arithmetic and copies ran while one was open for 10% -> 3% of each run, Pallas kernels for 0% -> 0%
where the time goes in v1:
time: 203 us; the launch traced here: 202 us
  waiting for transfers between devices  122 us (60%)
  starting transfers between devices  54.3 us (27%)
  between operations  14.3 us (7%)
  matrix products  8.45 us (4%)
  local copies, waits for them, and re-layouts  3.31 us (2%)
    all_gather x1, waiting for transfers between devices, local(): lax.all_gather(w_out, CTX, axis=1, tiled=True)  72.8 us
    ppermute x8, starting transfers between devices, ctx_scan(): arrived = lax.ppermute(window, CHIPS, pairs)  30.6 us
    ppermute x4, starting transfers between devices, swap_cores(): return lax.ppermute(value, 'core', [(0, 1), (1, 0)])  23.6 us
    all_gather x1, waiting for transfers between devices, local(): full_rows = lax.all_gather(grad_out, TP, axis=1, tiled=True)  22.7 us
    ppermute x8, waiting for transfers between devices, ctx_scan(): arrived = lax.ppermute(window, CHIPS, pairs)  22.4 us
  transfers between devices with their start and end apart: 14, of which 13 were waited for; matrix products, arithmetic and copies ran while one was open for 3% of the time, Pallas kernels for 0%

profile of v1, /device:TPU:1, one launch (start us, length us, event | category | flops | bytes accessed | tf_op | source)
XLA Modules:
  0.0 202.3 jit_solution(1962932447259268916)
XLA Ops:
  7.2 0.0 copy-start
  7.2 0.0 copy-start.1
  7.2 0.0 all-gather.3.cloned.1.call-start
  7.2 0.7 all-gather.3.cloned.1.call-update
  7.9 0.0 all-gather.5.cloned.1.call-start
  8.0 0.7 all-gather.5.cloned.1.call-update
  8.7 1.0 copy.76
  9.7 1.1 fusion.9
  10.8 8.7 %collective-permute-start = (f32[2,128,128]{2,1,0:T(8,128)S(1)}, f32[2,128,128]{2,1,0:T(8,128)S(1)}, u32[]{:S(2)}, u32[]{:S(2)}) collective-permute-start(f32[2,128,128]{2,1,0:T(8,128)S(1)} %fusion.9), channel_id=1, source_target_pairs={{0,16},{16,0},{1,17},{17,1},{2,18},{18,2},{3,19},{19,3},{4,20},{20... | collective-permute-start | bytes 393224 | tf_op jit(solution)/shard_map/ppermute | solution.py:19
  19.5 1.0 collective-permute-done
  20.5 1.3 collective-permute-start.1
  21.8 1.3 collective-permute-done.1
  23.1 3.2 %collective-permute-start.2 = (f32[128,128]{1,0:T(8,128)S(1)}, f32[128,128]{1,0:T(8,128)S(1)}, u32[]{:S(2)}, u32[]{:S(2)}) collective-permute-start(f32[128,128]{1,0:T(8,128)S(1)} %add.79), channel_id=1, source_target_pairs={{0,64},{32,96},{64,128},{96,160},{128,192},{160,224},{192,256},{22... | collective-permute-start | bytes 196616 | tf_op jit(solution)/shard_map/ppermute | solution.py:42
  26.3 1.3 collective-permute-done.2
  27.6 12.1 %collective-permute-start.3 = (f32[128,128]{1,0:T(8,128)S(1)}, f32[128,128]{1,0:T(8,128)S(1)}, u32[]{:S(2)}, u32[]{:S(2)}) collective-permute-start(f32[128,128]{1,0:T(8,128)S(1)} %add.81), channel_id=1, source_target_pairs={{0,128},{32,160},{64,192},{96,224},{128,256},{160,288},{192,320},{... | collective-permute-start | bytes 196616 | tf_op jit(solution)/shard_map/ppermute | solution.py:42
  39.8 1.3 collective-permute-done.3
  41.1 8.9 %collective-permute-start.4 = (f32[128,128]{1,0:T(8,128)S(1)}, f32[128,128]{1,0:T(8,128)S(1)}, u32[]{:S(2)}, u32[]{:S(2)}) collective-permute-start(f32[128,128]{1,0:T(8,128)S(1)} %add.83), channel_id=1, source_target_pairs={{0,256},{32,288},{64,320},{96,352},{128,384},{160,416},{192,448},{... | collective-permute-start | bytes 196616 | tf_op jit(solution)/shard_map/ppermute | solution.py:42
  50.0 1.1 convolution_select_fusion.1
  51.1 0.2 collective-permute-done.4
  51.3 5.9 %collective-permute-start.5 = (f32[128,128]{1,0:T(8,128)S(1)}, f32[128,128]{1,0:T(8,128)S(1)}, u32[]{:S(2)}, u32[]{:S(2)}) collective-permute-start(f32[128,128]{1,0:T(8,128)S(1)} %add_add_fusion.1), channel_id=1, source_target_pairs={{0,16},{16,0},{1,17},{17,1},{2,18},{18,2},{3,19},{19,3},{4,20},{20... | collective-permute-start | bytes 196616 | tf_op jit(solution)/shard_map/ppermute | solution.py:19
  57.2 0.4 convolution_bitcast_fusion.2
  57.7 0.4 collective-permute-done.5
  58.1 0.3 multiply_reduce_fusion.1
  58.5 22.7 %all-gather.3.cloned.1.call-done = bf16[256,4096]{1,0:T(8,128)(2,1)} async-done(((bf16[256,256]{1,0:T(8,128)(2,1)}), bf16[256,4096]{1,0:T(8,128)(2,1)}) %all-gather.3.cloned.1.call-update) | async-done | bytes 2097168 | tf_op jit(solution)/shard_map/all_gather | solution.py:57
  81.2 72.8 %all-gather.5.cloned.1.call-done = bf16[256,4096]{1,0:T(8,128)(2,1)} async-done(((bf16[256,128]{1,0:T(8,128)(2,1)}), bf16[256,4096]{1,0:T(8,128)(2,1)}) %all-gather.5.cloned.1.call-update) | async-done | bytes 2097168 | tf_op jit(solution)/shard_map/all_gather | solution.py:60
  153.9 3.0 %multiply_reduce_fusion = (f32[256,2]{0,1:T(2,128)S(1)}, f32[256,256]{0,1:T(8,128)S(1)}) fusion(f32[256,2,128]{0,2,1:T(8,128)S(1)} %get-tuple-element.11, f32[256,2]{0,1:T(2,128)S(1)} %add_rsqrt_fusion, bf16[256,4096]{1,0:T(8,128)(2,1)} %all-gather.3.cloned.1.call-done, bf16[256,4096]{1,0:T(8,128)(2,1)} %all-gather.5.cloned.1.call-done), kind=kOutput, calls=%fused_computation.17 | convolution fusion | flops 537067008 | bytes 4722688 | tf_op jit(solution)/shard_map/dot_general | solution.py:58
  157.0 0.2 convolution_bitcast_fusion.6
  157.2 2.2 %collective-permute-start.6 = (f32[2,128,128]{2,1,0:T(8,128)S(1)}, f32[2,128,128]{2,1,0:T(8,128)S(1)}, u32[]{:S(2)}, u32[]{:S(2)}) collective-permute-start(f32[2,128,128]{2,1,0:T(8,128)S(1)} %convolution_bitcast_fusion.6), channel_id=1, source_target_pairs={{0,16},{16,0},{1,17},{17,1},{2,18},{18,2},{3,19},{19,3},{4,20},{20... | collective-permute-start | bytes 393224 | tf_op jit(solution)/shard_map/ppermute | solution.py:19
  159.4 1.0 collective-permute-done.6
  160.5 1.3 collective-permute-start.7
  161.8 0.3 fusion.35
  162.1 3.4 %collective-permute-done.7 = f32[128,128]{1,0:T(8,128)S(1)} collective-permute-done((f32[128,128]{1,0:T(8,128)S(1)}, f32[128,128]{1,0:T(8,128)S(1)}, u32[]{:S(2)}, u32[]{:S(2)}) %collective-permute-start.7) | collective-permute-done | bytes 65568 | tf_op jit(solution)/shard_map/ppermute | solution.py:42
  165.5 1.3 collective-permute-start.8
  166.8 0.3 convolution_select_fusion
  167.1 4.3 %collective-permute-done.8 = f32[128,128]{1,0:T(8,128)S(1)} collective-permute-done((f32[128,128]{1,0:T(8,128)S(1)}, f32[128,128]{1,0:T(8,128)S(1)}, u32[]{:S(2)}, u32[]{:S(2)}) %collective-permute-start.8) | collective-permute-done | bytes 65568 | tf_op jit(solution)/shard_map/ppermute | solution.py:42
  171.4 1.3 collective-permute-start.9
  172.7 0.4 convolution_bitcast_fusion.1
  173.1 7.3 %collective-permute-done.9 = f32[128,128]{1,0:T(8,128)S(1)} collective-permute-done((f32[128,128]{1,0:T(8,128)S(1)}, f32[128,128]{1,0:T(8,128)S(1)}, u32[]{:S(2)}, u32[]{:S(2)}) %collective-permute-start.9) | collective-permute-done | bytes 65568 | tf_op jit(solution)/shard_map/ppermute | solution.py:42
  180.4 1.3 collective-permute-start.10
  181.7 0.4 convolution_bitcast_fusion
  182.1 3.4 %collective-permute-done.10 = f32[128,128]{1,0:T(8,128)S(1)} collective-permute-done((f32[128,128]{1,0:T(8,128)S(1)}, f32[128,128]{1,0:T(8,128)S(1)}, u32[]{:S(2)}, u32[]{:S(2)}) %collective-permute-start.10) | collective-permute-done | bytes 65568 | tf_op jit(solution)/shard_map/ppermute | solution.py:42
  185.5 6.8 %collective-permute-start.11 = (f32[128,128]{1,0:T(8,128)S(1)}, f32[128,128]{1,0:T(8,128)S(1)}, u32[]{:S(2)}, u32[]{:S(2)}) collective-permute-start(f32[128,128]{1,0:T(8,128)S(1)} %add_add_fusion), channel_id=1, source_target_pairs={{0,16},{16,0},{1,17},{17,1},{2,18},{18,2},{3,19},{19,3},{4,20},{20... | collective-permute-start | bytes 196616 | tf_op jit(solution)/shard_map/ppermute | solution.py:19
  192.2 0.3 fusion.3
  192.5 0.8 copy.25
  193.3 0.3 fusion.5
  193.6 0.8 copy.27
  194.4 0.3 fusion.4
  194.7 0.8 copy.26
  (21 shorter events, 0.2 us)
Async XLA Ops:
  7.2 42.8 %copy-start = (bf16[256,256]{1,0:T(8,128)(2,1)S(1)}, bf16[256,256]{1,0:T(8,128)(2,1)}, u32[]{:S(2)}) copy-start(bf16[256,256]{1,0:T(8,128)(2,1)} %param.5) | copy-start | bytes 393220
  7.2 50.0 %copy-start.1 = (bf16[256,256]{1,0:T(8,128)(2,1)S(1)}, bf16[256,256]{1,0:T(8,128)(2,1)}, u32[]{:S(2)}) copy-start(bf16[256,256]{1,0:T(8,128)(2,1)} %param.7) | copy-start | bytes 393220
  7.2 74.0 %all-gather.3.cloned.1.call-start = ((), (), s32[]{:S(2)}) async-start(), calls=%async_computation | async-start | bytes 2228224 | tf_op jit(solution)/shard_map/all_gather | solution.py:57
  7.9 146.0 %all-gather.5.cloned.1.call-start = ((), (), s32[]{:S(2)}) async-start(), calls=%async_computation.1 | async-start | bytes 2162688 | tf_op jit(solution)/shard_map/all_gather | solution.py:60
  10.8 9.7 %collective-permute-start = (f32[2,128,128]{2,1,0:T(8,128)S(1)}, f32[2,128,128]{2,1,0:T(8,128)S(1)}, u32[]{:S(2)}, u32[]{:S(2)}) collective-permute-start(f32[2,128,128]{2,1,0:T(8,128)S(1)} %fusion.9), channel_id=1, source_target_pairs={{0,16},{16,0},{1,17},{17,1},{2,18},{18,2},{3,19},{19,3},{4,20},{20... | collective-permute-start | bytes 393224 | tf_op jit(solution)/shard_map/ppermute | solution.py:19
  20.5 2.6 %collective-permute-start.1 = (f32[128,128]{1,0:T(8,128)S(1)}, f32[128,128]{1,0:T(8,128)S(1)}, u32[]{:S(2)}, u32[]{:S(2)}) collective-permute-start(f32[128,128]{1,0:T(8,128)S(1)} %add_bitcast_fusion.1), channel_id=1, source_target_pairs={{0,32},{32,64},{64,96},{96,128},{128,160},{160,192},{192,224},{224... | collective-permute-start | bytes 196616 | tf_op jit(solution)/shard_map/ppermute | solution.py:42
  23.1 4.5 %collective-permute-start.2 = (f32[128,128]{1,0:T(8,128)S(1)}, f32[128,128]{1,0:T(8,128)S(1)}, u32[]{:S(2)}, u32[]{:S(2)}) collective-permute-start(f32[128,128]{1,0:T(8,128)S(1)} %add.79), channel_id=1, source_target_pairs={{0,64},{32,96},{64,128},{96,160},{128,192},{160,224},{192,256},{22... | collective-permute-start | bytes 196616 | tf_op jit(solution)/shard_map/ppermute | solution.py:42
  27.6 13.5 %collective-permute-start.3 = (f32[128,128]{1,0:T(8,128)S(1)}, f32[128,128]{1,0:T(8,128)S(1)}, u32[]{:S(2)}, u32[]{:S(2)}) collective-permute-start(f32[128,128]{1,0:T(8,128)S(1)} %add.81), channel_id=1, source_target_pairs={{0,128},{32,160},{64,192},{96,224},{128,256},{160,288},{192,320},{... | collective-permute-start | bytes 196616 | tf_op jit(solution)/shard_map/ppermute | solution.py:42
  41.1 10.2 %collective-permute-start.4 = (f32[128,128]{1,0:T(8,128)S(1)}, f32[128,128]{1,0:T(8,128)S(1)}, u32[]{:S(2)}, u32[]{:S(2)}) collective-permute-start(f32[128,128]{1,0:T(8,128)S(1)} %add.83), channel_id=1, source_target_pairs={{0,256},{32,288},{64,320},{96,352},{128,384},{160,416},{192,448},{... | collective-permute-start | bytes 196616 | tf_op jit(solution)/shard_map/ppermute | solution.py:42
  51.3 6.8 %collective-permute-start.5 = (f32[128,128]{1,0:T(8,128)S(1)}, f32[128,128]{1,0:T(8,128)S(1)}, u32[]{:S(2)}, u32[]{:S(2)}) collective-permute-start(f32[128,128]{1,0:T(8,128)S(1)} %add_add_fusion.1), channel_id=1, source_target_pairs={{0,16},{16,0},{1,17},{17,1},{2,18},{18,2},{3,19},{19,3},{4,20},{20... | collective-permute-start | bytes 196616 | tf_op jit(solution)/shard_map/ppermute | solution.py:19
  157.2 3.2 %collective-permute-start.6 = (f32[2,128,128]{2,1,0:T(8,128)S(1)}, f32[2,128,128]{2,1,0:T(8,128)S(1)}, u32[]{:S(2)}, u32[]{:S(2)}) collective-permute-start(f32[2,128,128]{2,1,0:T(8,128)S(1)} %convolution_bitcast_fusion.6), channel_id=1, source_target_pairs={{0,16},{16,0},{1,17},{17,1},{2,18},{18,2},{3,19},{19,3},{4,20},{20... | collective-permute-start | bytes 393224 | tf_op jit(solution)/shard_map/ppermute | solution.py:19
  160.5 5.0 %collective-permute-start.7 = (f32[128,128]{1,0:T(8,128)S(1)}, f32[128,128]{1,0:T(8,128)S(1)}, u32[]{:S(2)}, u32[]{:S(2)}) collective-permute-start(f32[128,128]{1,0:T(8,128)S(1)} %add_bitcast_fusion), channel_id=1, source_target_pairs={{32,0},{64,32},{96,64},{128,96},{160,128},{192,160},{224,192},{256... | collective-permute-start | bytes 196616 | tf_op jit(solution)/shard_map/ppermute | solution.py:42
  165.5 5.9 %collective-permute-start.8 = (f32[128,128]{1,0:T(8,128)S(1)}, f32[128,128]{1,0:T(8,128)S(1)}, u32[]{:S(2)}, u32[]{:S(2)}) collective-permute-start(f32[128,128]{1,0:T(8,128)S(1)} %add.91), channel_id=1, source_target_pairs={{64,0},{96,32},{128,64},{160,96},{192,128},{224,160},{256,192},{28... | collective-permute-start | bytes 196616 | tf_op jit(solution)/shard_map/ppermute | solution.py:42
  167.1 26.2 %copy-start.2 = (bf16[256,256]{1,0:T(8,128)(2,1)S(1)}, bf16[256,256]{1,0:T(8,128)(2,1)}, u32[]{:S(2)}) copy-start(bf16[256,256]{1,0:T(8,128)(2,1)} %param.6) | copy-start | bytes 393220
  171.4 9.0 %collective-permute-start.9 = (f32[128,128]{1,0:T(8,128)S(1)}, f32[128,128]{1,0:T(8,128)S(1)}, u32[]{:S(2)}, u32[]{:S(2)}) collective-permute-start(f32[128,128]{1,0:T(8,128)S(1)} %add.93), channel_id=1, source_target_pairs={{128,0},{160,32},{192,64},{224,96},{256,128},{288,160},{320,192},{... | collective-permute-start | bytes 196616 | tf_op jit(solution)/shard_map/ppermute | solution.py:42
  180.4 5.0 %collective-permute-start.10 = (f32[128,128]{1,0:T(8,128)S(1)}, f32[128,128]{1,0:T(8,128)S(1)}, u32[]{:S(2)}, u32[]{:S(2)}) collective-permute-start(f32[128,128]{1,0:T(8,128)S(1)} %add.95), channel_id=1, source_target_pairs={{256,0},{288,32},{320,64},{352,96},{384,128},{416,160},{448,192},{... | collective-permute-start | bytes 196616 | tf_op jit(solution)/shard_map/ppermute | solution.py:42
  185.5 7.8 %collective-permute-start.11 = (f32[128,128]{1,0:T(8,128)S(1)}, f32[128,128]{1,0:T(8,128)S(1)}, u32[]{:S(2)}, u32[]{:S(2)}) collective-permute-start(f32[128,128]{1,0:T(8,128)S(1)} %add_add_fusion), channel_id=1, source_target_pairs={{0,16},{16,0},{1,17},{17,1},{2,18},{18,2},{3,19},{19,3},{4,20},{20... | collective-permute-start | bytes 196616 | tf_op jit(solution)/shard_map/ppermute | solution.py:19
Sparse Core Ops, SparseCore 0:
  11.0 70.1 all-gather.2
  83.2 70.6 all-gather.4

commit v2 on v1

--- a/solution.py
+++ b/solution.py
@@ -50,15 +50,27 @@
     return jnp.stack([head0, head1]) + within
 
 
+def gather_columns(w_block):
+    chips = lax.axis_size("ylo") * lax.axis_size("z")
+    spread = jnp.broadcast_to(w_block[None], (chips,) + w_block.shape)
+    mine = lax.all_to_all(spread, CHIPS, 0, 0, tiled=True)
+    others = swap_cores(mine)
+    core = lax.axis_index("core")
+    even = jnp.where(core == 0, mine, others)
+    odd = jnp.where(core == 0, others, mine)
+    return jnp.stack([even, odd], axis=1)
+
+
 def local(query, key_feat, value, grad_out, w_out):
     tok_rows = query.shape[0]
     feat_width = query.shape[1]
     head_count = feat_width // E
     full_rows = lax.all_gather(grad_out, TP, axis=1, tiled=True)
-    grad_z = lax.dot_general(
-        full_rows,
-        lax.all_gather(w_out, CTX, axis=1, tiled=True),
-        (((1,), (1,)), ((), ())),
+    columns = gather_columns(w_out)
+    grad_z = jnp.einsum(
+        "tqrk,qrjk->tj",
+        full_rows.reshape(tok_rows, columns.shape[0], 2, columns.shape[3]),
+        columns,
         preferred_element_type=jnp.float32,
     )
     query_heads = query.reshape(tok_rows, head_count, E)

time: 203 us -> 139 us (0.68)
  waiting for transfers between devices: 122 us -> 36.5 us
  starting transfers between devices: 54.3 us -> 68 us
  other arithmetic: 0.21 us -> 3.19 us
  local copies, waits for them, and re-layouts: 3.31 us -> 6.22 us
    all_gather x1 -> x0, waiting for transfers between devices: 72.8 us -> none  [local(): lax.all_gather(w_out, CTX, axis=1, tiled=True)]
    all_gather x1, waiting for transfers between devices: 22.7 us -> 0.01 us  [local(): full_rows = lax.all_gather(grad_out, TP, axis=1, tiled=True)]
    all_to_all x0 -> x1, starting transfers between devices: none -> 12 us  [gather_columns(): mine = lax.all_to_all(spread, CHIPS, 0, 0, tiled=True)]
    ppermute x8, waiting for transfers between devices: 22.4 us -> 34.2 us  [ctx_scan(): arrived = lax.ppermute(window, CHIPS, pairs)]
    ppermute x8, starting transfers between devices: 30.6 us -> 33.5 us  [ctx_scan(): arrived = lax.ppermute(window, CHIPS, pairs)]
    broadcast_in_dim x0 -> x1, local copies, waits for them, and re-layouts: none -> 2.03 us  [gather_columns(): spread = jnp.broadcast_to(w_block[None], (chips,) + w_block.shape)]
    unnamed x9 -> x22, local copies, waits for them, and re-layouts: 2.3 us -> 4.09 us
    ppermute x4 -> x5, starting transfers between devices: 23.6 us -> 22.5 us  [swap_cores(): return lax.ppermute(value, 'core', [(0, 1), (1, 0)])]
  transfers between devices with their start and end apart: 14 -> 15, of which waited for: 13 -> 9; matrix products, arithmetic and copies ran while one was open for 3% -> 8% of each run, Pallas kernels for 0% -> 0%
where the time goes in v2:
time: 139 us; the launch traced here: 137 us
  starting transfers between devices  68 us (49%)
  waiting for transfers between devices  36.5 us (26%)
  between operations  14.4 us (10%)
  matrix products  8.29 us (6%)
  local copies, waits for them, and re-layouts  6.22 us (4%)
  other arithmetic  3.19 us (2%)
    ppermute x8, waiting for transfers between devices, ctx_scan(): arrived = lax.ppermute(window, CHIPS, pairs)  34.2 us
    ppermute x8, starting transfers between devices, ctx_scan(): arrived = lax.ppermute(window, CHIPS, pairs)  33.5 us
    ppermute x5, starting transfers between devices, swap_cores(): return lax.ppermute(value, 'core', [(0, 1), (1, 0)])  22.5 us
    all_to_all x1, starting transfers between devices, gather_columns(): mine = lax.all_to_all(spread, CHIPS, 0, 0, tiled=True)  12 us
    unnamed x22, local copies, waits for them, and re-layouts  4.09 us
    dot_general x1, matrix products, local(): jnp.einsum('tqrk,qrjk->tj', full_rows.reshape(tok_rows, columns.shape[0],...  2.94 us
  transfers between devices with their start and end apart: 15, of which 9 were waited for; matrix products, arithmetic and copies ran while one was open for 8% of the time, Pallas kernels for 0%

profile of v2, /device:TPU:1, one launch (start us, length us, event | category | flops | bytes accessed | tf_op | source)
XLA Modules:
  0.0 136.6 jit_solution(17436582200278683226)
XLA Ops:
  7.2 0.0 all-gather.2.cloned.1.call-start
  7.2 1.8 %copy.37 = bf16[256,256]{0,1:T(8,128)(2,1)} copy(bf16[256,256]{1,0:T(8,128)(2,1)} %param.8) | data formatting | bytes 262144 | tf_op args[3]
  9.0 0.0 all-gather.2.cloned.1.call-update
  9.0 2.0 %broadcast_in_dim.29 = bf16[16,256,128]{2,1,0:T(8,128)(2,1)} broadcast(bf16[256,128]{1,0:T(8,128)(2,1)} %param.9), dimensions={1,2} | broadcast | bytes 1114112 | tf_op jit(solution)/shard_map/broadcast_in_dim | solution.py:55
  11.1 12.0 %all-to-all-start = ((bf16[16,256,128]{2,1,0:T(8,128)(2,1)}), bf16[16,256,128]{2,1,0:T(8,128)(2,1)S(1)}, u32[]{:S(2)}, u32[]{:S(2)}) async-start(bf16[16,256,128]{2,1,0:T(8,128)(2,1)} %broadcast_in_dim.29), calls=%async_computation | async-start | bytes 2097152 | tf_op jit(solution)/shard_map/all_to_all | solution.py:56
  23.1 0.1 copy.102
  23.2 0.2 fusion.13
  23.3 2.9 %collective-permute-start = (f32[2,128,128]{2,1,0:T(8,128)S(1)}, f32[2,128,128]{2,1,0:T(8,128)S(1)}, u32[]{:S(2)}, u32[]{:S(2)}) collective-permute-start(f32[2,128,128]{2,1,0:T(8,128)S(1)} %fusion.13), channel_id=1, source_target_pairs={{0,16},{16,0},{1,17},{17,1},{2,18},{18,2},{3,19},{19,3},{4,20},{20... | collective-permute-start | bytes 393224 | tf_op jit(solution)/shard_map/ppermute | solution.py:19
  26.2 1.0 collective-permute-done
  27.2 3.5 %collective-permute-start.1 = (f32[128,128]{1,0:T(8,128)S(1)}, f32[128,128]{1,0:T(8,128)S(1)}, u32[]{:S(2)}, u32[]{:S(2)}) collective-permute-start(f32[128,128]{1,0:T(8,128)S(1)} %add_bitcast_fusion.1), channel_id=1, source_target_pairs={{0,32},{32,64},{64,96},{96,128},{128,160},{160,192},{192,224},{224... | collective-permute-start | bytes 196616 | tf_op jit(solution)/shard_map/ppermute | solution.py:42
  30.8 11.7 %collective-permute-done.1 = f32[128,128]{1,0:T(8,128)S(1)} collective-permute-done((f32[128,128]{1,0:T(8,128)S(1)}, f32[128,128]{1,0:T(8,128)S(1)}, u32[]{:S(2)}, u32[]{:S(2)}) %collective-permute-start.1) | collective-permute-done | bytes 65568 | tf_op jit(solution)/shard_map/ppermute | solution.py:42
  42.5 9.3 %collective-permute-start.2 = (f32[128,128]{1,0:T(8,128)S(1)}, f32[128,128]{1,0:T(8,128)S(1)}, u32[]{:S(2)}, u32[]{:S(2)}) collective-permute-start(f32[128,128]{1,0:T(8,128)S(1)} %add.79), channel_id=1, source_target_pairs={{0,64},{32,96},{64,128},{96,160},{128,192},{160,224},{192,256},{22... | collective-permute-start | bytes 196616 | tf_op jit(solution)/shard_map/ppermute | solution.py:42
  51.8 1.3 collective-permute-done.2
  53.1 10.8 %collective-permute-start.3 = (f32[128,128]{1,0:T(8,128)S(1)}, f32[128,128]{1,0:T(8,128)S(1)}, u32[]{:S(2)}, u32[]{:S(2)}) collective-permute-start(f32[128,128]{1,0:T(8,128)S(1)} %add.81), channel_id=1, source_target_pairs={{0,128},{32,160},{64,192},{96,224},{128,256},{160,288},{192,320},{... | collective-permute-start | bytes 196616 | tf_op jit(solution)/shard_map/ppermute | solution.py:42
  64.0 1.3 collective-permute-done.3
  65.2 0.6 add.83
  65.9 4.6 %collective-permute-start.4 = (f32[128,128]{1,0:T(8,128)}, f32[128,128]{1,0:T(8,128)}, u32[]{:S(2)}, u32[]{:S(2)}) collective-permute-start(f32[128,128]{1,0:T(8,128)} %add.83), channel_id=1, source_target_pairs={{0,256},{32,288},{64,320},{96,352},{128,384},{160,416},{192,448},{... | collective-permute-start | bytes 196616 | tf_op jit(solution)/shard_map/ppermute | solution.py:42
  70.4 0.2 convolution_select_fusion.1
  70.7 8.1 %collective-permute-start.6 = (bf16[16,256,128]{2,1,0:T(8,128)(2,1)S(1)}, bf16[16,256,128]{2,1,0:T(8,128)(2,1)S(1)}, u32[]{:S(2)}, u32[]{:S(2)}) collective-permute-start(bf16[16,256,128]{2,1,0:T(8,128)(2,1)S(1)} %all-to-all-done), channel_id=1, source_target_pairs={{0,16},{16,0},{1,17},{17,1},{2,18},{18,2},{3,19},{19,3},{4,20},{20... | collective-permute-start | bytes 3145736 | tf_op jit(solution)/shard_map/ppermute | solution.py:19
  78.8 0.9 add_add_fusion.1
  79.7 2.8 %collective-permute-start.5 = (f32[128,128]{1,0:T(8,128)S(1)}, f32[128,128]{1,0:T(8,128)S(1)}, u32[]{:S(2)}, u32[]{:S(2)}) collective-permute-start(f32[128,128]{1,0:T(8,128)S(1)} %add_add_fusion.1), channel_id=1, source_target_pairs={{0,16},{16,0},{1,17},{17,1},{2,18},{18,2},{3,19},{19,3},{4,20},{20... | collective-permute-start | bytes 196616 | tf_op jit(solution)/shard_map/ppermute | solution.py:19
  82.5 1.1 convolution_bitcast_fusion.2
  83.7 1.3 multiply_reduce_fusion.1
  85.0 1.4 %select_bitcast_fusion.1 = (bf16[16,1,256,128]{3,2,1,0:T(8,128)(2,1)}, bf16[16,1,256,128]{3,2,1,0:T(8,128)(2,1)}) fusion(bf16[16,256,128]{2,1,0:T(8,128)(2,1)S(1)} %all-to-all-done, bf16[16,256,128]{2,1,0:T(8,128)(2,1)S(1)} %collective-permute-done.6, pred[]{:T(512)S(6)} %eq.4), kind=kLoop, calls=%fused_computation.21 | loop fusion | flops 1048576 | bytes 4194305 | tf_op jit(solution)/shard_map/stack | solution.py:61
  86.5 2.9 %fusion = f32[256,256,1,1]{1,0,3,2:T(8,128)S(1)} fusion(bf16[256,16,2,128]{0,3,2,1:T(8,128)(2,1)} %bitcast.132, bf16[16,1,256,128]{3,2,1,0:T(8,128)(2,1)} %get-tuple-element.10, bf16[16,1,256,128]{3,2,1,0:T(8,128)(2,1)} %get-tuple-element.9), kind=kOutput, calls=%fused_computation | convolution fusion | flops 537919488 | bytes 4456448 | tf_op jit(solution)/shard_map/tqrk,qrjk->tj/dot_general | solution.py:70
  89.4 0.1 multiply_reduce_fusion
  89.6 0.2 convolution_bitcast_fusion.6
  89.8 2.0 %collective-permute-start.7 = (f32[2,128,128]{2,1,0:T(8,128)S(1)}, f32[2,128,128]{2,1,0:T(8,128)S(1)}, u32[]{:S(2)}, u32[]{:S(2)}) collective-permute-start(f32[2,128,128]{2,1,0:T(8,128)S(1)} %convolution_bitcast_fusion.6), channel_id=1, source_target_pairs={{0,16},{16,0},{1,17},{17,1},{2,18},{18,2},{3,19},{19,3},{4,20},{20... | collective-permute-start | bytes 393224 | tf_op jit(solution)/shard_map/ppermute | solution.py:19
  91.8 1.2 collective-permute-done.7
  93.1 1.4 %collective-permute-start.8 = (f32[128,128]{1,0:T(8,128)S(1)}, f32[128,128]{1,0:T(8,128)S(1)}, u32[]{:S(2)}, u32[]{:S(2)}) collective-permute-start(f32[128,128]{1,0:T(8,128)S(1)} %add_bitcast_fusion), channel_id=1, source_target_pairs={{32,0},{64,32},{96,64},{128,96},{160,128},{192,160},{224,192},{256... | collective-permute-start | bytes 196616 | tf_op jit(solution)/shard_map/ppermute | solution.py:42
  94.5 0.3 fusion.40
  94.8 5.1 %collective-permute-done.8 = f32[128,128]{1,0:T(8,128)S(1)} collective-permute-done((f32[128,128]{1,0:T(8,128)S(1)}, f32[128,128]{1,0:T(8,128)S(1)}, u32[]{:S(2)}, u32[]{:S(2)}) %collective-permute-start.8) | collective-permute-done | bytes 65568 | tf_op jit(solution)/shard_map/ppermute | solution.py:42
  99.9 1.3 collective-permute-start.9
  101.2 0.3 convolution_select_fusion
  101.5 4.3 %collective-permute-done.9 = f32[128,128]{1,0:T(8,128)S(1)} collective-permute-done((f32[128,128]{1,0:T(8,128)S(1)}, f32[128,128]{1,0:T(8,128)S(1)}, u32[]{:S(2)}, u32[]{:S(2)}) %collective-permute-start.9) | collective-permute-done | bytes 65568 | tf_op jit(solution)/shard_map/ppermute | solution.py:42
  105.9 1.3 collective-permute-start.10
  107.2 0.4 convolution_bitcast_fusion
  107.5 7.3 %collective-permute-done.10 = f32[128,128]{1,0:T(8,128)S(1)} collective-permute-done((f32[128,128]{1,0:T(8,128)S(1)}, f32[128,128]{1,0:T(8,128)S(1)}, u32[]{:S(2)}, u32[]{:S(2)}) %collective-permute-start.10) | collective-permute-done | bytes 65568 | tf_op jit(solution)/shard_map/ppermute | solution.py:42
  114.8 1.3 collective-permute-start.11
  116.1 0.4 convolution_bitcast_fusion.1
  116.5 3.3 %collective-permute-done.11 = f32[128,128]{1,0:T(8,128)S(1)} collective-permute-done((f32[128,128]{1,0:T(8,128)S(1)}, f32[128,128]{1,0:T(8,128)S(1)}, u32[]{:S(2)}, u32[]{:S(2)}) %collective-permute-start.11) | collective-permute-done | bytes 65568 | tf_op jit(solution)/shard_map/ppermute | solution.py:42
  119.8 6.8 %collective-permute-start.12 = (f32[128,128]{1,0:T(8,128)S(1)}, f32[128,128]{1,0:T(8,128)S(1)}, u32[]{:S(2)}, u32[]{:S(2)}) collective-permute-start(f32[128,128]{1,0:T(8,128)S(1)} %add_add_fusion), channel_id=1, source_target_pairs={{0,16},{16,0},{1,17},{17,1},{2,18},{18,2},{3,19},{19,3},{4,20},{20... | collective-permute-start | bytes 196616 | tf_op jit(solution)/shard_map/ppermute | solution.py:19
  126.6 0.3 fusion.7
  126.9 0.8 copy.49
  127.7 0.3 fusion.9
  128.0 0.8 copy.51
  128.7 0.3 fusion.8
  129.0 0.8 copy.50
  (38 shorter events, 0.3 us)
Async XLA Ops:
  7.2 63.3 %copy-start = (bf16[256,256]{1,0:T(8,128)(2,1)S(1)}, bf16[256,256]{1,0:T(8,128)(2,1)}, u32[]{:S(2)}) copy-start(bf16[256,256]{1,0:T(8,128)(2,1)} %param.5) | copy-start | bytes 393220
  7.2 15.9 %copy-start.2 = (bf16[256,256]{1,0:T(8,128)(2,1)S(1)}, bf16[256,256]{1,0:T(8,128)(2,1)}, u32[]{:S(2)}) copy-start(bf16[256,256]{1,0:T(8,128)(2,1)} %param.6) | copy-start | bytes 393220
  7.2 16.0 %copy-start.1 = (bf16[256,256]{1,0:T(8,128)(2,1)S(1)}, bf16[256,256]{1,0:T(8,128)(2,1)}, u32[]{:S(2)}) copy-start(bf16[256,256]{1,0:T(8,128)(2,1)} %param.7) | copy-start | bytes 393220
  7.2 79.3 %all-gather.2.cloned.1.call-start = ((), (), s32[]{:S(2)}) async-start(), calls=%async_computation.1 | async-start | bytes 2228224 | tf_op jit(solution)/shard_map/all_gather | solution.py:68
  11.1 59.6 %all-to-all-start = ((bf16[16,256,128]{2,1,0:T(8,128)(2,1)}), bf16[16,256,128]{2,1,0:T(8,128)(2,1)S(1)}, u32[]{:S(2)}, u32[]{:S(2)}) async-start(bf16[16,256,128]{2,1,0:T(8,128)(2,1)} %broadcast_in_dim.29), calls=%async_computation | async-start | bytes 2097152 | tf_op jit(solution)/shard_map/all_to_all | solution.py:56
  23.3 3.8 %collective-permute-start = (f32[2,128,128]{2,1,0:T(8,128)S(1)}, f32[2,128,128]{2,1,0:T(8,128)S(1)}, u32[]{:S(2)}, u32[]{:S(2)}) collective-permute-start(f32[2,128,128]{2,1,0:T(8,128)S(1)} %fusion.13), channel_id=1, source_target_pairs={{0,16},{16,0},{1,17},{17,1},{2,18},{18,2},{3,19},{19,3},{4,20},{20... | collective-permute-start | bytes 393224 | tf_op jit(solution)/shard_map/ppermute | solution.py:19
  27.2 15.3 %collective-permute-start.1 = (f32[128,128]{1,0:T(8,128)S(1)}, f32[128,128]{1,0:T(8,128)S(1)}, u32[]{:S(2)}, u32[]{:S(2)}) collective-permute-start(f32[128,128]{1,0:T(8,128)S(1)} %add_bitcast_fusion.1), channel_id=1, source_target_pairs={{0,32},{32,64},{64,96},{96,128},{128,160},{160,192},{192,224},{224... | collective-permute-start | bytes 196616 | tf_op jit(solution)/shard_map/ppermute | solution.py:42
  42.5 10.6 %collective-permute-start.2 = (f32[128,128]{1,0:T(8,128)S(1)}, f32[128,128]{1,0:T(8,128)S(1)}, u32[]{:S(2)}, u32[]{:S(2)}) collective-permute-start(f32[128,128]{1,0:T(8,128)S(1)} %add.79), channel_id=1, source_target_pairs={{0,64},{32,96},{64,128},{96,160},{128,192},{160,224},{192,256},{22... | collective-permute-start | bytes 196616 | tf_op jit(solution)/shard_map/ppermute | solution.py:42
  53.1 12.1 %collective-permute-start.3 = (f32[128,128]{1,0:T(8,128)S(1)}, f32[128,128]{1,0:T(8,128)S(1)}, u32[]{:S(2)}, u32[]{:S(2)}) collective-permute-start(f32[128,128]{1,0:T(8,128)S(1)} %add.81), channel_id=1, source_target_pairs={{0,128},{32,160},{64,192},{96,224},{128,256},{160,288},{192,320},{... | collective-permute-start | bytes 196616 | tf_op jit(solution)/shard_map/ppermute | solution.py:42
  63.9 6.7 %copy-start.7 = (pred[256,256]{1,0:T(8,128)(4,1)}, pred[256,256]{1,0:T(8,128)(4,1)S(1)}, u32[]{:S(2)}) copy-start(pred[256,256]{1,0:T(8,128)(4,1)S(1)} %iota_compare_fusion) | copy-start | bytes 196612
  65.9 12.9 %collective-permute-start.4 = (f32[128,128]{1,0:T(8,128)}, f32[128,128]{1,0:T(8,128)}, u32[]{:S(2)}, u32[]{:S(2)}) collective-permute-start(f32[128,128]{1,0:T(8,128)} %add.83), channel_id=1, source_target_pairs={{0,256},{32,288},{64,320},{96,352},{128,384},{160,416},{192,448},{... | collective-permute-start | bytes 196616 | tf_op jit(solution)/shard_map/ppermute | solution.py:42
  70.7 14.3 %collective-permute-start.6 = (bf16[16,256,128]{2,1,0:T(8,128)(2,1)S(1)}, bf16[16,256,128]{2,1,0:T(8,128)(2,1)S(1)}, u32[]{:S(2)}, u32[]{:S(2)}) collective-permute-start(bf16[16,256,128]{2,1,0:T(8,128)(2,1)S(1)} %all-to-all-done), channel_id=1, source_target_pairs={{0,16},{16,0},{1,17},{17,1},{2,18},{18,2},{3,19},{19,3},{4,20},{20... | collective-permute-start | bytes 3145736 | tf_op jit(solution)/shard_map/ppermute | solution.py:19
  79.7 3.9 %collective-permute-start.5 = (f32[128,128]{1,0:T(8,128)S(1)}, f32[128,128]{1,0:T(8,128)S(1)}, u32[]{:S(2)}, u32[]{:S(2)}) collective-permute-start(f32[128,128]{1,0:T(8,128)S(1)} %add_add_fusion.1), channel_id=1, source_target_pairs={{0,16},{16,0},{1,17},{17,1},{2,18},{18,2},{3,19},{19,3},{4,20},{20... | collective-permute-start | bytes 196616 | tf_op jit(solution)/shard_map/ppermute | solution.py:19
  83.6 1.4 copy-start.3
  83.6 1.4 %copy-start.5 = (f32[1,128,128]{2,1,0:T(8,128)}, f32[1,128,128]{2,1,0:T(8,128)S(1)}, u32[]{:S(2)}) copy-start(f32[1,128,128]{2,1,0:T(8,128)S(1)} %get-tuple-element.14) | copy-start | bytes 196612
  89.4 11.8 %copy-start.8 = (pred[256,256]{1,0:T(8,128)(4,1)S(1)}, pred[256,256]{1,0:T(8,128)(4,1)}, u32[]{:S(2)}) copy-start(pred[256,256]{1,0:T(8,128)(4,1)} %copy-done.7) | copy-start | bytes 196612
  89.8 3.2 %collective-permute-start.7 = (f32[2,128,128]{2,1,0:T(8,128)S(1)}, f32[2,128,128]{2,1,0:T(8,128)S(1)}, u32[]{:S(2)}, u32[]{:S(2)}) collective-permute-start(f32[2,128,128]{2,1,0:T(8,128)S(1)} %convolution_bitcast_fusion.6), channel_id=1, source_target_pairs={{0,16},{16,0},{1,17},{17,1},{2,18},{18,2},{3,19},{19,3},{4,20},{20... | collective-permute-start | bytes 393224 | tf_op jit(solution)/shard_map/ppermute | solution.py:19
  93.0 33.6 %copy-start.4 = (f32[1,128,128]{2,1,0:T(8,128)S(1)}, f32[1,128,128]{2,1,0:T(8,128)}, u32[]{:S(2)}) copy-start(f32[1,128,128]{2,1,0:T(8,128)} %copy-done.3) | copy-start | bytes 196612
  93.0 33.6 %copy-start.6 = (f32[1,128,128]{2,1,0:T(8,128)S(1)}, f32[1,128,128]{2,1,0:T(8,128)}, u32[]{:S(2)}) copy-start(f32[1,128,128]{2,1,0:T(8,128)} %copy-done.5) | copy-start | bytes 196612
  93.1 6.9 %collective-permute-start.8 = (f32[128,128]{1,0:T(8,128)S(1)}, f32[128,128]{1,0:T(8,128)S(1)}, u32[]{:S(2)}, u32[]{:S(2)}) collective-permute-start(f32[128,128]{1,0:T(8,128)S(1)} %add_bitcast_fusion), channel_id=1, source_target_pairs={{32,0},{64,32},{96,64},{128,96},{160,128},{192,160},{224,192},{256... | collective-permute-start | bytes 196616 | tf_op jit(solution)/shard_map/ppermute | solution.py:42
  99.9 5.9 %collective-permute-start.9 = (f32[128,128]{1,0:T(8,128)S(1)}, f32[128,128]{1,0:T(8,128)S(1)}, u32[]{:S(2)}, u32[]{:S(2)}) collective-permute-start(f32[128,128]{1,0:T(8,128)S(1)} %add.91), channel_id=1, source_target_pairs={{64,0},{96,32},{128,64},{160,96},{192,128},{224,160},{256,192},{28... | collective-permute-start | bytes 196616 | tf_op jit(solution)/shard_map/ppermute | solution.py:42
  105.9 8.9 %collective-permute-start.10 = (f32[128,128]{1,0:T(8,128)S(1)}, f32[128,128]{1,0:T(8,128)S(1)}, u32[]{:S(2)}, u32[]{:S(2)}) collective-permute-start(f32[128,128]{1,0:T(8,128)S(1)} %add.93), channel_id=1, source_target_pairs={{128,0},{160,32},{192,64},{224,96},{256,128},{288,160},{320,192},{... | collective-permute-start | bytes 196616 | tf_op jit(solution)/shard_map/ppermute | solution.py:42
  114.8 5.0 %collective-permute-start.11 = (f32[128,128]{1,0:T(8,128)S(1)}, f32[128,128]{1,0:T(8,128)S(1)}, u32[]{:S(2)}, u32[]{:S(2)}) collective-permute-start(f32[128,128]{1,0:T(8,128)S(1)} %add.95), channel_id=1, source_target_pairs={{256,0},{288,32},{320,64},{352,96},{384,128},{416,160},{448,192},{... | collective-permute-start | bytes 196616 | tf_op jit(solution)/shard_map/ppermute | solution.py:42
  119.8 7.8 %collective-permute-start.12 = (f32[128,128]{1,0:T(8,128)S(1)}, f32[128,128]{1,0:T(8,128)S(1)}, u32[]{:S(2)}, u32[]{:S(2)}) collective-permute-start(f32[128,128]{1,0:T(8,128)S(1)} %add_add_fusion), channel_id=1, source_target_pairs={{0,16},{16,0},{1,17},{17,1},{2,18},{18,2},{3,19},{19,3},{4,20},{20... | collective-permute-start | bytes 196616 | tf_op jit(solution)/shard_map/ppermute | solution.py:19
Sparse Core Ops, SparseCore 0:
  11.6 69.3 all-gather.1

commit v3 on v2

--- a/solution.py
+++ b/solution.py
@@ -65,11 +65,13 @@
     tok_rows = query.shape[0]
     feat_width = query.shape[1]
     head_count = feat_width // E
-    full_rows = lax.all_gather(grad_out, TP, axis=1, tiled=True)
+    tp_size = lax.axis_size("x") * lax.axis_size("yhi")
+    spread_rows = jnp.broadcast_to(grad_out[None], (tp_size,) + grad_out.shape)
+    full_rows = lax.all_to_all(spread_rows, TP, 0, 0, tiled=True)
     columns = gather_columns(w_out)
     grad_z = jnp.einsum(
-        "tqrk,qrjk->tj",
-        full_rows.reshape(tok_rows, columns.shape[0], 2, columns.shape[3]),
+        "qtrk,qrjk->tj",
+        full_rows.reshape(tp_size, tok_rows, 2, columns.shape[3]),
         columns,
         preferred_element_type=jnp.float32,
     )

time: 139 us -> 175 us (1.26)
  starting transfers between devices: 68 us -> 108 us
  between operations: 14.4 us -> 1.07 us
  waiting for transfers between devices: 36.5 us -> 49.4 us
    all_to_all x1, waiting for transfers between devices: 0.01 us -> 25.2 us  [gather_columns(): mine = lax.all_to_all(spread, CHIPS, 0, 0, tiled=True)]
    ppermute x8, starting transfers between devices: 33.5 us -> 54.3 us  [ctx_scan(): arrived = lax.ppermute(window, CHIPS, pairs)]
    ppermute x8, waiting for transfers between devices: 34.2 us -> 22.2 us  [ctx_scan(): arrived = lax.ppermute(window, CHIPS, pairs)]
    ppermute x5, starting transfers between devices: 22.5 us -> 32.7 us  [swap_cores(): return lax.ppermute(value, 'core', [(0, 1), (1, 0)])]
    all_to_all x0 -> x1, starting transfers between devices: none -> 8.67 us  [local(): full_rows = lax.all_to_all(spread_rows, TP, 0, 0, tiled=True)]
    unnamed x22 -> x24, local copies, waits for them, and re-layouts: 4.09 us -> 2.44 us
  transfers between devices with their start and end apart: 15 -> 15, of which waited for: 9 -> 11; matrix products, arithmetic and copies ran while one was open for 8% -> 4% of each run, Pallas kernels for 0% -> 0%
where the time goes in v3:
time: 175 us; the launch traced here: 174 us
  starting transfers between devices  108 us (62%)
  waiting for transfers between devices  49.4 us (28%)
  matrix products  8.33 us (5%)
  local copies, waits for them, and re-layouts  6.14 us (4%)
  other arithmetic  1.77 us (1%)
    ppermute x8, starting transfers between devices, ctx_scan(): arrived = lax.ppermute(window, CHIPS, pairs)  54.3 us
    ppermute x5, starting transfers between devices, swap_cores(): return lax.ppermute(value, 'core', [(0, 1), (1, 0)])  32.7 us
    all_to_all x1, waiting for transfers between devices, gather_columns(): mine = lax.all_to_all(spread, CHIPS, 0, 0, tiled=True)  25.2 us
    ppermute x8, waiting for transfers between devices, ctx_scan(): arrived = lax.ppermute(window, CHIPS, pairs)  22.2 us
    all_to_all x1, starting transfers between devices, gather_columns(): mine = lax.all_to_all(spread, CHIPS, 0, 0, tiled=True)  12 us
    all_to_all x1, starting transfers between devices, local(): full_rows = lax.all_to_all(spread_rows, TP, 0, 0, tiled=True)  8.67 us
  transfers between devices with their start and end apart: 15, of which 11 were waited for; matrix products, arithmetic and copies ran while one was open for 4% of the time, Pallas kernels for 0%

profile of v3, /device:TPU:1, one launch (start us, length us, event | category | flops | bytes accessed | tf_op | source)
XLA Modules:
  0.0 174.4 jit_solution(4075116849565219516)
XLA Ops:
  0.7 2.1 %broadcast_in_dim.35 = bf16[16,256,128]{2,1,0:T(8,128)(2,1)} broadcast(bf16[256,128]{1,0:T(8,128)(2,1)} %param.9), dimensions={1,2} | broadcast | bytes 1114112 | tf_op jit(solution)/shard_map/broadcast_in_dim | solution.py:55
  2.8 12.0 %all-to-all-start = ((bf16[16,256,128]{2,1,0:T(8,128)(2,1)}), bf16[16,256,128]{2,1,0:T(8,128)(2,1)S(1)}, u32[]{:S(2)}, u32[]{:S(2)}) async-start(bf16[16,256,128]{2,1,0:T(8,128)(2,1)} %broadcast_in_dim.35), calls=%async_computation | async-start | bytes 2097152 | tf_op jit(solution)/shard_map/all_to_all | solution.py:56
  14.7 0.1 copy.37
  14.9 25.2 %all-to-all-done = bf16[16,256,128]{2,1,0:T(8,128)(2,1)S(1)} async-done(((bf16[16,256,128]{2,1,0:T(8,128)(2,1)}), bf16[16,256,128]{2,1,0:T(8,128)(2,1)S(1)}, u32[]{:S(2)}, u32[]{:S(2)}) %all-to-all-start) | async-done | bytes 1048608 | tf_op jit(solution)/shard_map/all_to_all | solution.py:56
  40.1 1.5 broadcast_in_dim.36
  41.6 8.7 %all-to-all-start.1 = ((bf16[16,256,256]{1,2,0:T(8,128)(2,1)}), bf16[16,256,256]{1,2,0:T(8,128)(2,1)}, u32[]{:S(2)}, u32[]{:S(2)}) async-start(bf16[16,256,256]{1,2,0:T(8,128)(2,1)} %broadcast_in_dim.36), calls=%async_computation.1 | async-start | bytes 4194304 | tf_op jit(solution)/shard_map/all_to_all | solution.py:70
  50.3 0.1 copy.102
  50.4 0.2 fusion.13
  50.6 3.6 %collective-permute-start = (f32[2,128,128]{2,1,0:T(8,128)S(1)}, f32[2,128,128]{2,1,0:T(8,128)S(1)}, u32[]{:S(2)}, u32[]{:S(2)}) collective-permute-start(f32[2,128,128]{2,1,0:T(8,128)S(1)} %fusion.13), channel_id=1, source_target_pairs={{0,16},{16,0},{1,17},{17,1},{2,18},{18,2},{3,19},{19,3},{4,20},{20... | collective-permute-start | bytes 393224 | tf_op jit(solution)/shard_map/ppermute | solution.py:19
  54.2 1.0 collective-permute-done
  55.1 5.2 %collective-permute-start.1 = (f32[128,128]{1,0:T(8,128)S(1)}, f32[128,128]{1,0:T(8,128)S(1)}, u32[]{:S(2)}, u32[]{:S(2)}) collective-permute-start(f32[128,128]{1,0:T(8,128)S(1)} %add_bitcast_fusion.1), channel_id=1, source_target_pairs={{0,32},{32,64},{64,96},{96,128},{128,160},{160,192},{192,224},{224... | collective-permute-start | bytes 196616 | tf_op jit(solution)/shard_map/ppermute | solution.py:42
  60.4 1.3 collective-permute-done.1
  61.7 3.9 %collective-permute-start.2 = (f32[128,128]{1,0:T(8,128)S(1)}, f32[128,128]{1,0:T(8,128)S(1)}, u32[]{:S(2)}, u32[]{:S(2)}) collective-permute-start(f32[128,128]{1,0:T(8,128)S(1)} %add.79), channel_id=1, source_target_pairs={{0,64},{32,96},{64,128},{96,160},{128,192},{160,224},{192,256},{22... | collective-permute-start | bytes 196616 | tf_op jit(solution)/shard_map/ppermute | solution.py:42
  65.6 1.3 collective-permute-done.2
  66.9 9.0 %collective-permute-start.3 = (f32[128,128]{1,0:T(8,128)S(1)}, f32[128,128]{1,0:T(8,128)S(1)}, u32[]{:S(2)}, u32[]{:S(2)}) collective-permute-start(f32[128,128]{1,0:T(8,128)S(1)} %add.81), channel_id=1, source_target_pairs={{0,128},{32,160},{64,192},{96,224},{128,256},{160,288},{192,320},{... | collective-permute-start | bytes 196616 | tf_op jit(solution)/shard_map/ppermute | solution.py:42
  76.0 1.3 collective-permute-done.3
  77.2 30.9 %collective-permute-start.4 = (f32[128,128]{1,0:T(8,128)S(1)}, f32[128,128]{1,0:T(8,128)S(1)}, u32[]{:S(2)}, u32[]{:S(2)}) collective-permute-start(f32[128,128]{1,0:T(8,128)S(1)} %add.83), channel_id=1, source_target_pairs={{0,256},{32,288},{64,320},{96,352},{128,384},{160,416},{192,448},{... | collective-permute-start | bytes 196616 | tf_op jit(solution)/shard_map/ppermute | solution.py:42
  108.2 0.2 convolution_select_fusion.1
  108.4 17.7 %collective-permute-start.6 = (bf16[16,256,128]{2,1,0:T(8,128)(2,1)S(1)}, bf16[16,256,128]{2,1,0:T(8,128)(2,1)S(1)}, u32[]{:S(2)}, u32[]{:S(2)}) collective-permute-start(bf16[16,256,128]{2,1,0:T(8,128)(2,1)S(1)} %all-to-all-done), channel_id=1, source_target_pairs={{0,16},{16,0},{1,17},{17,1},{2,18},{18,2},{3,19},{19,3},{4,20},{20... | collective-permute-start | bytes 3145736 | tf_op jit(solution)/shard_map/ppermute | solution.py:19
  126.1 1.9 %collective-permute-start.5 = (f32[128,128]{1,0:T(8,128)S(1)}, f32[128,128]{1,0:T(8,128)S(1)}, u32[]{:S(2)}, u32[]{:S(2)}) collective-permute-start(f32[128,128]{1,0:T(8,128)S(1)} %add_add_fusion.1), channel_id=1, source_target_pairs={{0,16},{16,0},{1,17},{17,1},{2,18},{18,2},{3,19},{19,3},{4,20},{20... | collective-permute-start | bytes 196616 | tf_op jit(solution)/shard_map/ppermute | solution.py:19
  128.0 1.2 convolution_bitcast_fusion.2
  129.2 0.1 collective-permute-done.5
  129.3 1.3 multiply_reduce_fusion.1
  130.7 1.5 select_bitcast_fusion.1
  132.2 3.0 %fusion = f32[256,256,1,1]{1,0,3,2:T(8,128)S(1)} fusion(bf16[16,256,2,128]{1,3,2,0:T(8,128)(2,1)} %bitcast.8, bf16[16,1,256,128]{3,2,1,0:T(8,128)(2,1)} %get-tuple-element.10, bf16[16,1,256,128]{3,2,1,0:T(8,128)(2,1)} %get-tuple-element.9), kind=kOutput, calls=%fused_computation | convolution fusion | flops 537919488 | bytes 4456448 | tf_op jit(solution)/shard_map/qtrk,qrjk->tj/dot_general | solution.py:72
  135.1 0.1 multiply_reduce_fusion
  135.3 0.2 convolution_bitcast_fusion.6
  135.5 2.4 %collective-permute-start.7 = (f32[2,128,128]{2,1,0:T(8,128)S(1)}, f32[2,128,128]{2,1,0:T(8,128)S(1)}, u32[]{:S(2)}, u32[]{:S(2)}) collective-permute-start(f32[2,128,128]{2,1,0:T(8,128)S(1)} %convolution_bitcast_fusion.6), channel_id=1, source_target_pairs={{0,16},{16,0},{1,17},{17,1},{2,18},{18,2},{3,19},{19,3},{4,20},{20... | collective-permute-start | bytes 393224 | tf_op jit(solution)/shard_map/ppermute | solution.py:19
  137.8 1.0 collective-permute-done.7
  138.9 1.4 collective-permute-start.8
  140.3 0.3 convolution_select_fusion
  140.6 3.4 %collective-permute-done.8 = f32[128,128]{1,0:T(8,128)S(1)} collective-permute-done((f32[128,128]{1,0:T(8,128)S(1)}, f32[128,128]{1,0:T(8,128)S(1)}, u32[]{:S(2)}, u32[]{:S(2)}) %collective-permute-start.8) | collective-permute-done | bytes 65568 | tf_op jit(solution)/shard_map/ppermute | solution.py:42
  144.0 1.3 collective-permute-start.9
  145.3 0.4 convolution_bitcast_fusion.1
  145.7 4.3 %collective-permute-done.9 = f32[128,128]{1,0:T(8,128)S(1)} collective-permute-done((f32[128,128]{1,0:T(8,128)S(1)}, f32[128,128]{1,0:T(8,128)S(1)}, u32[]{:S(2)}, u32[]{:S(2)}) %collective-permute-start.9) | collective-permute-done | bytes 65568 | tf_op jit(solution)/shard_map/ppermute | solution.py:42
  150.0 1.3 collective-permute-start.10
  151.3 0.4 convolution_bitcast_fusion
  151.7 7.3 %collective-permute-done.10 = f32[128,128]{1,0:T(8,128)S(1)} collective-permute-done((f32[128,128]{1,0:T(8,128)S(1)}, f32[128,128]{1,0:T(8,128)S(1)}, u32[]{:S(2)}, u32[]{:S(2)}) %collective-permute-start.10) | collective-permute-done | bytes 65568 | tf_op jit(solution)/shard_map/ppermute | solution.py:42
  159.0 1.3 collective-permute-start.11
  160.3 0.3 fusion.40
  160.7 3.4 %collective-permute-done.11 = f32[128,128]{1,0:T(8,128)S(1)} collective-permute-done((f32[128,128]{1,0:T(8,128)S(1)}, f32[128,128]{1,0:T(8,128)S(1)}, u32[]{:S(2)}, u32[]{:S(2)}) %collective-permute-start.11) | collective-permute-done | bytes 65568 | tf_op jit(solution)/shard_map/ppermute | solution.py:42
  164.0 7.2 %collective-permute-start.12 = (f32[128,128]{1,0:T(8,128)S(1)}, f32[128,128]{1,0:T(8,128)S(1)}, u32[]{:S(2)}, u32[]{:S(2)}) collective-permute-start(f32[128,128]{1,0:T(8,128)S(1)} %add_add_fusion), channel_id=1, source_target_pairs={{0,16},{16,0},{1,17},{17,1},{2,18},{18,2},{3,19},{19,3},{4,20},{20... | collective-permute-start | bytes 196616 | tf_op jit(solution)/shard_map/ppermute | solution.py:19
  171.2 0.3 fusion.7
  171.5 0.8 copy.49
  172.3 0.3 fusion.8
  172.5 0.8 copy.50
  173.3 0.3 fusion.9
  173.6 0.8 copy.51
  (40 shorter events, 0.3 us)
Async XLA Ops:
  0.6 107.5 %copy-start = (bf16[256,256]{1,0:T(8,128)(2,1)S(1)}, bf16[256,256]{1,0:T(8,128)(2,1)}, u32[]{:S(2)}) copy-start(bf16[256,256]{1,0:T(8,128)(2,1)} %param.5) | copy-start | bytes 393220
  0.6 14.1 %copy-start.9 = (bf16[256,256]{1,0:T(8,128)(2,1)S(1)}, bf16[256,256]{1,0:T(8,128)(2,1)}, u32[]{:S(2)}) copy-start(bf16[256,256]{1,0:T(8,128)(2,1)} %param.8) | copy-start | bytes 393220
  2.8 37.3 %all-to-all-start = ((bf16[16,256,128]{2,1,0:T(8,128)(2,1)}), bf16[16,256,128]{2,1,0:T(8,128)(2,1)S(1)}, u32[]{:S(2)}, u32[]{:S(2)}) async-start(bf16[16,256,128]{2,1,0:T(8,128)(2,1)} %broadcast_in_dim.35), calls=%async_computation | async-start | bytes 2097152 | tf_op jit(solution)/shard_map/all_to_all | solution.py:56
  41.6 8.7 %copy-start.2 = (bf16[256,256]{1,0:T(8,128)(2,1)S(1)}, bf16[256,256]{1,0:T(8,128)(2,1)}, u32[]{:S(2)}) copy-start(bf16[256,256]{1,0:T(8,128)(2,1)} %param.6) | copy-start | bytes 393220
  41.6 8.8 %copy-start.1 = (bf16[256,256]{1,0:T(8,128)(2,1)S(1)}, bf16[256,256]{1,0:T(8,128)(2,1)}, u32[]{:S(2)}) copy-start(bf16[256,256]{1,0:T(8,128)(2,1)} %param.7) | copy-start | bytes 393220
  41.6 90.6 %all-to-all-start.1 = ((bf16[16,256,256]{1,2,0:T(8,128)(2,1)}), bf16[16,256,256]{1,2,0:T(8,128)(2,1)}, u32[]{:S(2)}, u32[]{:S(2)}) async-start(bf16[16,256,256]{1,2,0:T(8,128)(2,1)} %broadcast_in_dim.36), calls=%async_computation.1 | async-start | bytes 4194304 | tf_op jit(solution)/shard_map/all_to_all | solution.py:70
  50.6 4.6 %collective-permute-start = (f32[2,128,128]{2,1,0:T(8,128)S(1)}, f32[2,128,128]{2,1,0:T(8,128)S(1)}, u32[]{:S(2)}, u32[]{:S(2)}) collective-permute-start(f32[2,128,128]{2,1,0:T(8,128)S(1)} %fusion.13), channel_id=1, source_target_pairs={{0,16},{16,0},{1,17},{17,1},{2,18},{18,2},{3,19},{19,3},{4,20},{20... | collective-permute-start | bytes 393224 | tf_op jit(solution)/shard_map/ppermute | solution.py:19
  55.1 6.6 %collective-permute-start.1 = (f32[128,128]{1,0:T(8,128)S(1)}, f32[128,128]{1,0:T(8,128)S(1)}, u32[]{:S(2)}, u32[]{:S(2)}) collective-permute-start(f32[128,128]{1,0:T(8,128)S(1)} %add_bitcast_fusion.1), channel_id=1, source_target_pairs={{0,32},{32,64},{64,96},{96,128},{128,160},{160,192},{192,224},{224... | collective-permute-start | bytes 196616 | tf_op jit(solution)/shard_map/ppermute | solution.py:42
  61.7 5.2 %collective-permute-start.2 = (f32[128,128]{1,0:T(8,128)S(1)}, f32[128,128]{1,0:T(8,128)S(1)}, u32[]{:S(2)}, u32[]{:S(2)}) collective-permute-start(f32[128,128]{1,0:T(8,128)S(1)} %add.79), channel_id=1, source_target_pairs={{0,64},{32,96},{64,128},{96,160},{128,192},{160,224},{192,256},{22... | collective-permute-start | bytes 196616 | tf_op jit(solution)/shard_map/ppermute | solution.py:42
  66.9 10.3 %collective-permute-start.3 = (f32[128,128]{1,0:T(8,128)S(1)}, f32[128,128]{1,0:T(8,128)S(1)}, u32[]{:S(2)}, u32[]{:S(2)}) collective-permute-start(f32[128,128]{1,0:T(8,128)S(1)} %add.81), channel_id=1, source_target_pairs={{0,128},{32,160},{64,192},{96,224},{128,256},{160,288},{192,320},{... | collective-permute-start | bytes 196616 | tf_op jit(solution)/shard_map/ppermute | solution.py:42
  75.9 32.2 %copy-start.7 = (pred[256,256]{1,0:T(8,128)(4,1)}, pred[256,256]{1,0:T(8,128)(4,1)S(1)}, u32[]{:S(2)}) copy-start(pred[256,256]{1,0:T(8,128)(4,1)S(1)} %iota_compare_fusion) | copy-start | bytes 196612
  77.2 48.8 %collective-permute-start.4 = (f32[128,128]{1,0:T(8,128)S(1)}, f32[128,128]{1,0:T(8,128)S(1)}, u32[]{:S(2)}, u32[]{:S(2)}) collective-permute-start(f32[128,128]{1,0:T(8,128)S(1)} %add.83), channel_id=1, source_target_pairs={{0,256},{32,288},{64,320},{96,352},{128,384},{160,416},{192,448},{... | collective-permute-start | bytes 196616 | tf_op jit(solution)/shard_map/ppermute | solution.py:42
  108.4 22.3 %collective-permute-start.6 = (bf16[16,256,128]{2,1,0:T(8,128)(2,1)S(1)}, bf16[16,256,128]{2,1,0:T(8,128)(2,1)S(1)}, u32[]{:S(2)}, u32[]{:S(2)}) collective-permute-start(bf16[16,256,128]{2,1,0:T(8,128)(2,1)S(1)} %all-to-all-done), channel_id=1, source_target_pairs={{0,16},{16,0},{1,17},{17,1},{2,18},{18,2},{3,19},{19,3},{4,20},{20... | collective-permute-start | bytes 3145736 | tf_op jit(solution)/shard_map/ppermute | solution.py:19
  126.1 3.1 %collective-permute-start.5 = (f32[128,128]{1,0:T(8,128)S(1)}, f32[128,128]{1,0:T(8,128)S(1)}, u32[]{:S(2)}, u32[]{:S(2)}) collective-permute-start(f32[128,128]{1,0:T(8,128)S(1)} %add_add_fusion.1), channel_id=1, source_target_pairs={{0,16},{16,0},{1,17},{17,1},{2,18},{18,2},{3,19},{19,3},{4,20},{20... | collective-permute-start | bytes 196616 | tf_op jit(solution)/shard_map/ppermute | solution.py:19
  129.3 1.4 copy-start.3
  129.3 1.4 copy-start.5
  132.2 8.1 %copy-start.8 = (pred[256,256]{1,0:T(8,128)(4,1)S(1)}, pred[256,256]{1,0:T(8,128)(4,1)}, u32[]{:S(2)}) copy-start(pred[256,256]{1,0:T(8,128)(4,1)} %copy-done.7) | copy-start | bytes 196612
  135.5 3.3 %collective-permute-start.7 = (f32[2,128,128]{2,1,0:T(8,128)S(1)}, f32[2,128,128]{2,1,0:T(8,128)S(1)}, u32[]{:S(2)}, u32[]{:S(2)}) collective-permute-start(f32[2,128,128]{2,1,0:T(8,128)S(1)} %convolution_bitcast_fusion.6), channel_id=1, source_target_pairs={{0,16},{16,0},{1,17},{17,1},{2,18},{18,2},{3,19},{19,3},{4,20},{20... | collective-permute-start | bytes 393224 | tf_op jit(solution)/shard_map/ppermute | solution.py:19
  138.8 32.4 %copy-start.4 = (f32[1,128,128]{2,1,0:T(8,128)S(1)}, f32[1,128,128]{2,1,0:T(8,128)}, u32[]{:S(2)}) copy-start(f32[1,128,128]{2,1,0:T(8,128)} %copy-done.3) | copy-start | bytes 196612
  138.8 32.4 %copy-start.6 = (f32[1,128,128]{2,1,0:T(8,128)S(1)}, f32[1,128,128]{2,1,0:T(8,128)}, u32[]{:S(2)}) copy-start(f32[1,128,128]{2,1,0:T(8,128)} %copy-done.5) | copy-start | bytes 196612
  138.9 5.1 %collective-permute-start.8 = (f32[128,128]{1,0:T(8,128)S(1)}, f32[128,128]{1,0:T(8,128)S(1)}, u32[]{:S(2)}, u32[]{:S(2)}) collective-permute-start(f32[128,128]{1,0:T(8,128)S(1)} %add_bitcast_fusion), channel_id=1, source_target_pairs={{32,0},{64,32},{96,64},{128,96},{160,128},{192,160},{224,192},{256... | collective-permute-start | bytes 196616 | tf_op jit(solution)/shard_map/ppermute | solution.py:42
  144.0 6.0 %collective-permute-start.9 = (f32[128,128]{1,0:T(8,128)S(1)}, f32[128,128]{1,0:T(8,128)S(1)}, u32[]{:S(2)}, u32[]{:S(2)}) collective-permute-start(f32[128,128]{1,0:T(8,128)S(1)} %add.91), channel_id=1, source_target_pairs={{64,0},{96,32},{128,64},{160,96},{192,128},{224,160},{256,192},{28... | collective-permute-start | bytes 196616 | tf_op jit(solution)/shard_map/ppermute | solution.py:42
  150.0 9.0 %collective-permute-start.10 = (f32[128,128]{1,0:T(8,128)S(1)}, f32[128,128]{1,0:T(8,128)S(1)}, u32[]{:S(2)}, u32[]{:S(2)}) collective-permute-start(f32[128,128]{1,0:T(8,128)S(1)} %add.93), channel_id=1, source_target_pairs={{128,0},{160,32},{192,64},{224,96},{256,128},{288,160},{320,192},{... | collective-permute-start | bytes 196616 | tf_op jit(solution)/shard_map/ppermute | solution.py:42
  159.0 5.0 %collective-permute-start.11 = (f32[128,128]{1,0:T(8,128)S(1)}, f32[128,128]{1,0:T(8,128)S(1)}, u32[]{:S(2)}, u32[]{:S(2)}) collective-permute-start(f32[128,128]{1,0:T(8,128)S(1)} %add.95), channel_id=1, source_target_pairs={{256,0},{288,32},{320,64},{352,96},{384,128},{416,160},{448,192},{... | collective-permute-start | bytes 196616 | tf_op jit(solution)/shard_map/ppermute | solution.py:42
  164.0 8.2 %collective-permute-start.12 = (f32[128,128]{1,0:T(8,128)S(1)}, f32[128,128]{1,0:T(8,128)S(1)}, u32[]{:S(2)}, u32[]{:S(2)}) collective-permute-start(f32[128,128]{1,0:T(8,128)S(1)} %add_add_fusion), channel_id=1, source_target_pairs={{0,16},{16,0},{1,17},{17,1},{2,18},{18,2},{3,19},{19,3},{4,20},{20... | collective-permute-start | bytes 196616 | tf_op jit(solution)/shard_map/ppermute | solution.py:19

commit v4 on v2

--- a/solution.py
+++ b/solution.py
@@ -21,24 +21,26 @@
 
 def ctx_scan(local_state, backward):
     core = lax.axis_index("core")
+    chips = lax.axis_size("ylo") * lax.axis_size("z")
+    step = -1 if backward else 1
+    nearest = [(q, q + step) for q in range(chips) if 0 <= q + step < chips]
     other = swap_cores(local_state)
-    first = jnp.where(core == 0, local_state, other)
-    second = jnp.where(core == 0, other, local_state)
-    chip_total = first + second
+    own_head = lax.dynamic_index_in_dim(local_state, core, 0, keepdims=False)
+    cross_head = lax.dynamic_index_in_dim(local_state, 1 - core, 0, keepdims=False)
+    same = lax.ppermute(own_head, CHIPS, nearest)
+    cross = lax.ppermute(
+        cross_head, CTX, [(2 * q + c, 2 * t + 1 - c) for q, t in nearest for c in (0, 1)]
+    )
+    below = jnp.where(core == 0, same + cross, cross + same)
+    paired = lax.dynamic_index_in_dim(other, core, 0, keepdims=False)
+    window = jnp.where(core == 0, own_head + paired, paired + own_head) + below
     if backward:
         within = jnp.where(core == 0, other, jnp.zeros_like(other))
     else:
         within = jnp.where(core == 1, other, jnp.zeros_like(other))
-    half = lax.dynamic_index_in_dim(chip_total, core, 0, keepdims=False)
-    chips = lax.axis_size("ylo") * lax.axis_size("z")
-    window = half
-    below = jnp.zeros_like(half)
-    distance = 1
+    distance = 2
     while distance < chips:
-        if backward:
-            pairs = [(q, q - distance) for q in range(distance, chips)]
-        else:
-            pairs = [(q, q + distance) for q in range(chips - distance)]
+        pairs = [(q, q + step * distance) for q in range(chips) if 0 <= q + step * distance < chips]
         arrived = lax.ppermute(window, CHIPS, pairs)
         below = below + arrived
         if distance * 2 < chips:

time: 139 us -> 140 us (level)
  the two profiles are of different devices: /device:TPU:1 before, /device:TPU:51 now
where the time goes in v4:
time: 140 us
  starting transfers between devices  72.4 us (52%)
  waiting for transfers between devices  34.3 us (24%)
  between operations  14.5 us (10%)
  matrix products  8.32 us (6%)
  local copies, waits for them, and re-layouts  6.88 us (5%)
  other arithmetic  3.2 us (2%)
    ppermute x6, starting transfers between devices, ctx_scan(): arrived = lax.ppermute(window, CHIPS, pairs)  32.2 us
    ppermute x5, starting transfers between devices, swap_cores(): return lax.ppermute(value, 'core', [(0, 1), (1, 0)])  20.4 us
    ppermute x6, waiting for transfers between devices, ctx_scan(): arrived = lax.ppermute(window, CHIPS, pairs)  18.9 us
    all_to_all x1, starting transfers between devices, gather_columns(): mine = lax.all_to_all(spread, CHIPS, 0, 0, tiled=True)  10.3 us
    ppermute x2, waiting for transfers between devices, ctx_scan(): same = lax.ppermute(own_head, CHIPS, nearest)  9.43 us
    ppermute x2, waiting for transfers between devices, ctx_scan(): lax.ppermute(cross_head, CTX, [(2 * q + c, 2 * t + 1 - c) for q, t in nea...  5.93 us
    ppermute x2, starting transfers between devices, ctx_scan(): same = lax.ppermute(own_head, CHIPS, nearest)  4.84 us
    unnamed x24, local copies, waits for them, and re-layouts  4.72 us
  transfers between devices with their start and end apart: 17, of which 9 were waited for; matrix products, arithmetic and copies ran while one was open for 8% of the time, Pallas kernels for 0%

profile of v4, /device:TPU:51, one launch (start us, length us, event | category | flops | bytes accessed | tf_op | source)
XLA Modules:
  0.0 139.6 jit_solution(1405060664615943810)
XLA Ops:
  7.2 1.8 %copy.39 = bf16[256,256]{0,1:T(8,128)(2,1)} copy(bf16[256,256]{1,0:T(8,128)(2,1)} %param.8) | data formatting | bytes 262144 | tf_op args[3]
  9.0 2.0 %broadcast_in_dim.29 = bf16[16,256,128]{2,1,0:T(8,128)(2,1)} broadcast(bf16[256,128]{1,0:T(8,128)(2,1)} %param.9), dimensions={1,2} | broadcast | bytes 1114112 | tf_op jit(solution)/shard_map/broadcast_in_dim | solution.py:57
  11.1 10.3 %all-to-all-start = ((bf16[16,256,128]{2,1,0:T(8,128)(2,1)}), bf16[16,256,128]{2,1,0:T(8,128)(2,1)S(1)}, u32[]{:S(2)}, u32[]{:S(2)}) async-start(bf16[16,256,128]{2,1,0:T(8,128)(2,1)} %broadcast_in_dim.29), calls=%async_computation | async-start | bytes 2097152 | tf_op jit(solution)/shard_map/all_to_all | solution.py:58
  21.3 0.1 copy.106
  21.4 0.2 fusion.13
  21.6 2.9 %collective-permute-start.2 = (f32[2,128,128]{2,1,0:T(8,128)S(1)}, f32[2,128,128]{2,1,0:T(8,128)S(1)}, u32[]{:S(2)}, u32[]{:S(2)}) collective-permute-start(f32[2,128,128]{2,1,0:T(8,128)S(1)} %fusion.13), channel_id=1, source_target_pairs={{0,16},{16,0},{1,17},{17,1},{2,18},{18,2},{3,19},{19,3},{4,20},{20... | collective-permute-start | bytes 393224 | tf_op jit(solution)/shard_map/ppermute | solution.py:19
  24.5 3.5 %collective-permute-start = (f32[128,128]{1,0:T(8,128)S(1)}, f32[128,128]{1,0:T(8,128)S(1)}, u32[]{:S(2)}, u32[]{:S(2)}) collective-permute-start(f32[128,128]{1,0:T(8,128)S(1)} %get-tuple-element.22), channel_id=1, source_target_pairs={{0,32},{32,64},{64,96},{96,128},{128,160},{160,192},{192,224},{224... | collective-permute-start | bytes 196616 | tf_op jit(solution)/shard_map/ppermute | solution.py:30
  28.1 3.3 %collective-permute-start.1 = (f32[128,128]{1,0:T(8,128)S(1)}, f32[128,128]{1,0:T(8,128)S(1)}, u32[]{:S(2)}, u32[]{:S(2)}) collective-permute-start(f32[128,128]{1,0:T(8,128)S(1)} %get-tuple-element.21), channel_id=1, source_target_pairs={{0,48},{16,32},{32,80},{48,64},{64,112},{80,96},{96,144},{112,128}... | collective-permute-start | bytes 196616 | tf_op jit(solution)/shard_map/ppermute | solution.py:31
  31.4 9.4 %collective-permute-done = f32[128,128]{1,0:T(8,128)S(1)} collective-permute-done((f32[128,128]{1,0:T(8,128)S(1)}, f32[128,128]{1,0:T(8,128)S(1)}, u32[]{:S(2)}, u32[]{:S(2)}) %collective-permute-start) | collective-permute-done | bytes 65568 | tf_op jit(solution)/shard_map/ppermute | solution.py:30
  40.8 3.4 %collective-permute-done.1 = f32[128,128]{1,0:T(8,128)S(1)} collective-permute-done((f32[128,128]{1,0:T(8,128)S(1)}, f32[128,128]{1,0:T(8,128)S(1)}, u32[]{:S(2)}, u32[]{:S(2)}) %collective-permute-start.1) | collective-permute-done | bytes 65568 | tf_op jit(solution)/shard_map/ppermute | solution.py:31
  44.3 8.0 %collective-permute-start.3 = (f32[128,128]{1,0:T(8,128)S(1)}, f32[128,128]{1,0:T(8,128)S(1)}, u32[]{:S(2)}, u32[]{:S(2)}) collective-permute-start(f32[128,128]{1,0:T(8,128)S(1)} %get-tuple-element.11), channel_id=1, source_target_pairs={{0,64},{32,96},{64,128},{96,160},{128,192},{160,224},{192,256},{22... | collective-permute-start | bytes 196616 | tf_op jit(solution)/shard_map/ppermute | solution.py:44
  52.3 1.8 %collective-permute-done.3 = f32[128,128]{1,0:T(8,128)S(1)} collective-permute-done((f32[128,128]{1,0:T(8,128)S(1)}, f32[128,128]{1,0:T(8,128)S(1)}, u32[]{:S(2)}, u32[]{:S(2)}) %collective-permute-start.3) | collective-permute-done | bytes 65568 | tf_op jit(solution)/shard_map/ppermute | solution.py:44
  54.1 9.8 %collective-permute-start.4 = (f32[128,128]{1,0:T(8,128)S(1)}, f32[128,128]{1,0:T(8,128)S(1)}, u32[]{:S(2)}, u32[]{:S(2)}) collective-permute-start(f32[128,128]{1,0:T(8,128)S(1)} %add.100), channel_id=1, source_target_pairs={{0,128},{32,160},{64,192},{96,224},{128,256},{160,288},{192,320},{... | collective-permute-start | bytes 196616 | tf_op jit(solution)/shard_map/ppermute | solution.py:44
  63.9 1.3 collective-permute-done.4
  65.1 0.6 add.102
  65.8 10.6 %collective-permute-start.5 = (f32[128,128]{1,0:T(8,128)}, f32[128,128]{1,0:T(8,128)S(1)}, u32[]{:S(2)}, u32[]{:S(2)}) collective-permute-start(f32[128,128]{1,0:T(8,128)} %add.102), channel_id=1, source_target_pairs={{0,256},{32,288},{64,320},{96,352},{128,384},{160,416},{192,448},{... | collective-permute-start | bytes 196616 | tf_op jit(solution)/shard_map/ppermute | solution.py:44
  76.4 0.2 convolution_select_fusion.1
  76.6 7.3 %collective-permute-start.7 = (bf16[16,256,128]{2,1,0:T(8,128)(2,1)S(1)}, bf16[16,256,128]{2,1,0:T(8,128)(2,1)S(1)}, u32[]{:S(2)}, u32[]{:S(2)}) collective-permute-start(bf16[16,256,128]{2,1,0:T(8,128)(2,1)S(1)} %all-to-all-done), channel_id=1, source_target_pairs={{0,16},{16,0},{1,17},{17,1},{2,18},{18,2},{3,19},{19,3},{4,20},{20... | collective-permute-start | bytes 3145736 | tf_op jit(solution)/shard_map/ppermute | solution.py:19
  84.0 0.6 copy-done.9
  84.6 0.9 add_add_fusion.1
  85.5 1.9 %collective-permute-start.6 = (f32[128,128]{1,0:T(8,128)S(1)}, f32[128,128]{1,0:T(8,128)S(1)}, u32[]{:S(2)}, u32[]{:S(2)}) collective-permute-start(f32[128,128]{1,0:T(8,128)S(1)} %add_add_fusion.1), channel_id=1, source_target_pairs={{0,16},{16,0},{1,17},{17,1},{2,18},{18,2},{3,19},{19,3},{4,20},{20... | collective-permute-start | bytes 196616 | tf_op jit(solution)/shard_map/ppermute | solution.py:19
  87.4 1.2 convolution_bitcast_fusion.2
  88.6 0.1 collective-permute-done.6
  88.6 1.3 multiply_reduce_fusion.1
  90.0 1.5 %select_bitcast_fusion.1 = (bf16[16,1,256,128]{3,2,1,0:T(8,128)(2,1)}, bf16[16,1,256,128]{3,2,1,0:T(8,128)(2,1)}) fusion(bf16[16,256,128]{2,1,0:T(8,128)(2,1)S(1)} %all-to-all-done, bf16[16,256,128]{2,1,0:T(8,128)(2,1)S(1)} %collective-permute-done.7, pred[]{:T(512)S(6)} %eq.4), kind=kLoop, calls=%fused_computation.20 | loop fusion | flops 1048576 | bytes 4194305 | tf_op jit(solution)/shard_map/stack | solution.py:63
  91.5 2.9 %fusion = f32[256,256,1,1]{1,0,3,2:T(8,128)S(1)} fusion(bf16[256,16,2,128]{0,3,2,1:T(8,128)(2,1)} %bitcast.152, bf16[16,1,256,128]{3,2,1,0:T(8,128)(2,1)} %get-tuple-element.14, bf16[16,1,256,128]{3,2,1,0:T(8,128)(2,1)} %get-tuple-element.13), kind=kOutput, calls=%fused_computation | convolution fusion | flops 537919488 | bytes 4456448 | tf_op jit(solution)/shard_map/tqrk,qrjk->tj/dot_general | solution.py:72
  94.6 0.2 fusion.18
  94.8 1.3 collective-permute-start.8
  96.1 1.3 collective-permute-start.9
  97.4 2.4 %collective-permute-start.10 = (f32[2,128,128]{2,1,0:T(8,128)S(1)}, f32[2,128,128]{2,1,0:T(8,128)S(1)}, u32[]{:S(2)}, u32[]{:S(2)}) collective-permute-start(f32[2,128,128]{2,1,0:T(8,128)S(1)} %bitcast.148), channel_id=1, source_target_pairs={{0,16},{16,0},{1,17},{17,1},{2,18},{18,2},{3,19},{19,3},{4,20},{20... | collective-permute-start | bytes 393224 | tf_op jit(solution)/shard_map/ppermute | solution.py:19
  99.8 0.3 fusion.43
  100.2 2.5 %collective-permute-done.9 = f32[128,128]{1,0:T(8,128)S(1)} collective-permute-done((f32[128,128]{1,0:T(8,128)S(1)}, f32[128,128]{1,0:T(8,128)S(1)}, u32[]{:S(2)}, u32[]{:S(2)}) %collective-permute-start.9) | collective-permute-done | bytes 65568 | tf_op jit(solution)/shard_map/ppermute | solution.py:31
  102.7 1.3 collective-permute-start.11
  104.0 0.3 convolution_select_fusion
  104.3 5.3 %collective-permute-done.11 = f32[128,128]{1,0:T(8,128)S(1)} collective-permute-done((f32[128,128]{1,0:T(8,128)S(1)}, f32[128,128]{1,0:T(8,128)S(1)}, u32[]{:S(2)}, u32[]{:S(2)}) %collective-permute-start.11) | collective-permute-done | bytes 65568 | tf_op jit(solution)/shard_map/ppermute | solution.py:44
  109.6 1.3 collective-permute-start.12
  110.9 0.4 convolution_bitcast_fusion
  111.2 7.3 %collective-permute-done.12 = f32[128,128]{1,0:T(8,128)S(1)} collective-permute-done((f32[128,128]{1,0:T(8,128)S(1)}, f32[128,128]{1,0:T(8,128)S(1)}, u32[]{:S(2)}, u32[]{:S(2)}) %collective-permute-start.12) | collective-permute-done | bytes 65568 | tf_op jit(solution)/shard_map/ppermute | solution.py:44
  118.5 1.3 collective-permute-start.13
  119.8 0.4 convolution_bitcast_fusion.1
  120.2 3.3 %collective-permute-done.13 = f32[128,128]{1,0:T(8,128)S(1)} collective-permute-done((f32[128,128]{1,0:T(8,128)S(1)}, f32[128,128]{1,0:T(8,128)S(1)}, u32[]{:S(2)}, u32[]{:S(2)}) %collective-permute-start.13) | collective-permute-done | bytes 65568 | tf_op jit(solution)/shard_map/ppermute | solution.py:44
  123.5 6.0 %collective-permute-start.14 = (f32[128,128]{1,0:T(8,128)S(1)}, f32[128,128]{1,0:T(8,128)S(1)}, u32[]{:S(2)}, u32[]{:S(2)}) collective-permute-start(f32[128,128]{1,0:T(8,128)S(1)} %add_add_fusion), channel_id=1, source_target_pairs={{0,16},{16,0},{1,17},{17,1},{2,18},{18,2},{3,19},{19,3},{4,20},{20... | collective-permute-start | bytes 196616 | tf_op jit(solution)/shard_map/ppermute | solution.py:19
  129.5 0.3 fusion.7
  129.8 0.8 copy.53
  130.6 0.3 fusion.9
  130.9 0.8 copy.55
  131.7 0.3 fusion.8
  132.0 0.8 copy.54
  (44 shorter events, 0.4 us)
Async XLA Ops:
  7.2 69.2 %copy-start = (bf16[256,256]{1,0:T(8,128)(2,1)S(1)}, bf16[256,256]{1,0:T(8,128)(2,1)}, u32[]{:S(2)}) copy-start(bf16[256,256]{1,0:T(8,128)(2,1)} %param.5) | copy-start | bytes 393220
  7.2 14.1 %copy-start.2 = (bf16[256,256]{1,0:T(8,128)(2,1)S(1)}, bf16[256,256]{1,0:T(8,128)(2,1)}, u32[]{:S(2)}) copy-start(bf16[256,256]{1,0:T(8,128)(2,1)} %param.6) | copy-start | bytes 393220
  7.2 14.3 %copy-start.1 = (bf16[256,256]{1,0:T(8,128)(2,1)S(1)}, bf16[256,256]{1,0:T(8,128)(2,1)}, u32[]{:S(2)}) copy-start(bf16[256,256]{1,0:T(8,128)(2,1)} %param.7) | copy-start | bytes 393220
  7.2 84.3 %all-gather.2.cloned.1.call-start = ((), (), s32[]{:S(2)}) async-start(), calls=%async_computation.1 | async-start | bytes 2228224 | tf_op jit(solution)/shard_map/all_gather | solution.py:70
  11.1 65.6 %all-to-all-start = ((bf16[16,256,128]{2,1,0:T(8,128)(2,1)}), bf16[16,256,128]{2,1,0:T(8,128)(2,1)S(1)}, u32[]{:S(2)}, u32[]{:S(2)}) async-start(bf16[16,256,128]{2,1,0:T(8,128)(2,1)} %broadcast_in_dim.29), calls=%async_computation | async-start | bytes 2097152 | tf_op jit(solution)/shard_map/all_to_all | solution.py:58
  21.6 22.6 %collective-permute-start.2 = (f32[2,128,128]{2,1,0:T(8,128)S(1)}, f32[2,128,128]{2,1,0:T(8,128)S(1)}, u32[]{:S(2)}, u32[]{:S(2)}) collective-permute-start(f32[2,128,128]{2,1,0:T(8,128)S(1)} %fusion.13), channel_id=1, source_target_pairs={{0,16},{16,0},{1,17},{17,1},{2,18},{18,2},{3,19},{19,3},{4,20},{20... | collective-permute-start | bytes 393224 | tf_op jit(solution)/shard_map/ppermute | solution.py:19
  24.5 16.3 %collective-permute-start = (f32[128,128]{1,0:T(8,128)S(1)}, f32[128,128]{1,0:T(8,128)S(1)}, u32[]{:S(2)}, u32[]{:S(2)}) collective-permute-start(f32[128,128]{1,0:T(8,128)S(1)} %get-tuple-element.22), channel_id=1, source_target_pairs={{0,32},{32,64},{64,96},{96,128},{128,160},{160,192},{192,224},{224... | collective-permute-start | bytes 196616 | tf_op jit(solution)/shard_map/ppermute | solution.py:30
  28.1 16.1 %collective-permute-start.1 = (f32[128,128]{1,0:T(8,128)S(1)}, f32[128,128]{1,0:T(8,128)S(1)}, u32[]{:S(2)}, u32[]{:S(2)}) collective-permute-start(f32[128,128]{1,0:T(8,128)S(1)} %get-tuple-element.21), channel_id=1, source_target_pairs={{0,48},{16,32},{32,80},{48,64},{64,112},{80,96},{96,144},{112,128}... | collective-permute-start | bytes 196616 | tf_op jit(solution)/shard_map/ppermute | solution.py:31
  44.3 9.8 %collective-permute-start.3 = (f32[128,128]{1,0:T(8,128)S(1)}, f32[128,128]{1,0:T(8,128)S(1)}, u32[]{:S(2)}, u32[]{:S(2)}) collective-permute-start(f32[128,128]{1,0:T(8,128)S(1)} %get-tuple-element.11), channel_id=1, source_target_pairs={{0,64},{32,96},{64,128},{96,160},{128,192},{160,224},{192,256},{22... | collective-permute-start | bytes 196616 | tf_op jit(solution)/shard_map/ppermute | solution.py:44
  54.1 11.1 %collective-permute-start.4 = (f32[128,128]{1,0:T(8,128)S(1)}, f32[128,128]{1,0:T(8,128)S(1)}, u32[]{:S(2)}, u32[]{:S(2)}) collective-permute-start(f32[128,128]{1,0:T(8,128)S(1)} %add.100), channel_id=1, source_target_pairs={{0,128},{32,160},{64,192},{96,224},{128,256},{160,288},{192,320},{... | collective-permute-start | bytes 196616 | tf_op jit(solution)/shard_map/ppermute | solution.py:44
  63.9 12.8 %copy-start.7 = (pred[256,256]{1,0:T(8,128)(4,1)}, pred[256,256]{1,0:T(8,128)(4,1)S(1)}, u32[]{:S(2)}) copy-start(pred[256,256]{1,0:T(8,128)(4,1)S(1)} %iota_compare_fusion) | copy-start | bytes 196612
  65.8 18.2 %collective-permute-start.5 = (f32[128,128]{1,0:T(8,128)}, f32[128,128]{1,0:T(8,128)S(1)}, u32[]{:S(2)}, u32[]{:S(2)}) collective-permute-start(f32[128,128]{1,0:T(8,128)} %add.102), channel_id=1, source_target_pairs={{0,256},{32,288},{64,320},{96,352},{128,384},{160,416},{192,448},{... | collective-permute-start | bytes 196616 | tf_op jit(solution)/shard_map/ppermute | solution.py:44
  76.6 13.4 %collective-permute-start.7 = (bf16[16,256,128]{2,1,0:T(8,128)(2,1)S(1)}, bf16[16,256,128]{2,1,0:T(8,128)(2,1)S(1)}, u32[]{:S(2)}, u32[]{:S(2)}) collective-permute-start(bf16[16,256,128]{2,1,0:T(8,128)(2,1)S(1)} %all-to-all-done), channel_id=1, source_target_pairs={{0,16},{16,0},{1,17},{17,1},{2,18},{18,2},{3,19},{19,3},{4,20},{20... | collective-permute-start | bytes 3145736 | tf_op jit(solution)/shard_map/ppermute | solution.py:19
  84.0 0.6 copy-start.9
  85.5 3.1 %collective-permute-start.6 = (f32[128,128]{1,0:T(8,128)S(1)}, f32[128,128]{1,0:T(8,128)S(1)}, u32[]{:S(2)}, u32[]{:S(2)}) collective-permute-start(f32[128,128]{1,0:T(8,128)S(1)} %add_add_fusion.1), channel_id=1, source_target_pairs={{0,16},{16,0},{1,17},{17,1},{2,18},{18,2},{3,19},{19,3},{4,20},{20... | collective-permute-start | bytes 196616 | tf_op jit(solution)/shard_map/ppermute | solution.py:19
  88.6 1.4 copy-start.3
  88.6 1.4 copy-start.5
  94.5 9.5 %copy-start.8 = (pred[256,256]{1,0:T(8,128)(4,1)S(1)}, pred[256,256]{1,0:T(8,128)(4,1)}, u32[]{:S(2)}) copy-start(pred[256,256]{1,0:T(8,128)(4,1)} %copy-done.7) | copy-start | bytes 196612
  94.8 5.3 %collective-permute-start.8 = (f32[128,128]{1,0:T(8,128)S(1)}, f32[128,128]{1,0:T(8,128)S(1)}, u32[]{:S(2)}, u32[]{:S(2)}) collective-permute-start(f32[128,128]{1,0:T(8,128)S(1)} %get-tuple-element.18), channel_id=1, source_target_pairs={{32,0},{64,32},{96,64},{128,96},{160,128},{192,160},{224,192},{256... | collective-permute-start | bytes 196616 | tf_op jit(solution)/shard_map/ppermute | solution.py:30
  96.1 6.5 %collective-permute-start.9 = (f32[128,128]{1,0:T(8,128)S(1)}, f32[128,128]{1,0:T(8,128)S(1)}, u32[]{:S(2)}, u32[]{:S(2)}) collective-permute-start(f32[128,128]{1,0:T(8,128)S(1)} %get-tuple-element.17), channel_id=1, source_target_pairs={{32,16},{48,0},{64,48},{80,32},{96,80},{112,64},{128,112},{144,96}... | collective-permute-start | bytes 196616 | tf_op jit(solution)/shard_map/ppermute | solution.py:31
  97.4 5.2 %collective-permute-start.10 = (f32[2,128,128]{2,1,0:T(8,128)S(1)}, f32[2,128,128]{2,1,0:T(8,128)S(1)}, u32[]{:S(2)}, u32[]{:S(2)}) collective-permute-start(f32[2,128,128]{2,1,0:T(8,128)S(1)} %bitcast.148), channel_id=1, source_target_pairs={{0,16},{16,0},{1,17},{17,1},{2,18},{18,2},{3,19},{19,3},{4,20},{20... | collective-permute-start | bytes 393224 | tf_op jit(solution)/shard_map/ppermute | solution.py:19
  100.1 29.4 %copy-start.4 = (f32[1,128,128]{2,1,0:T(8,128)S(1)}, f32[1,128,128]{2,1,0:T(8,128)}, u32[]{:S(2)}) copy-start(f32[1,128,128]{2,1,0:T(8,128)} %copy-done.3) | copy-start | bytes 196612
  100.1 29.4 %copy-start.6 = (f32[1,128,128]{2,1,0:T(8,128)S(1)}, f32[1,128,128]{2,1,0:T(8,128)}, u32[]{:S(2)}) copy-start(f32[1,128,128]{2,1,0:T(8,128)} %copy-done.5) | copy-start | bytes 196612
  102.7 6.9 %collective-permute-start.11 = (f32[128,128]{1,0:T(8,128)S(1)}, f32[128,128]{1,0:T(8,128)S(1)}, u32[]{:S(2)}, u32[]{:S(2)}) collective-permute-start(f32[128,128]{1,0:T(8,128)S(1)} %get-tuple-element.9), channel_id=1, source_target_pairs={{64,0},{96,32},{128,64},{160,96},{192,128},{224,160},{256,192},{28... | collective-permute-start | bytes 196616 | tf_op jit(solution)/shard_map/ppermute | solution.py:44
  109.6 8.9 %collective-permute-start.12 = (f32[128,128]{1,0:T(8,128)S(1)}, f32[128,128]{1,0:T(8,128)S(1)}, u32[]{:S(2)}, u32[]{:S(2)}) collective-permute-start(f32[128,128]{1,0:T(8,128)S(1)} %add.113), channel_id=1, source_target_pairs={{128,0},{160,32},{192,64},{224,96},{256,128},{288,160},{320,192},{... | collective-permute-start | bytes 196616 | tf_op jit(solution)/shard_map/ppermute | solution.py:44
  118.5 5.0 %collective-permute-start.13 = (f32[128,128]{1,0:T(8,128)S(1)}, f32[128,128]{1,0:T(8,128)S(1)}, u32[]{:S(2)}, u32[]{:S(2)}) collective-permute-start(f32[128,128]{1,0:T(8,128)S(1)} %add.115), channel_id=1, source_target_pairs={{256,0},{288,32},{320,64},{352,96},{384,128},{416,160},{448,192},{... | collective-permute-start | bytes 196616 | tf_op jit(solution)/shard_map/ppermute | solution.py:44
  123.5 7.1 %collective-permute-start.14 = (f32[128,128]{1,0:T(8,128)S(1)}, f32[128,128]{1,0:T(8,128)S(1)}, u32[]{:S(2)}, u32[]{:S(2)}) collective-permute-start(f32[128,128]{1,0:T(8,128)S(1)} %add_add_fusion), channel_id=1, source_target_pairs={{0,16},{16,0},{1,17},{17,1},{2,18},{18,2},{3,19},{19,3},{4,20},{20... | collective-permute-start | bytes 196616 | tf_op jit(solution)/shard_map/ppermute | solution.py:19
Sparse Core Ops, SparseCore 0:
  11.6 66.1 all-gather.1

commit v5 on v2

--- a/solution.py
+++ b/solution.py
@@ -31,19 +31,12 @@
         within = jnp.where(core == 1, other, jnp.zeros_like(other))
     half = lax.dynamic_index_in_dim(chip_total, core, 0, keepdims=False)
     chips = lax.axis_size("ylo") * lax.axis_size("z")
-    window = half
-    below = jnp.zeros_like(half)
-    distance = 1
-    while distance < chips:
-        if backward:
-            pairs = [(q, q - distance) for q in range(distance, chips)]
-        else:
-            pairs = [(q, q + distance) for q in range(chips - distance)]
-        arrived = lax.ppermute(window, CHIPS, pairs)
-        below = below + arrived
-        if distance * 2 < chips:
-            window = window + arrived
-        distance *= 2
+    spread = jnp.broadcast_to(half[None], (chips,) + half.shape)
+    totals = lax.all_to_all(spread, CHIPS, 0, 0, tiled=True)
+    order = lax.broadcasted_iota(jnp.int32, (chips, 1, 1), 0)
+    here = lax.axis_index(CHIPS)
+    taken = order > here if backward else order < here
+    below = jnp.sum(jnp.where(taken, totals, 0.0), axis=0)
     other_half = swap_cores(below)
     head0 = jnp.where(core == 0, below, other_half)
     head1 = jnp.where(core == 0, other_half, below)

time: 139 us -> 145 us (1.043); the launches traced: 137 us -> 145 us
  waiting for transfers between devices: 36.5 us -> 71.4 us
  starting transfers between devices: 68 us -> 42.1 us
  matrix products: 8.29 us -> 6.28 us
  local copies, waits for them, and re-layouts: 6.22 us -> 7.71 us
    all_to_all x0 -> x2, waiting for transfers between devices: none -> 46.6 us  [ctx_scan(): totals = lax.all_to_all(spread, CHIPS, 0, 0, tiled=True)]
    ppermute x8 -> x0, waiting for transfers between devices: 34.2 us -> none  [ctx_scan(): arrived = lax.ppermute(window, CHIPS, pairs)]
    ppermute x8 -> x0, starting transfers between devices: 33.5 us -> none  [ctx_scan(): arrived = lax.ppermute(window, CHIPS, pairs)]
    all_to_all x1, waiting for transfers between devices: 0.01 us -> 20.4 us  [gather_columns(): mine = lax.all_to_all(spread, CHIPS, 0, 0, tiled=True)]
    all_to_all x0 -> x2, starting transfers between devices: none -> 14.4 us  [ctx_scan(): totals = lax.all_to_all(spread, CHIPS, 0, 0, tiled=True)]
    ppermute x5, starting transfers between devices: 22.5 us -> 15.6 us  [swap_cores(): return lax.ppermute(value, 'core', [(0, 1), (1, 0)])]
    broadcast_in_dim x0 -> x2, local copies, waits for them, and re-layouts: none -> 2.19 us  [ctx_scan(): spread = jnp.broadcast_to(half[None], (chips,) + half.shape)]
    all_gather x1, waiting for transfers between devices: 0.01 us -> 1.98 us  [local(): full_rows = lax.all_gather(grad_out, TP, axis=1, tiled=True)]
  transfers between devices with their start and end apart: 15 -> 9, of which waited for: 9 -> 7; matrix products, arithmetic and copies ran while one was open for 8% -> 6% of each run, Pallas kernels for 0% -> 0%
where the time goes in v5:
time: 145 us
  waiting for transfers between devices  71.4 us (49%)
  starting transfers between devices  42.1 us (29%)
  between operations  14.4 us (10%)
  local copies, waits for them, and re-layouts  7.71 us (5%)
  matrix products  6.28 us (4%)
  other arithmetic  2.85 us (2%)
    all_to_all x2, waiting for transfers between devices, ctx_scan(): totals = lax.all_to_all(spread, CHIPS, 0, 0, tiled=True)  46.6 us
    all_to_all x1, waiting for transfers between devices, gather_columns(): mine = lax.all_to_all(spread, CHIPS, 0, 0, tiled=True)  20.4 us
    ppermute x5, starting transfers between devices, swap_cores(): return lax.ppermute(value, 'core', [(0, 1), (1, 0)])  15.6 us
    all_to_all x2, starting transfers between devices, ctx_scan(): totals = lax.all_to_all(spread, CHIPS, 0, 0, tiled=True)  14.4 us
    all_to_all x1, starting transfers between devices, gather_columns(): mine = lax.all_to_all(spread, CHIPS, 0, 0, tiled=True)  12 us
    unnamed x24, local copies, waits for them, and re-layouts  3.36 us
  transfers between devices with their start and end apart: 9, of which 7 were waited for; matrix products, arithmetic and copies ran while one was open for 6% of the time, Pallas kernels for 0%

profile of v5, /device:TPU:1, one launch (start us, length us, event | category | flops | bytes accessed | tf_op | source)
XLA Modules:
  0.0 144.8 jit_solution(8844878808658716625)
XLA Ops:
  7.2 0.0 copy-start
  7.2 2.1 %broadcast_in_dim.67 = bf16[16,256,128]{2,1,0:T(8,128)(2,1)} broadcast(bf16[256,128]{1,0:T(8,128)(2,1)} %param.9), dimensions={1,2} | broadcast | bytes 1114112 | tf_op jit(solution)/shard_map/broadcast_in_dim | solution.py:48
  9.3 12.0 %all-to-all-start.1 = ((bf16[16,256,128]{2,1,0:T(8,128)(2,1)}), bf16[16,256,128]{2,1,0:T(8,128)(2,1)S(1)}, u32[]{:S(2)}, u32[]{:S(2)}) async-start(bf16[16,256,128]{2,1,0:T(8,128)(2,1)} %broadcast_in_dim.67), calls=%async_computation.1 | async-start | bytes 2097152 | tf_op jit(solution)/shard_map/all_to_all | solution.py:49
  21.3 0.0 all-gather.2.cloned.1.call-start
  21.3 0.8 copy.60
  22.1 0.0 all-gather.2.cloned.1.call-update
  22.1 0.1 copy.125
  22.2 0.2 fusion.13
  22.4 2.9 %collective-permute-start = (f32[2,128,128]{2,1,0:T(8,128)S(1)}, f32[2,128,128]{2,1,0:T(8,128)S(1)}, u32[]{:S(2)}, u32[]{:S(2)}) collective-permute-start(f32[2,128,128]{2,1,0:T(8,128)S(1)} %fusion.13), channel_id=1, source_target_pairs={{0,16},{16,0},{1,17},{17,1},{2,18},{18,2},{3,19},{19,3},{4,20},{20... | collective-permute-start | bytes 393224 | tf_op jit(solution)/shard_map/ppermute | solution.py:19
  25.3 1.0 collective-permute-done
  26.3 20.4 %all-to-all-done.1 = bf16[16,256,128]{2,1,0:T(8,128)(2,1)S(1)} async-done(((bf16[16,256,128]{2,1,0:T(8,128)(2,1)}), bf16[16,256,128]{2,1,0:T(8,128)(2,1)S(1)}, u32[]{:S(2)}, u32[]{:S(2)}) %all-to-all-start.1) | async-done | bytes 1048608 | tf_op jit(solution)/shard_map/all_to_all | solution.py:49
  46.7 1.1 broadcast_in_dim.65
  47.8 7.2 %all-to-all-start = ((f32[16,128,128]{2,1,0:T(8,128)}), f32[16,128,128]{2,1,0:T(8,128)S(1)}, u32[]{:S(2)}, u32[]{:S(2)}) async-start(f32[16,128,128]{2,1,0:T(8,128)} %broadcast_in_dim.65), calls=%async_computation | async-start | bytes 2097152 | tf_op jit(solution)/shard_map/all_to_all | solution.py:35
  55.1 0.0 copy-start.7
  55.1 0.2 convolution_select_fusion.1
  55.4 2.6 %collective-permute-start.2 = (bf16[16,256,128]{2,1,0:T(8,128)(2,1)S(1)}, bf16[16,256,128]{2,1,0:T(8,128)(2,1)}, u32[]{:S(2)}, u32[]{:S(2)}) collective-permute-start(bf16[16,256,128]{2,1,0:T(8,128)(2,1)S(1)} %all-to-all-done.1), channel_id=1, source_target_pairs={{0,16},{16,0},{1,17},{17,1},{2,18},{18,2},{3,19},{19,3},{4,20},{20... | collective-permute-start | bytes 3145736 | tf_op jit(solution)/shard_map/ppermute | solution.py:19
  57.9 22.6 %all-to-all-done = f32[16,128,128]{2,1,0:T(8,128)S(1)} async-done(((f32[16,128,128]{2,1,0:T(8,128)}), f32[16,128,128]{2,1,0:T(8,128)S(1)}, u32[]{:S(2)}, u32[]{:S(2)}) %all-to-all-start) | async-done | bytes 1048608 | tf_op jit(solution)/shard_map/all_to_all | solution.py:35
  80.6 0.1 select_reduce_fusion.1
  80.7 3.2 %collective-permute-start.1 = (f32[128,128]{1,0:T(8,128)S(1)}, f32[128,128]{1,0:T(8,128)S(1)}, u32[]{:S(2)}, u32[]{:S(2)}) collective-permute-start(f32[128,128]{1,0:T(8,128)S(1)} %select_reduce_fusion.1), channel_id=1, source_target_pairs={{0,16},{16,0},{1,17},{17,1},{2,18},{18,2},{3,19},{19,3},{4,20},{20... | collective-permute-start | bytes 196616 | tf_op jit(solution)/shard_map/ppermute | solution.py:19
  83.9 0.4 convolution_bitcast_fusion.2
  84.4 0.4 collective-permute-done.1
  84.8 0.0 copy-start.5
  84.9 0.3 multiply_reduce_fusion.1
  85.2 0.2 copy-done.3
  85.5 0.0 copy-done.5
  85.5 2.4 %select_bitcast_fusion.1 = (bf16[16,1,256,128]{3,2,1,0:T(8,128)(2,1)S(1)}, bf16[16,1,256,128]{3,2,1,0:T(8,128)(2,1)}) fusion(bf16[16,256,128]{2,1,0:T(8,128)(2,1)S(1)} %all-to-all-done.1, bf16[16,256,128]{2,1,0:T(8,128)(2,1)} %collective-permute-done.2, pred[]{:T(512)S(6)} %eq.4), kind=kLoop, calls=%fused_computation.22 | loop fusion | flops 1048576 | bytes 4194305 | tf_op jit(solution)/shard_map/stack | solution.py:54
  87.9 2.0 %all-gather.2.cloned.1.call-done = bf16[256,4096]{0,1:T(8,128)(2,1)} async-done(((bf16[256,256]{0,1:T(8,128)(2,1)}), bf16[256,4096]{0,1:T(8,128)(2,1)}) %all-gather.2.cloned.1.call-update) | async-done | bytes 2097168 | tf_op jit(solution)/shard_map/all_gather | solution.py:61
  89.8 2.6 %fusion = f32[256,256,1,1]{1,0,3,2:T(8,128)S(1)} fusion(bf16[256,16,2,128]{0,3,2,1:T(8,128)(2,1)} %bitcast.132, bf16[16,1,256,128]{3,2,1,0:T(8,128)(2,1)} %get-tuple-element.13, bf16[16,1,256,128]{3,2,1,0:T(8,128)(2,1)S(1)} %get-tuple-element.12), kind=kOutput, calls=%fused_computation | convolution fusion | flops 537919488 | bytes 4456448 | tf_op jit(solution)/shard_map/tqrk,qrjk->tj/dot_general | solution.py:63
  92.5 0.1 multiply_reduce_fusion
  92.5 0.0 copy-start.8
  92.6 0.2 convolution_bitcast_fusion.6
  92.8 3.7 %collective-permute-start.3 = (f32[2,128,128]{2,1,0:T(8,128)S(1)}, f32[2,128,128]{2,1,0:T(8,128)S(1)}, u32[]{:S(2)}, u32[]{:S(2)}) collective-permute-start(f32[2,128,128]{2,1,0:T(8,128)S(1)} %convolution_bitcast_fusion.6), channel_id=1, source_target_pairs={{0,16},{16,0},{1,17},{17,1},{2,18},{18,2},{3,19},{19,3},{4,20},{20... | collective-permute-start | bytes 393224 | tf_op jit(solution)/shard_map/ppermute | solution.py:19
  96.5 1.0 collective-permute-done.3
  97.5 1.1 broadcast_in_dim.70
  98.6 7.2 %all-to-all-start.2 = ((f32[16,128,128]{2,1,0:T(8,128)}), f32[16,128,128]{2,1,0:T(8,128)S(1)}, u32[]{:S(2)}, u32[]{:S(2)}) async-start(f32[16,128,128]{2,1,0:T(8,128)} %broadcast_in_dim.70), calls=%async_computation.2 | async-start | bytes 2097152 | tf_op jit(solution)/shard_map/all_to_all | solution.py:35
  105.8 0.3 convolution_select_fusion
  106.1 0.3 fusion.40
  106.5 0.4 convolution_bitcast_fusion
  106.8 0.4 convolution_bitcast_fusion.1
  107.3 24.0 %all-to-all-done.2 = f32[16,128,128]{2,1,0:T(8,128)S(1)} async-done(((f32[16,128,128]{2,1,0:T(8,128)}), f32[16,128,128]{2,1,0:T(8,128)S(1)}, u32[]{:S(2)}, u32[]{:S(2)}) %all-to-all-start.2) | async-done | bytes 1048608 | tf_op jit(solution)/shard_map/all_to_all | solution.py:35
  131.3 0.1 select_reduce_fusion
  131.4 3.3 %collective-permute-start.4 = (f32[128,128]{1,0:T(8,128)S(1)}, f32[128,128]{1,0:T(8,128)S(1)}, u32[]{:S(2)}, u32[]{:S(2)}) collective-permute-start(f32[128,128]{1,0:T(8,128)S(1)} %select_reduce_fusion), channel_id=1, source_target_pairs={{0,16},{16,0},{1,17},{17,1},{2,18},{18,2},{3,19},{19,3},{4,20},{20... | collective-permute-start | bytes 196616 | tf_op jit(solution)/shard_map/ppermute | solution.py:19
  134.7 0.3 fusion.7
  135.0 0.8 copy.72
  135.8 0.3 fusion.9
  136.1 0.8 copy.74
  136.9 0.3 fusion.8
  137.2 0.8 copy.73
  (26 shorter events, 0.2 us)
Async XLA Ops:
  7.2 47.9 %copy-start = (bf16[256,256]{1,0:T(8,128)(2,1)S(1)}, bf16[256,256]{1,0:T(8,128)(2,1)}, u32[]{:S(2)}) copy-start(bf16[256,256]{1,0:T(8,128)(2,1)} %param.5) | copy-start | bytes 393220
  7.2 14.1 %copy-start.9 = (bf16[256,256]{1,0:T(8,128)(2,1)S(1)}, bf16[256,256]{1,0:T(8,128)(2,1)}, u32[]{:S(2)}) copy-start(bf16[256,256]{1,0:T(8,128)(2,1)} %param.8) | copy-start | bytes 393220
  7.2 14.9 %copy-start.2 = (bf16[256,256]{1,0:T(8,128)(2,1)S(1)}, bf16[256,256]{1,0:T(8,128)(2,1)}, u32[]{:S(2)}) copy-start(bf16[256,256]{1,0:T(8,128)(2,1)} %param.6) | copy-start | bytes 393220
  7.2 15.0 %copy-start.1 = (bf16[256,256]{1,0:T(8,128)(2,1)S(1)}, bf16[256,256]{1,0:T(8,128)(2,1)}, u32[]{:S(2)}) copy-start(bf16[256,256]{1,0:T(8,128)(2,1)} %param.7) | copy-start | bytes 393220
  9.3 37.4 %all-to-all-start.1 = ((bf16[16,256,128]{2,1,0:T(8,128)(2,1)}), bf16[16,256,128]{2,1,0:T(8,128)(2,1)S(1)}, u32[]{:S(2)}, u32[]{:S(2)}) async-start(bf16[16,256,128]{2,1,0:T(8,128)(2,1)} %broadcast_in_dim.67), calls=%async_computation.1 | async-start | bytes 2097152 | tf_op jit(solution)/shard_map/all_to_all | solution.py:49
  21.3 68.6 %all-gather.2.cloned.1.call-start = ((), (), s32[]{:S(2)}) async-start(), calls=%async_computation.3 | async-start | bytes 2228224 | tf_op jit(solution)/shard_map/all_gather | solution.py:61
  22.4 3.8 %collective-permute-start = (f32[2,128,128]{2,1,0:T(8,128)S(1)}, f32[2,128,128]{2,1,0:T(8,128)S(1)}, u32[]{:S(2)}, u32[]{:S(2)}) collective-permute-start(f32[2,128,128]{2,1,0:T(8,128)S(1)} %fusion.13), channel_id=1, source_target_pairs={{0,16},{16,0},{1,17},{17,1},{2,18},{18,2},{3,19},{19,3},{4,20},{20... | collective-permute-start | bytes 393224 | tf_op jit(solution)/shard_map/ppermute | solution.py:19
  47.8 32.8 %all-to-all-start = ((f32[16,128,128]{2,1,0:T(8,128)}), f32[16,128,128]{2,1,0:T(8,128)S(1)}, u32[]{:S(2)}, u32[]{:S(2)}) async-start(f32[16,128,128]{2,1,0:T(8,128)} %broadcast_in_dim.65), calls=%async_computation | async-start | bytes 2097152 | tf_op jit(solution)/shard_map/all_to_all | solution.py:35
  55.1 30.1 %copy-start.7 = (pred[256,256]{1,0:T(8,128)(4,1)}, pred[256,256]{1,0:T(8,128)(4,1)S(1)}, u32[]{:S(2)}) copy-start(pred[256,256]{1,0:T(8,128)(4,1)S(1)} %iota_compare_fusion) | copy-start | bytes 196612
  55.4 30.1 %collective-permute-start.2 = (bf16[16,256,128]{2,1,0:T(8,128)(2,1)S(1)}, bf16[16,256,128]{2,1,0:T(8,128)(2,1)}, u32[]{:S(2)}, u32[]{:S(2)}) collective-permute-start(bf16[16,256,128]{2,1,0:T(8,128)(2,1)S(1)} %all-to-all-done.1), channel_id=1, source_target_pairs={{0,16},{16,0},{1,17},{17,1},{2,18},{18,2},{3,19},{19,3},{4,20},{20... | collective-permute-start | bytes 3145736 | tf_op jit(solution)/shard_map/ppermute | solution.py:19
  80.7 4.1 %collective-permute-start.1 = (f32[128,128]{1,0:T(8,128)S(1)}, f32[128,128]{1,0:T(8,128)S(1)}, u32[]{:S(2)}, u32[]{:S(2)}) collective-permute-start(f32[128,128]{1,0:T(8,128)S(1)} %select_reduce_fusion.1), channel_id=1, source_target_pairs={{0,16},{16,0},{1,17},{17,1},{2,18},{18,2},{3,19},{19,3},{4,20},{20... | collective-permute-start | bytes 196616 | tf_op jit(solution)/shard_map/ppermute | solution.py:19
  84.8 0.6 copy-start.3
  84.8 0.6 copy-start.5
  92.5 13.3 %copy-start.8 = (pred[256,256]{1,0:T(8,128)(4,1)S(1)}, pred[256,256]{1,0:T(8,128)(4,1)}, u32[]{:S(2)}) copy-start(pred[256,256]{1,0:T(8,128)(4,1)} %copy-done.7) | copy-start | bytes 196612
  92.8 4.7 %collective-permute-start.3 = (f32[2,128,128]{2,1,0:T(8,128)S(1)}, f32[2,128,128]{2,1,0:T(8,128)S(1)}, u32[]{:S(2)}, u32[]{:S(2)}) collective-permute-start(f32[2,128,128]{2,1,0:T(8,128)S(1)} %convolution_bitcast_fusion.6), channel_id=1, source_target_pairs={{0,16},{16,0},{1,17},{17,1},{2,18},{18,2},{3,19},{19,3},{4,20},{20... | collective-permute-start | bytes 393224 | tf_op jit(solution)/shard_map/ppermute | solution.py:19
  98.6 32.7 %all-to-all-start.2 = ((f32[16,128,128]{2,1,0:T(8,128)}), f32[16,128,128]{2,1,0:T(8,128)S(1)}, u32[]{:S(2)}, u32[]{:S(2)}) async-start(f32[16,128,128]{2,1,0:T(8,128)} %broadcast_in_dim.70), calls=%async_computation.2 | async-start | bytes 2097152 | tf_op jit(solution)/shard_map/all_to_all | solution.py:35
  106.4 28.3 %copy-start.4 = (f32[1,128,128]{2,1,0:T(8,128)S(1)}, f32[1,128,128]{2,1,0:T(8,128)}, u32[]{:S(2)}) copy-start(f32[1,128,128]{2,1,0:T(8,128)} %copy-done.3) | copy-start | bytes 196612
  106.4 28.3 %copy-start.6 = (f32[1,128,128]{2,1,0:T(8,128)S(1)}, f32[1,128,128]{2,1,0:T(8,128)}, u32[]{:S(2)}) copy-start(f32[1,128,128]{2,1,0:T(8,128)} %copy-done.5) | copy-start | bytes 196612
  131.4 4.4 %collective-permute-start.4 = (f32[128,128]{1,0:T(8,128)S(1)}, f32[128,128]{1,0:T(8,128)S(1)}, u32[]{:S(2)}, u32[]{:S(2)}) collective-permute-start(f32[128,128]{1,0:T(8,128)S(1)} %select_reduce_fusion), channel_id=1, source_target_pairs={{0,16},{16,0},{1,17},{17,1},{2,18},{18,2},{3,19},{19,3},{4,20},{20... | collective-permute-start | bytes 196616 | tf_op jit(solution)/shard_map/ppermute | solution.py:19
Sparse Core Ops, SparseCore 0:
  25.7 64.1 all-gather.1

commit v6 on v2

--- a/solution.py
+++ b/solution.py
@@ -50,6 +50,23 @@
     return jnp.stack([head0, head1]) + within
 
 
+def place_rows(w_block):
+    z_size, y_groups = lax.axis_size("z"), lax.axis_size("yhi")
+    pairs = []
+    for ylo in range(lax.axis_size("ylo")):
+        for z in range(z_size):
+            for core in range(2):
+                for yhi in range(y_groups):
+                    if z % y_groups != yhi:
+                        target_z = (z // y_groups) * y_groups + yhi
+                        source = ((ylo * z_size + z) * 2 + core) * y_groups + yhi
+                        target = ((ylo * z_size + target_z) * 2 + core) * y_groups + z % y_groups
+                        pairs.append((source, target))
+    moved = lax.ppermute(w_block, ("ylo", "z", "core", "yhi"), pairs)
+    kept = lax.axis_index("z") % y_groups == lax.axis_index("yhi")
+    return jnp.where(kept, w_block, moved)
+
+
 def gather_columns(w_block):
     chips = lax.axis_size("ylo") * lax.axis_size("z")
     spread = jnp.broadcast_to(w_block[None], (chips,) + w_block.shape)
@@ -61,18 +78,28 @@
     return jnp.stack([even, odd], axis=1)
 
 
+def output_gradient(grad_out, w_out):
+    x_size, y_groups = lax.axis_size("x"), lax.axis_size("yhi")
+    spread_rows = jnp.broadcast_to(grad_out[None], (x_size,) + grad_out.shape)
+    rows = lax.all_to_all(spread_rows, "x", 0, 0, tiled=True)
+    columns = gather_columns(place_rows(w_out))
+    columns = columns.reshape((x_size, y_groups) + columns.shape[1:])
+    tok_rows = grad_out.shape[0]
+    partial = jnp.einsum(
+        "atrk,abrjk->btj",
+        rows.reshape(x_size, tok_rows, 2, columns.shape[-1]),
+        columns,
+        preferred_element_type=jnp.float32,
+    )
+    parts = lax.all_to_all(partial, "yhi", 0, 0, tiled=True)
+    return jnp.sum(parts, axis=0)
+
+
 def local(query, key_feat, value, grad_out, w_out):
     tok_rows = query.shape[0]
     feat_width = query.shape[1]
     head_count = feat_width // E
-    full_rows = lax.all_gather(grad_out, TP, axis=1, tiled=True)
-    columns = gather_columns(w_out)
-    grad_z = jnp.einsum(
-        "tqrk,qrjk->tj",
-        full_rows.reshape(tok_rows, columns.shape[0], 2, columns.shape[3]),
-        columns,
-        preferred_element_type=jnp.float32,
-    )
+    grad_z = output_gradient(grad_out, w_out)
     query_heads = query.reshape(tok_rows, head_count, E)
     key_heads = key_feat.reshape(tok_rows, head_count, E)
     value_heads = value.reshape(tok_rows, head_count, E)

time: 139 us -> 160 us (1.15)
  blocking collectives: 0 us -> 48.3 us
  between operations: 14.4 us -> 1.03 us
  starting transfers between devices: 68 us -> 60 us
  local copies, waits for them, and re-layouts: 6.22 us -> 3.55 us
    all_to_all x0 -> x1, blocking collectives: none -> 48.3 us  [gather_columns(): mine = lax.all_to_all(spread, CHIPS, 0, 0, tiled=True)]
    ppermute x8, waiting for transfers between devices: 34.2 us -> 28.4 us  [ctx_scan(): arrived = lax.ppermute(window, CHIPS, pairs)]
    all_to_all x1 -> x2, waiting for transfers between devices: 0.01 us -> 4.65 us  [the longest x1 4.65 us: output_gradient(): rows = lax.all_to_all(spread_rows, 'x', 0, 0, tiled=True)]
    all_to_all x1 -> x2, starting transfers between devices: 12 us -> 8.06 us  [the longest x1 4.04 us: output_gradient(): parts = lax.all_to_all(partial, 'yhi', 0, 0, tiled=True)]
    ppermute x8, starting transfers between devices: 33.5 us -> 30.1 us  [ctx_scan(): arrived = lax.ppermute(window, CHIPS, pairs)]
    select_n x0 -> x2, other arithmetic: none -> 2.34 us  [the longest x1 1.48 us: gather_columns(): even = jnp.where(core == 0, mine, others)]
    broadcast_in_dim x1, local copies, waits for them, and re-layouts: 2.03 us -> 0.19 us  [gather_columns(): spread = jnp.broadcast_to(w_block[None], (chips,) + w_block.shape)]
    unnamed x22 -> x12, local copies, waits for them, and re-layouts: 4.09 us -> 2.41 us
  transfers between devices with their start and end apart: 15 -> 16, of which waited for: 9 -> 10; matrix products, arithmetic and copies ran while one was open for 8% -> 6% of each run, Pallas kernels for 0% -> 0%
where the time goes in v6:
time: 160 us; the launch traced here: 158 us
  starting transfers between devices  60 us (38%)
  blocking collectives  48.3 us (30%)
  waiting for transfers between devices  35.7 us (22%)
  matrix products  6.86 us (4%)
  local copies, waits for them, and re-layouts  3.55 us (2%)
  other arithmetic  2.69 us (2%)
    all_to_all x1, blocking collectives, gather_columns(): mine = lax.all_to_all(spread, CHIPS, 0, 0, tiled=True)  48.3 us
    ppermute x8, starting transfers between devices, ctx_scan(): arrived = lax.ppermute(window, CHIPS, pairs)  30.1 us
    ppermute x8, waiting for transfers between devices, ctx_scan(): arrived = lax.ppermute(window, CHIPS, pairs)  28.4 us
    ppermute x5, starting transfers between devices, swap_cores(): return lax.ppermute(value, 'core', [(0, 1), (1, 0)])  21 us
    all_to_all x1, waiting for transfers between devices, output_gradient(): rows = lax.all_to_all(spread_rows, 'x', 0, 0, tiled=True)  4.65 us
    all_to_all x1, starting transfers between devices, output_gradient(): parts = lax.all_to_all(partial, 'yhi', 0, 0, tiled=True)  4.04 us
    all_to_all x1, starting transfers between devices, output_gradient(): rows = lax.all_to_all(spread_rows, 'x', 0, 0, tiled=True)  4.02 us
    dot_general x1, matrix products, output_gradient(): jnp.einsum('atrk,abrjk->btj', rows.reshape(x_size, tok_rows, 2, columns.s...  3.21 us
  transfers between devices with their start and end apart: 16, of which 10 were waited for; matrix products, arithmetic and copies ran while one was open for 6% of the time, Pallas kernels for 0%

profile of v6, /device:TPU:1, one launch (start us, length us, event | category | flops | bytes accessed | tf_op | source)
XLA Modules:
  0.0 158.2 jit_solution(14529672408864721924)
XLA Ops:
  0.6 0.8 collective-permute-start.6
  1.5 0.9 broadcast_select_fusion.2
  2.3 0.2 broadcast_in_dim.35
  2.6 48.3 %all_to_all.15 = bf16[16,256,128]{2,1,0:T(8,128)(2,1)S(1)} all-to-all(bf16[16,256,128]{2,1,0:T(8,128)(2,1)S(1)} %broadcast_in_dim.35), channel_id=1, replica_groups=mesh['ylo'=2,'z'=8,'core'=2,'x'=4,'yhi'=4] {'ylo','z'}, dimensions={0} | all-to-all | bytes 2097152 | tf_op jit(solution)/shard_map/all_to_all | solution.py:73
  50.9 4.8 %collective-permute-start.7 = (bf16[16,256,128]{2,1,0:T(8,128)(2,1)S(1)}, bf16[16,256,128]{2,1,0:T(8,128)(2,1)S(1)}, u32[]{:S(2)}, u32[]{:S(2)}) collective-permute-start(bf16[16,256,128]{2,1,0:T(8,128)(2,1)S(1)} %all_to_all.15), channel_id=1, source_target_pairs={{0,16},{16,0},{1,17},{17,1},{2,18},{18,2},{3,19},{19,3},{4,20},{20... | collective-permute-start | bytes 3145736 | tf_op jit(solution)/shard_map/ppermute | solution.py:19
  55.7 0.1 copy.111
  55.8 0.2 fusion.14
  56.0 1.9 %collective-permute-start = (f32[2,128,128]{2,1,0:T(8,128)S(1)}, f32[2,128,128]{2,1,0:T(8,128)S(1)}, u32[]{:S(2)}, u32[]{:S(2)}) collective-permute-start(f32[2,128,128]{2,1,0:T(8,128)S(1)} %fusion.14), channel_id=1, source_target_pairs={{0,16},{16,0},{1,17},{17,1},{2,18},{18,2},{3,19},{19,3},{4,20},{20... | collective-permute-start | bytes 393224 | tf_op jit(solution)/shard_map/ppermute | solution.py:19
  57.9 1.3 collective-permute-done
  59.3 3.9 %collective-permute-start.1 = (f32[128,128]{1,0:T(8,128)S(1)}, f32[128,128]{1,0:T(8,128)S(1)}, u32[]{:S(2)}, u32[]{:S(2)}) collective-permute-start(f32[128,128]{1,0:T(8,128)S(1)} %add_bitcast_fusion.1), channel_id=1, source_target_pairs={{0,32},{32,64},{64,96},{96,128},{128,160},{160,192},{192,224},{224... | collective-permute-start | bytes 196616 | tf_op jit(solution)/shard_map/ppermute | solution.py:42
  63.3 0.9 broadcast_in_dim.36
  64.2 4.0 %all-to-all-start.1 = ((bf16[4,256,256]{1,2,0:T(8,128)(2,1)}), bf16[4,256,256]{1,2,0:T(8,128)(2,1)S(1)}, u32[]{:S(2)}, u32[]{:S(2)}) async-start(bf16[4,256,256]{1,2,0:T(8,128)(2,1)} %broadcast_in_dim.36), calls=%async_computation.1 | async-start | bytes 1048576 | tf_op jit(solution)/shard_map/all_to_all | solution.py:84
  68.2 2.7 %collective-permute-start.2 = (f32[128,128]{1,0:T(8,128)S(1)}, f32[128,128]{1,0:T(8,128)S(1)}, u32[]{:S(2)}, u32[]{:S(2)}) collective-permute-start(f32[128,128]{1,0:T(8,128)S(1)} %add.83), channel_id=1, source_target_pairs={{0,64},{32,96},{64,128},{96,160},{128,192},{160,224},{192,256},{22... | collective-permute-start | bytes 196616 | tf_op jit(solution)/shard_map/ppermute | solution.py:42
  70.9 1.5 broadcast_select_fusion.1
  72.4 4.6 %all-to-all-done.1 = bf16[4,256,256]{1,2,0:T(8,128)(2,1)S(1)} async-done(((bf16[4,256,256]{1,2,0:T(8,128)(2,1)}), bf16[4,256,256]{1,2,0:T(8,128)(2,1)S(1)}, u32[]{:S(2)}, u32[]{:S(2)}) %all-to-all-start.1) | async-done | bytes 524320 | tf_op jit(solution)/shard_map/all_to_all | solution.py:84
  77.1 3.2 %fusion.2 = f32[4,256,256]{1,2,0:T(8,128)} fusion(bf16[4,256,2,128,1]{1,3,2,4,0:T(8,128)(2,1)S(1)} %bitcast.131, bf16[4,4,1,256,128]{4,3,1,0,2:T(8,128)(2,1)} %bitcast.130, bf16[4,4,1,256,128]{4,3,1,0,2:T(8,128)(2,1)} %bitcast.129), kind=kOutput, calls=%fused_computation.3 | convolution fusion | flops 537919488 | bytes 3670016 | tf_op jit(solution)/shard_map/atrk,abrjk->btj/dot_general | solution.py:88
  80.3 4.0 %all-to-all-start.2 = ((f32[4,256,256]{1,2,0:T(8,128)}), f32[4,256,256]{1,2,0:T(8,128)S(1)}, u32[]{:S(2)}, u32[]{:S(2)}) async-start(f32[4,256,256]{1,2,0:T(8,128)} %fusion.2), calls=%async_computation.2 | async-start | bytes 2097152 | tf_op jit(solution)/shard_map/all_to_all | solution.py:94
  84.3 3.7 %collective-permute-start.3 = (f32[128,128]{1,0:T(8,128)S(1)}, f32[128,128]{1,0:T(8,128)S(1)}, u32[]{:S(2)}, u32[]{:S(2)}) collective-permute-start(f32[128,128]{1,0:T(8,128)S(1)} %add.85), channel_id=1, source_target_pairs={{0,128},{32,160},{64,192},{96,224},{128,256},{160,288},{192,320},{... | collective-permute-start | bytes 196616 | tf_op jit(solution)/shard_map/ppermute | solution.py:42
  88.0 1.3 collective-permute-done.3
  89.3 14.7 %collective-permute-start.4 = (f32[128,128]{1,0:T(8,128)S(1)}, f32[128,128]{1,0:T(8,128)S(1)}, u32[]{:S(2)}, u32[]{:S(2)}) collective-permute-start(f32[128,128]{1,0:T(8,128)S(1)} %add.87), channel_id=1, source_target_pairs={{0,256},{32,288},{64,320},{96,352},{128,384},{160,416},{192,448},{... | collective-permute-start | bytes 196616 | tf_op jit(solution)/shard_map/ppermute | solution.py:42
  104.0 0.2 convolution_select_fusion.1
  104.2 6.7 %collective-permute-done.4 = f32[128,128]{1,0:T(8,128)S(1)} collective-permute-done((f32[128,128]{1,0:T(8,128)S(1)}, f32[128,128]{1,0:T(8,128)S(1)}, u32[]{:S(2)}, u32[]{:S(2)}) %collective-permute-start.4) | collective-permute-done | bytes 65568 | tf_op jit(solution)/shard_map/ppermute | solution.py:42
  110.9 4.7 %collective-permute-start.5 = (f32[128,128]{1,0:T(8,128)S(1)}, f32[128,128]{1,0:T(8,128)S(1)}, u32[]{:S(2)}, u32[]{:S(2)}) collective-permute-start(f32[128,128]{1,0:T(8,128)S(1)} %add_add_fusion.1), channel_id=1, source_target_pairs={{0,16},{16,0},{1,17},{17,1},{2,18},{18,2},{3,19},{19,3},{4,20},{20... | collective-permute-start | bytes 196616 | tf_op jit(solution)/shard_map/ppermute | solution.py:19
  115.6 0.4 convolution_bitcast_fusion.2
  116.1 0.4 collective-permute-done.5
  116.5 0.3 multiply_reduce_fusion.1
  117.1 0.2 convolution_bitcast_fusion.6
  117.3 2.3 %collective-permute-start.8 = (f32[2,128,128]{2,1,0:T(8,128)S(1)}, f32[2,128,128]{2,1,0:T(8,128)S(1)}, u32[]{:S(2)}, u32[]{:S(2)}) collective-permute-start(f32[2,128,128]{2,1,0:T(8,128)S(1)} %convolution_bitcast_fusion.6), channel_id=1, source_target_pairs={{0,16},{16,0},{1,17},{17,1},{2,18},{18,2},{3,19},{19,3},{4,20},{20... | collective-permute-start | bytes 393224 | tf_op jit(solution)/shard_map/ppermute | solution.py:19
  119.6 1.0 collective-permute-done.8
  120.6 1.3 collective-permute-start.9
  121.9 0.3 fusion.40
  122.2 3.4 %collective-permute-done.9 = f32[128,128]{1,0:T(8,128)S(1)} collective-permute-done((f32[128,128]{1,0:T(8,128)S(1)}, f32[128,128]{1,0:T(8,128)S(1)}, u32[]{:S(2)}, u32[]{:S(2)}) %collective-permute-start.9) | collective-permute-done | bytes 65568 | tf_op jit(solution)/shard_map/ppermute | solution.py:42
  125.6 1.3 collective-permute-start.10
  126.9 0.3 convolution_select_fusion
  127.2 6.5 %collective-permute-done.10 = f32[128,128]{1,0:T(8,128)S(1)} collective-permute-done((f32[128,128]{1,0:T(8,128)S(1)}, f32[128,128]{1,0:T(8,128)S(1)}, u32[]{:S(2)}, u32[]{:S(2)}) %collective-permute-start.10) | collective-permute-done | bytes 65568 | tf_op jit(solution)/shard_map/ppermute | solution.py:42
  133.7 1.3 collective-permute-start.11
  135.0 0.4 convolution_bitcast_fusion
  135.3 7.3 %collective-permute-done.11 = f32[128,128]{1,0:T(8,128)S(1)} collective-permute-done((f32[128,128]{1,0:T(8,128)S(1)}, f32[128,128]{1,0:T(8,128)S(1)}, u32[]{:S(2)}, u32[]{:S(2)}) %collective-permute-start.11) | collective-permute-done | bytes 65568 | tf_op jit(solution)/shard_map/ppermute | solution.py:42
  142.6 1.3 collective-permute-start.12
  143.9 0.4 convolution_bitcast_fusion.1
  144.4 3.3 %collective-permute-done.12 = f32[128,128]{1,0:T(8,128)S(1)} collective-permute-done((f32[128,128]{1,0:T(8,128)S(1)}, f32[128,128]{1,0:T(8,128)S(1)}, u32[]{:S(2)}, u32[]{:S(2)}) %collective-permute-start.12) | collective-permute-done | bytes 65568 | tf_op jit(solution)/shard_map/ppermute | solution.py:42
  147.6 7.3 %collective-permute-start.13 = (f32[128,128]{1,0:T(8,128)S(1)}, f32[128,128]{1,0:T(8,128)S(1)}, u32[]{:S(2)}, u32[]{:S(2)}) collective-permute-start(f32[128,128]{1,0:T(8,128)S(1)} %add_add_fusion), channel_id=1, source_target_pairs={{0,16},{16,0},{1,17},{17,1},{2,18},{18,2},{3,19},{19,3},{4,20},{20... | collective-permute-start | bytes 196616 | tf_op jit(solution)/shard_map/ppermute | solution.py:19
  155.0 0.3 fusion.8
  155.3 0.8 copy.49
  156.0 0.3 fusion.10
  156.4 0.8 copy.51
  157.1 0.3 fusion.9
  157.4 0.8 copy.50
  (33 shorter events, 0.5 us)
Async XLA Ops:
  0.6 103.4 %copy-start = (bf16[256,256]{1,0:T(8,128)(2,1)S(1)}, bf16[256,256]{1,0:T(8,128)(2,1)}, u32[]{:S(2)}) copy-start(bf16[256,256]{1,0:T(8,128)(2,1)} %param.5) | copy-start | bytes 393220
  0.6 0.8 collective-permute-start.6
  2.5 53.2 %copy-start.2 = (bf16[256,256]{1,0:T(8,128)(2,1)S(1)}, bf16[256,256]{1,0:T(8,128)(2,1)}, u32[]{:S(2)}) copy-start(bf16[256,256]{1,0:T(8,128)(2,1)} %param.6) | copy-start | bytes 393220
  2.5 53.3 %copy-start.1 = (bf16[256,256]{1,0:T(8,128)(2,1)S(1)}, bf16[256,256]{1,0:T(8,128)(2,1)}, u32[]{:S(2)}) copy-start(bf16[256,256]{1,0:T(8,128)(2,1)} %param.7) | copy-start | bytes 393220
  2.6 60.7 %copy-start.3 = (bf16[256,256]{1,0:T(8,128)(2,1)S(1)}, bf16[256,256]{1,0:T(8,128)(2,1)}, u32[]{:S(2)}) copy-start(bf16[256,256]{1,0:T(8,128)(2,1)} %param.8) | copy-start | bytes 393220
  50.9 20.1 %collective-permute-start.7 = (bf16[16,256,128]{2,1,0:T(8,128)(2,1)S(1)}, bf16[16,256,128]{2,1,0:T(8,128)(2,1)S(1)}, u32[]{:S(2)}, u32[]{:S(2)}) collective-permute-start(bf16[16,256,128]{2,1,0:T(8,128)(2,1)S(1)} %all_to_all.15), channel_id=1, source_target_pairs={{0,16},{16,0},{1,17},{17,1},{2,18},{18,2},{3,19},{19,3},{4,20},{20... | collective-permute-start | bytes 3145736 | tf_op jit(solution)/shard_map/ppermute | solution.py:19
  56.0 3.2 %collective-permute-start = (f32[2,128,128]{2,1,0:T(8,128)S(1)}, f32[2,128,128]{2,1,0:T(8,128)S(1)}, u32[]{:S(2)}, u32[]{:S(2)}) collective-permute-start(f32[2,128,128]{2,1,0:T(8,128)S(1)} %fusion.14), channel_id=1, source_target_pairs={{0,16},{16,0},{1,17},{17,1},{2,18},{18,2},{3,19},{19,3},{4,20},{20... | collective-permute-start | bytes 393224 | tf_op jit(solution)/shard_map/ppermute | solution.py:19
  59.3 8.9 %collective-permute-start.1 = (f32[128,128]{1,0:T(8,128)S(1)}, f32[128,128]{1,0:T(8,128)S(1)}, u32[]{:S(2)}, u32[]{:S(2)}) collective-permute-start(f32[128,128]{1,0:T(8,128)S(1)} %add_bitcast_fusion.1), channel_id=1, source_target_pairs={{0,32},{32,64},{64,96},{96,128},{128,160},{160,192},{192,224},{224... | collective-permute-start | bytes 196616 | tf_op jit(solution)/shard_map/ppermute | solution.py:42
  64.2 12.9 %all-to-all-start.1 = ((bf16[4,256,256]{1,2,0:T(8,128)(2,1)}), bf16[4,256,256]{1,2,0:T(8,128)(2,1)S(1)}, u32[]{:S(2)}, u32[]{:S(2)}) async-start(bf16[4,256,256]{1,2,0:T(8,128)(2,1)} %broadcast_in_dim.36), calls=%async_computation.1 | async-start | bytes 1048576 | tf_op jit(solution)/shard_map/all_to_all | solution.py:84
  68.2 16.1 %collective-permute-start.2 = (f32[128,128]{1,0:T(8,128)S(1)}, f32[128,128]{1,0:T(8,128)S(1)}, u32[]{:S(2)}, u32[]{:S(2)}) collective-permute-start(f32[128,128]{1,0:T(8,128)S(1)} %add.83), channel_id=1, source_target_pairs={{0,64},{32,96},{64,128},{96,160},{128,192},{160,224},{192,256},{22... | collective-permute-start | bytes 196616 | tf_op jit(solution)/shard_map/ppermute | solution.py:42
  80.3 36.6 %all-to-all-start.2 = ((f32[4,256,256]{1,2,0:T(8,128)}), f32[4,256,256]{1,2,0:T(8,128)S(1)}, u32[]{:S(2)}, u32[]{:S(2)}) async-start(f32[4,256,256]{1,2,0:T(8,128)} %fusion.2), calls=%async_computation.2 | async-start | bytes 2097152 | tf_op jit(solution)/shard_map/all_to_all | solution.py:94
  84.3 5.0 %collective-permute-start.3 = (f32[128,128]{1,0:T(8,128)S(1)}, f32[128,128]{1,0:T(8,128)S(1)}, u32[]{:S(2)}, u32[]{:S(2)}) collective-permute-start(f32[128,128]{1,0:T(8,128)S(1)} %add.85), channel_id=1, source_target_pairs={{0,128},{32,160},{64,192},{96,224},{128,256},{160,288},{192,320},{... | collective-permute-start | bytes 196616 | tf_op jit(solution)/shard_map/ppermute | solution.py:42
  89.3 21.6 %collective-permute-start.4 = (f32[128,128]{1,0:T(8,128)S(1)}, f32[128,128]{1,0:T(8,128)S(1)}, u32[]{:S(2)}, u32[]{:S(2)}) collective-permute-start(f32[128,128]{1,0:T(8,128)S(1)} %add.87), channel_id=1, source_target_pairs={{0,256},{32,288},{64,320},{96,352},{128,384},{160,416},{192,448},{... | collective-permute-start | bytes 196616 | tf_op jit(solution)/shard_map/ppermute | solution.py:42
  110.9 5.5 %collective-permute-start.5 = (f32[128,128]{1,0:T(8,128)S(1)}, f32[128,128]{1,0:T(8,128)S(1)}, u32[]{:S(2)}, u32[]{:S(2)}) collective-permute-start(f32[128,128]{1,0:T(8,128)S(1)} %add_add_fusion.1), channel_id=1, source_target_pairs={{0,16},{16,0},{1,17},{17,1},{2,18},{18,2},{3,19},{19,3},{4,20},{20... | collective-permute-start | bytes 196616 | tf_op jit(solution)/shard_map/ppermute | solution.py:19
  117.3 3.2 %collective-permute-start.8 = (f32[2,128,128]{2,1,0:T(8,128)S(1)}, f32[2,128,128]{2,1,0:T(8,128)S(1)}, u32[]{:S(2)}, u32[]{:S(2)}) collective-permute-start(f32[2,128,128]{2,1,0:T(8,128)S(1)} %convolution_bitcast_fusion.6), channel_id=1, source_target_pairs={{0,16},{16,0},{1,17},{17,1},{2,18},{18,2},{3,19},{19,3},{4,20},{20... | collective-permute-start | bytes 393224 | tf_op jit(solution)/shard_map/ppermute | solution.py:19
  120.6 5.0 %collective-permute-start.9 = (f32[128,128]{1,0:T(8,128)S(1)}, f32[128,128]{1,0:T(8,128)S(1)}, u32[]{:S(2)}, u32[]{:S(2)}) collective-permute-start(f32[128,128]{1,0:T(8,128)S(1)} %add_bitcast_fusion), channel_id=1, source_target_pairs={{32,0},{64,32},{96,64},{128,96},{160,128},{192,160},{224,192},{256... | collective-permute-start | bytes 196616 | tf_op jit(solution)/shard_map/ppermute | solution.py:42
  125.6 8.1 %collective-permute-start.10 = (f32[128,128]{1,0:T(8,128)S(1)}, f32[128,128]{1,0:T(8,128)S(1)}, u32[]{:S(2)}, u32[]{:S(2)}) collective-permute-start(f32[128,128]{1,0:T(8,128)S(1)} %add.96), channel_id=1, source_target_pairs={{64,0},{96,32},{128,64},{160,96},{192,128},{224,160},{256,192},{28... | collective-permute-start | bytes 196616 | tf_op jit(solution)/shard_map/ppermute | solution.py:42
  133.7 8.9 %collective-permute-start.11 = (f32[128,128]{1,0:T(8,128)S(1)}, f32[128,128]{1,0:T(8,128)S(1)}, u32[]{:S(2)}, u32[]{:S(2)}) collective-permute-start(f32[128,128]{1,0:T(8,128)S(1)} %add.98), channel_id=1, source_target_pairs={{128,0},{160,32},{192,64},{224,96},{256,128},{288,160},{320,192},{... | collective-permute-start | bytes 196616 | tf_op jit(solution)/shard_map/ppermute | solution.py:42
  142.6 5.0 %collective-permute-start.12 = (f32[128,128]{1,0:T(8,128)S(1)}, f32[128,128]{1,0:T(8,128)S(1)}, u32[]{:S(2)}, u32[]{:S(2)}) collective-permute-start(f32[128,128]{1,0:T(8,128)S(1)} %add.100), channel_id=1, source_target_pairs={{256,0},{288,32},{320,64},{352,96},{384,128},{416,160},{448,192},{... | collective-permute-start | bytes 196616 | tf_op jit(solution)/shard_map/ppermute | solution.py:42
  147.6 8.4 %collective-permute-start.13 = (f32[128,128]{1,0:T(8,128)S(1)}, f32[128,128]{1,0:T(8,128)S(1)}, u32[]{:S(2)}, u32[]{:S(2)}) collective-permute-start(f32[128,128]{1,0:T(8,128)S(1)} %add_add_fusion), channel_id=1, source_target_pairs={{0,16},{16,0},{1,17},{17,1},{2,18},{18,2},{3,19},{19,3},{4,20},{20... | collective-permute-start | bytes 196616 | tf_op jit(solution)/shard_map/ppermute | solution.py:19

commit v7 on v6

--- a/solution.py
+++ b/solution.py
@@ -80,8 +80,12 @@
 
 def output_gradient(grad_out, w_out):
     x_size, y_groups = lax.axis_size("x"), lax.axis_size("yhi")
-    spread_rows = jnp.broadcast_to(grad_out[None], (x_size,) + grad_out.shape)
-    rows = lax.all_to_all(spread_rows, "x", 0, 0, tiled=True)
+    here = lax.axis_index("x")
+    shifted = [grad_out] + [
+        lax.ppermute(grad_out, "x", [(i, (i - shift) % x_size) for i in range(x_size)])
+        for shift in range(1, x_size)
+    ]
+    rows = jnp.roll(jnp.stack(shifted), here, axis=0)
     columns = gather_columns(place_rows(w_out))
     columns = columns.reshape((x_size, y_groups) + columns.shape[1:])
     tok_rows = grad_out.shape[0]

time: 160 us -> 145 us (0.906)
  blocking collectives: 48.3 us -> 0 us
  starting transfers between devices: 60 us -> 92 us
  waiting for transfers between devices: 35.7 us -> 41 us
    all_to_all x1 -> x0, blocking collectives: 48.3 us -> none  [gather_columns(): mine = lax.all_to_all(spread, CHIPS, 0, 0, tiled=True)]
    all_to_all x1, starting transfers between devices: 4.02 us -> 24.1 us  [gather_columns(): mine = lax.all_to_all(spread, CHIPS, 0, 0, tiled=True)]
    ppermute x0 -> x3, starting transfers between devices: none -> 9.33 us  [output_gradient(): lax.ppermute(grad_out, 'x', [(i, (i - shift) % x_size) for i in range(x_s...]
    ppermute x8, starting transfers between devices: 30.1 us -> 35 us  [ctx_scan(): arrived = lax.ppermute(window, CHIPS, pairs)]
    ppermute x8, waiting for transfers between devices: 28.4 us -> 31.3 us  [ctx_scan(): arrived = lax.ppermute(window, CHIPS, pairs)]
    all_to_all x1, waiting for transfers between devices: 4.65 us -> 7.36 us  [gather_columns(): mine = lax.all_to_all(spread, CHIPS, 0, 0, tiled=True)]
    ppermute x5, starting transfers between devices: 21 us -> 18.6 us  [swap_cores(): return lax.ppermute(value, 'core', [(0, 1), (1, 0)])]
  transfers between devices with their start and end apart: 16 -> 19, of which waited for: 10 -> 10; matrix products, arithmetic and copies ran while one was open for 6% -> 4% of each run, Pallas kernels for 0% -> 0%
where the time goes in v7:
time: 145 us
  starting transfers between devices  92 us (63%)
  waiting for transfers between devices  41 us (28%)
  matrix products  5.36 us (4%)
  local copies, waits for them, and re-layouts  3.83 us (3%)
    ppermute x8, starting transfers between devices, ctx_scan(): arrived = lax.ppermute(window, CHIPS, pairs)  35 us
    ppermute x8, waiting for transfers between devices, ctx_scan(): arrived = lax.ppermute(window, CHIPS, pairs)  31.3 us
    all_to_all x1, starting transfers between devices, gather_columns(): mine = lax.all_to_all(spread, CHIPS, 0, 0, tiled=True)  24.1 us
    ppermute x5, starting transfers between devices, swap_cores(): return lax.ppermute(value, 'core', [(0, 1), (1, 0)])  18.6 us
    ppermute x3, starting transfers between devices, output_gradient(): lax.ppermute(grad_out, 'x', [(i, (i - shift) % x_size) for i in range(x_s...  9.33 us
    all_to_all x1, waiting for transfers between devices, gather_columns(): mine = lax.all_to_all(spread, CHIPS, 0, 0, tiled=True)  7.36 us
    all_to_all x1, starting transfers between devices, output_gradient(): parts = lax.all_to_all(partial, 'yhi', 0, 0, tiled=True)  4.18 us
  transfers between devices with their start and end apart: 19, of which 10 were waited for; matrix products, arithmetic and copies ran while one was open for 4% of the time, Pallas kernels for 0%

profile of v7, /device:TPU:1, one launch (start us, length us, event | category | flops | bytes accessed | tf_op | source)
XLA Modules:
  0.0 144.7 jit_solution(7404574019158304857)
XLA Ops:
  0.6 0.8 collective-permute-start.6
  1.5 0.9 broadcast_select_fusion.2
  2.3 1.2 broadcast_in_dim.29
  3.5 24.1 %all-to-all-start = ((bf16[16,256,128]{2,1,0:T(8,128)(2,1)}), bf16[16,256,128]{2,1,0:T(8,128)(2,1)S(1)}, u32[]{:S(2)}, u32[]{:S(2)}) async-start(bf16[16,256,128]{2,1,0:T(8,128)(2,1)} %broadcast_in_dim.29), calls=%async_computation | async-start | bytes 2097152 | tf_op jit(solution)/shard_map/all_to_all | solution.py:73
  27.8 4.4 %collective-permute-start.8 = (bf16[256,256]{0,1:T(8,128)(2,1)S(1)}, bf16[256,256]{0,1:T(8,128)(2,1)S(1)}, u32[]{:S(2)}, u32[]{:S(2)}) collective-permute-start(bf16[256,256]{0,1:T(8,128)(2,1)S(1)} %copy.37), channel_id=1, source_target_pairs={{0,12},{4,0},{8,4},{12,8},{1,13},{5,1},{9,5},{13,9},{2,14},{6,2},{... | collective-permute-start | bytes 393224 | tf_op jit(solution)/shard_map/ppermute | solution.py:85
  32.1 2.4 %collective-permute-start.9 = (bf16[256,256]{0,1:T(8,128)(2,1)S(1)}, bf16[256,256]{0,1:T(8,128)(2,1)S(1)}, u32[]{:S(2)}, u32[]{:S(2)}) collective-permute-start(bf16[256,256]{0,1:T(8,128)(2,1)S(1)} %copy.37), channel_id=1, source_target_pairs={{0,8},{4,12},{8,0},{12,4},{1,9},{5,13},{9,1},{13,5},{2,10},{6,14},... | collective-permute-start | bytes 393224 | tf_op jit(solution)/shard_map/ppermute | solution.py:85
  34.6 2.5 %collective-permute-start.10 = (bf16[256,256]{0,1:T(8,128)(2,1)S(1)}, bf16[256,256]{0,1:T(8,128)(2,1)S(1)}, u32[]{:S(2)}, u32[]{:S(2)}) collective-permute-start(bf16[256,256]{0,1:T(8,128)(2,1)S(1)} %copy.37), channel_id=1, source_target_pairs={{0,4},{4,8},{8,12},{12,0},{1,5},{5,9},{9,13},{13,1},{2,6},{6,10},{... | collective-permute-start | bytes 393224 | tf_op jit(solution)/shard_map/ppermute | solution.py:85
  37.2 0.2 fusion.14
  37.4 3.6 %collective-permute-start = (f32[2,128,128]{2,1,0:T(8,128)S(1)}, f32[2,128,128]{2,1,0:T(8,128)S(1)}, u32[]{:S(2)}, u32[]{:S(2)}) collective-permute-start(f32[2,128,128]{2,1,0:T(8,128)S(1)} %fusion.14), channel_id=1, source_target_pairs={{0,16},{16,0},{1,17},{17,1},{2,18},{18,2},{3,19},{19,3},{4,20},{20... | collective-permute-start | bytes 393224 | tf_op jit(solution)/shard_map/ppermute | solution.py:19
  41.1 0.9 collective-permute-done
  42.0 3.5 %collective-permute-start.1 = (f32[128,128]{1,0:T(8,128)S(1)}, f32[128,128]{1,0:T(8,128)S(1)}, u32[]{:S(2)}, u32[]{:S(2)}) collective-permute-start(f32[128,128]{1,0:T(8,128)S(1)} %add_bitcast_fusion.1), channel_id=1, source_target_pairs={{0,32},{32,64},{64,96},{96,128},{128,160},{160,192},{192,224},{224... | collective-permute-start | bytes 196616 | tf_op jit(solution)/shard_map/ppermute | solution.py:42
  45.6 7.4 %all-to-all-done = bf16[16,256,128]{2,1,0:T(8,128)(2,1)S(1)} async-done(((bf16[16,256,128]{2,1,0:T(8,128)(2,1)}), bf16[16,256,128]{2,1,0:T(8,128)(2,1)S(1)}, u32[]{:S(2)}, u32[]{:S(2)}) %all-to-all-start) | async-done | bytes 1048608 | tf_op jit(solution)/shard_map/all_to_all | solution.py:73
  53.0 3.3 %collective-permute-start.7 = (bf16[16,256,128]{2,1,0:T(8,128)(2,1)S(1)}, bf16[16,256,128]{2,1,0:T(8,128)(2,1)S(1)}, u32[]{:S(2)}, u32[]{:S(2)}) collective-permute-start(bf16[16,256,128]{2,1,0:T(8,128)(2,1)S(1)} %all-to-all-done), channel_id=1, source_target_pairs={{0,16},{16,0},{1,17},{17,1},{2,18},{18,2},{3,19},{19,3},{4,20},{20... | collective-permute-start | bytes 3145736 | tf_op jit(solution)/shard_map/ppermute | solution.py:19
  56.5 4.7 %collective-permute-start.2 = (f32[128,128]{1,0:T(8,128)S(1)}, f32[128,128]{1,0:T(8,128)S(1)}, u32[]{:S(2)}, u32[]{:S(2)}) collective-permute-start(f32[128,128]{1,0:T(8,128)S(1)} %add.93), channel_id=1, source_target_pairs={{0,64},{32,96},{64,128},{96,160},{128,192},{160,224},{192,256},{22... | collective-permute-start | bytes 196616 | tf_op jit(solution)/shard_map/ppermute | solution.py:42
  61.2 0.1 broadcast_select_fusion.1
  61.3 1.7 %fusion.2 = f32[4,256,256]{1,2,0:T(8,128)} fusion(bf16[4,256,2,128,1]{1,3,2,4,0:T(8,128)(2,1)S(1)} %bitcast.143, bf16[4,4,1,256,128]{4,3,1,0,2:T(8,128)(2,1)S(1)} %bitcast.142, bf16[4,4,1,256,128]{4,3,1,0,2:T(8,128)(2,1)S(1)} %bitcast.141), kind=kOutput, calls=%fused_computation.3 | convolution fusion | flops 537919488 | bytes 3670016 | tf_op jit(solution)/shard_map/atrk,abrjk->btj/dot_general | solution.py:92
  63.0 4.2 %all-to-all-start.1 = ((f32[4,256,256]{1,2,0:T(8,128)}), f32[4,256,256]{1,2,0:T(8,128)S(1)}, u32[]{:S(2)}, u32[]{:S(2)}) async-start(f32[4,256,256]{1,2,0:T(8,128)} %fusion.2), calls=%async_computation.1 | async-start | bytes 2097152 | tf_op jit(solution)/shard_map/all_to_all | solution.py:98
  67.2 4.8 %collective-permute-start.3 = (f32[128,128]{1,0:T(8,128)S(1)}, f32[128,128]{1,0:T(8,128)S(1)}, u32[]{:S(2)}, u32[]{:S(2)}) collective-permute-start(f32[128,128]{1,0:T(8,128)S(1)} %add.95), channel_id=1, source_target_pairs={{0,128},{32,160},{64,192},{96,224},{128,256},{160,288},{192,320},{... | collective-permute-start | bytes 196616 | tf_op jit(solution)/shard_map/ppermute | solution.py:42
  72.1 1.3 collective-permute-done.3
  73.4 16.8 %collective-permute-start.4 = (f32[128,128]{1,0:T(8,128)S(1)}, f32[128,128]{1,0:T(8,128)S(1)}, u32[]{:S(2)}, u32[]{:S(2)}) collective-permute-start(f32[128,128]{1,0:T(8,128)S(1)} %add.97), channel_id=1, source_target_pairs={{0,256},{32,288},{64,320},{96,352},{128,384},{160,416},{192,448},{... | collective-permute-start | bytes 196616 | tf_op jit(solution)/shard_map/ppermute | solution.py:42
  90.2 0.2 convolution_select_fusion.1
  90.4 4.5 %collective-permute-done.4 = f32[128,128]{1,0:T(8,128)S(1)} collective-permute-done((f32[128,128]{1,0:T(8,128)S(1)}, f32[128,128]{1,0:T(8,128)S(1)}, u32[]{:S(2)}, u32[]{:S(2)}) %collective-permute-start.4) | collective-permute-done | bytes 65568 | tf_op jit(solution)/shard_map/ppermute | solution.py:42
  95.0 2.4 %collective-permute-start.5 = (f32[128,128]{1,0:T(8,128)S(1)}, f32[128,128]{1,0:T(8,128)S(1)}, u32[]{:S(2)}, u32[]{:S(2)}) collective-permute-start(f32[128,128]{1,0:T(8,128)S(1)} %add_add_fusion.1), channel_id=1, source_target_pairs={{0,16},{16,0},{1,17},{17,1},{2,18},{18,2},{3,19},{19,3},{4,20},{20... | collective-permute-start | bytes 196616 | tf_op jit(solution)/shard_map/ppermute | solution.py:19
  97.4 0.4 convolution_bitcast_fusion.2
  97.9 0.4 collective-permute-done.5
  98.3 0.3 multiply_reduce_fusion.1
  98.9 0.2 convolution_bitcast_fusion.6
  99.1 2.3 %collective-permute-start.11 = (f32[2,128,128]{2,1,0:T(8,128)S(1)}, f32[2,128,128]{2,1,0:T(8,128)S(1)}, u32[]{:S(2)}, u32[]{:S(2)}) collective-permute-start(f32[2,128,128]{2,1,0:T(8,128)S(1)} %convolution_bitcast_fusion.6), channel_id=1, source_target_pairs={{0,16},{16,0},{1,17},{17,1},{2,18},{18,2},{3,19},{19,3},{4,20},{20... | collective-permute-start | bytes 393224 | tf_op jit(solution)/shard_map/ppermute | solution.py:19
  101.4 1.0 collective-permute-done.11
  102.4 1.3 collective-permute-start.12
  103.7 0.4 fusion.40
  104.0 3.4 %collective-permute-done.12 = f32[128,128]{1,0:T(8,128)S(1)} collective-permute-done((f32[128,128]{1,0:T(8,128)S(1)}, f32[128,128]{1,0:T(8,128)S(1)}, u32[]{:S(2)}, u32[]{:S(2)}) %collective-permute-start.12) | collective-permute-done | bytes 65568 | tf_op jit(solution)/shard_map/ppermute | solution.py:42
  107.4 1.3 collective-permute-start.13
  108.7 0.3 convolution_select_fusion
  109.0 11.6 %collective-permute-done.13 = f32[128,128]{1,0:T(8,128)S(1)} collective-permute-done((f32[128,128]{1,0:T(8,128)S(1)}, f32[128,128]{1,0:T(8,128)S(1)}, u32[]{:S(2)}, u32[]{:S(2)}) %collective-permute-start.13) | collective-permute-done | bytes 65568 | tf_op jit(solution)/shard_map/ppermute | solution.py:42
  120.5 1.3 collective-permute-start.14
  121.8 0.4 convolution_bitcast_fusion
  122.2 7.3 %collective-permute-done.14 = f32[128,128]{1,0:T(8,128)S(1)} collective-permute-done((f32[128,128]{1,0:T(8,128)S(1)}, f32[128,128]{1,0:T(8,128)S(1)}, u32[]{:S(2)}, u32[]{:S(2)}) %collective-permute-start.14) | collective-permute-done | bytes 65568 | tf_op jit(solution)/shard_map/ppermute | solution.py:42
  129.5 1.3 collective-permute-start.15
  130.8 0.4 convolution_bitcast_fusion.1
  131.2 3.3 %collective-permute-done.15 = f32[128,128]{1,0:T(8,128)S(1)} collective-permute-done((f32[128,128]{1,0:T(8,128)S(1)}, f32[128,128]{1,0:T(8,128)S(1)}, u32[]{:S(2)}, u32[]{:S(2)}) %collective-permute-start.15) | collective-permute-done | bytes 65568 | tf_op jit(solution)/shard_map/ppermute | solution.py:42
  134.5 7.0 %collective-permute-start.16 = (f32[128,128]{1,0:T(8,128)S(1)}, f32[128,128]{1,0:T(8,128)S(1)}, u32[]{:S(2)}, u32[]{:S(2)}) collective-permute-start(f32[128,128]{1,0:T(8,128)S(1)} %add_add_fusion), channel_id=1, source_target_pairs={{0,16},{16,0},{1,17},{17,1},{2,18},{18,2},{3,19},{19,3},{4,20},{20... | collective-permute-start | bytes 196616 | tf_op jit(solution)/shard_map/ppermute | solution.py:19
  141.5 0.3 fusion.8
  141.8 0.8 copy.52
  142.6 0.3 fusion.10
  142.9 0.8 copy.54
  143.7 0.3 fusion.9
  144.0 0.8 copy.53
  (46 shorter events, 0.7 us)
Async XLA Ops:
  0.6 89.6 %copy-start = (bf16[256,256]{1,0:T(8,128)(2,1)S(1)}, bf16[256,256]{1,0:T(8,128)(2,1)}, u32[]{:S(2)}) copy-start(bf16[256,256]{1,0:T(8,128)(2,1)} %param.5) | copy-start | bytes 393220
  0.6 0.8 collective-permute-start.6
  3.5 24.1 %copy-start.3 = (bf16[256,256]{1,0:T(8,128)(2,1)S(1)}, bf16[256,256]{1,0:T(8,128)(2,1)}, u32[]{:S(2)}) copy-start(bf16[256,256]{1,0:T(8,128)(2,1)} %param.8) | copy-start | bytes 393220
  3.5 33.6 %copy-start.2 = (bf16[256,256]{1,0:T(8,128)(2,1)S(1)}, bf16[256,256]{1,0:T(8,128)(2,1)}, u32[]{:S(2)}) copy-start(bf16[256,256]{1,0:T(8,128)(2,1)} %param.6) | copy-start | bytes 393220
  3.5 33.7 %copy-start.1 = (bf16[256,256]{1,0:T(8,128)(2,1)S(1)}, bf16[256,256]{1,0:T(8,128)(2,1)}, u32[]{:S(2)}) copy-start(bf16[256,256]{1,0:T(8,128)(2,1)} %param.7) | copy-start | bytes 393220
  3.5 49.4 %all-to-all-start = ((bf16[16,256,128]{2,1,0:T(8,128)(2,1)}), bf16[16,256,128]{2,1,0:T(8,128)(2,1)S(1)}, u32[]{:S(2)}, u32[]{:S(2)}) async-start(bf16[16,256,128]{2,1,0:T(8,128)(2,1)} %broadcast_in_dim.29), calls=%async_computation | async-start | bytes 2097152 | tf_op jit(solution)/shard_map/all_to_all | solution.py:73
  27.8 17.8 %collective-permute-start.8 = (bf16[256,256]{0,1:T(8,128)(2,1)S(1)}, bf16[256,256]{0,1:T(8,128)(2,1)S(1)}, u32[]{:S(2)}, u32[]{:S(2)}) collective-permute-start(bf16[256,256]{0,1:T(8,128)(2,1)S(1)} %copy.37), channel_id=1, source_target_pairs={{0,12},{4,0},{8,4},{12,8},{1,13},{5,1},{9,5},{13,9},{2,14},{6,2},{... | collective-permute-start | bytes 393224 | tf_op jit(solution)/shard_map/ppermute | solution.py:85
  32.1 13.4 %collective-permute-start.9 = (bf16[256,256]{0,1:T(8,128)(2,1)S(1)}, bf16[256,256]{0,1:T(8,128)(2,1)S(1)}, u32[]{:S(2)}, u32[]{:S(2)}) collective-permute-start(bf16[256,256]{0,1:T(8,128)(2,1)S(1)} %copy.37), channel_id=1, source_target_pairs={{0,8},{4,12},{8,0},{12,4},{1,9},{5,13},{9,1},{13,5},{2,10},{6,14},... | collective-permute-start | bytes 393224 | tf_op jit(solution)/shard_map/ppermute | solution.py:85
  34.6 21.7 %collective-permute-start.10 = (bf16[256,256]{0,1:T(8,128)(2,1)S(1)}, bf16[256,256]{0,1:T(8,128)(2,1)S(1)}, u32[]{:S(2)}, u32[]{:S(2)}) collective-permute-start(bf16[256,256]{0,1:T(8,128)(2,1)S(1)} %copy.37), channel_id=1, source_target_pairs={{0,4},{4,8},{8,12},{12,0},{1,5},{5,9},{9,13},{13,1},{2,6},{6,10},{... | collective-permute-start | bytes 393224 | tf_op jit(solution)/shard_map/ppermute | solution.py:85
  37.4 4.6 %collective-permute-start = (f32[2,128,128]{2,1,0:T(8,128)S(1)}, f32[2,128,128]{2,1,0:T(8,128)S(1)}, u32[]{:S(2)}, u32[]{:S(2)}) collective-permute-start(f32[2,128,128]{2,1,0:T(8,128)S(1)} %fusion.14), channel_id=1, source_target_pairs={{0,16},{16,0},{1,17},{17,1},{2,18},{18,2},{3,19},{19,3},{4,20},{20... | collective-permute-start | bytes 393224 | tf_op jit(solution)/shard_map/ppermute | solution.py:19
  42.0 14.4 %collective-permute-start.1 = (f32[128,128]{1,0:T(8,128)S(1)}, f32[128,128]{1,0:T(8,128)S(1)}, u32[]{:S(2)}, u32[]{:S(2)}) collective-permute-start(f32[128,128]{1,0:T(8,128)S(1)} %add_bitcast_fusion.1), channel_id=1, source_target_pairs={{0,32},{32,64},{64,96},{96,128},{128,160},{160,192},{192,224},{224... | collective-permute-start | bytes 196616 | tf_op jit(solution)/shard_map/ppermute | solution.py:42
  53.0 8.2 %collective-permute-start.7 = (bf16[16,256,128]{2,1,0:T(8,128)(2,1)S(1)}, bf16[16,256,128]{2,1,0:T(8,128)(2,1)S(1)}, u32[]{:S(2)}, u32[]{:S(2)}) collective-permute-start(bf16[16,256,128]{2,1,0:T(8,128)(2,1)S(1)} %all-to-all-done), channel_id=1, source_target_pairs={{0,16},{16,0},{1,17},{17,1},{2,18},{18,2},{3,19},{19,3},{4,20},{20... | collective-permute-start | bytes 3145736 | tf_op jit(solution)/shard_map/ppermute | solution.py:19
  56.5 10.7 %collective-permute-start.2 = (f32[128,128]{1,0:T(8,128)S(1)}, f32[128,128]{1,0:T(8,128)S(1)}, u32[]{:S(2)}, u32[]{:S(2)}) collective-permute-start(f32[128,128]{1,0:T(8,128)S(1)} %add.93), channel_id=1, source_target_pairs={{0,64},{32,96},{64,128},{96,160},{128,192},{160,224},{192,256},{22... | collective-permute-start | bytes 196616 | tf_op jit(solution)/shard_map/ppermute | solution.py:42
  63.0 35.6 %all-to-all-start.1 = ((f32[4,256,256]{1,2,0:T(8,128)}), f32[4,256,256]{1,2,0:T(8,128)S(1)}, u32[]{:S(2)}, u32[]{:S(2)}) async-start(f32[4,256,256]{1,2,0:T(8,128)} %fusion.2), calls=%async_computation.1 | async-start | bytes 2097152 | tf_op jit(solution)/shard_map/all_to_all | solution.py:98
  67.2 6.1 %collective-permute-start.3 = (f32[128,128]{1,0:T(8,128)S(1)}, f32[128,128]{1,0:T(8,128)S(1)}, u32[]{:S(2)}, u32[]{:S(2)}) collective-permute-start(f32[128,128]{1,0:T(8,128)S(1)} %add.95), channel_id=1, source_target_pairs={{0,128},{32,160},{64,192},{96,224},{128,256},{160,288},{192,320},{... | collective-permute-start | bytes 196616 | tf_op jit(solution)/shard_map/ppermute | solution.py:42
  73.4 21.6 %collective-permute-start.4 = (f32[128,128]{1,0:T(8,128)S(1)}, f32[128,128]{1,0:T(8,128)S(1)}, u32[]{:S(2)}, u32[]{:S(2)}) collective-permute-start(f32[128,128]{1,0:T(8,128)S(1)} %add.97), channel_id=1, source_target_pairs={{0,256},{32,288},{64,320},{96,352},{128,384},{160,416},{192,448},{... | collective-permute-start | bytes 196616 | tf_op jit(solution)/shard_map/ppermute | solution.py:42
  95.0 3.3 %collective-permute-start.5 = (f32[128,128]{1,0:T(8,128)S(1)}, f32[128,128]{1,0:T(8,128)S(1)}, u32[]{:S(2)}, u32[]{:S(2)}) collective-permute-start(f32[128,128]{1,0:T(8,128)S(1)} %add_add_fusion.1), channel_id=1, source_target_pairs={{0,16},{16,0},{1,17},{17,1},{2,18},{18,2},{3,19},{19,3},{4,20},{20... | collective-permute-start | bytes 196616 | tf_op jit(solution)/shard_map/ppermute | solution.py:19
  99.1 3.2 %collective-permute-start.11 = (f32[2,128,128]{2,1,0:T(8,128)S(1)}, f32[2,128,128]{2,1,0:T(8,128)S(1)}, u32[]{:S(2)}, u32[]{:S(2)}) collective-permute-start(f32[2,128,128]{2,1,0:T(8,128)S(1)} %convolution_bitcast_fusion.6), channel_id=1, source_target_pairs={{0,16},{16,0},{1,17},{17,1},{2,18},{18,2},{3,19},{19,3},{4,20},{20... | collective-permute-start | bytes 393224 | tf_op jit(solution)/shard_map/ppermute | solution.py:19
  102.4 5.0 %collective-permute-start.12 = (f32[128,128]{1,0:T(8,128)S(1)}, f32[128,128]{1,0:T(8,128)S(1)}, u32[]{:S(2)}, u32[]{:S(2)}) collective-permute-start(f32[128,128]{1,0:T(8,128)S(1)} %add_bitcast_fusion), channel_id=1, source_target_pairs={{32,0},{64,32},{96,64},{128,96},{160,128},{192,160},{224,192},{256... | collective-permute-start | bytes 196616 | tf_op jit(solution)/shard_map/ppermute | solution.py:42
  107.4 13.1 %collective-permute-start.13 = (f32[128,128]{1,0:T(8,128)S(1)}, f32[128,128]{1,0:T(8,128)S(1)}, u32[]{:S(2)}, u32[]{:S(2)}) collective-permute-start(f32[128,128]{1,0:T(8,128)S(1)} %add.108), channel_id=1, source_target_pairs={{64,0},{96,32},{128,64},{160,96},{192,128},{224,160},{256,192},{28... | collective-permute-start | bytes 196616 | tf_op jit(solution)/shard_map/ppermute | solution.py:42
  120.5 8.9 %collective-permute-start.14 = (f32[128,128]{1,0:T(8,128)S(1)}, f32[128,128]{1,0:T(8,128)S(1)}, u32[]{:S(2)}, u32[]{:S(2)}) collective-permute-start(f32[128,128]{1,0:T(8,128)S(1)} %add.110), channel_id=1, source_target_pairs={{128,0},{160,32},{192,64},{224,96},{256,128},{288,160},{320,192},{... | collective-permute-start | bytes 196616 | tf_op jit(solution)/shard_map/ppermute | solution.py:42
  129.5 5.0 %collective-permute-start.15 = (f32[128,128]{1,0:T(8,128)S(1)}, f32[128,128]{1,0:T(8,128)S(1)}, u32[]{:S(2)}, u32[]{:S(2)}) collective-permute-start(f32[128,128]{1,0:T(8,128)S(1)} %add.112), channel_id=1, source_target_pairs={{256,0},{288,32},{320,64},{352,96},{384,128},{416,160},{448,192},{... | collective-permute-start | bytes 196616 | tf_op jit(solution)/shard_map/ppermute | solution.py:42
  134.5 8.1 %collective-permute-start.16 = (f32[128,128]{1,0:T(8,128)S(1)}, f32[128,128]{1,0:T(8,128)S(1)}, u32[]{:S(2)}, u32[]{:S(2)}) collective-permute-start(f32[128,128]{1,0:T(8,128)S(1)} %add_add_fusion), channel_id=1, source_target_pairs={{0,16},{16,0},{1,17},{17,1},{2,18},{18,2},{3,19},{19,3},{4,20},{20... | collective-permute-start | bytes 196616 | tf_op jit(solution)/shard_map/ppermute | solution.py:19

commit v8 on v7

--- a/solution.py
+++ b/solution.py
@@ -19,7 +19,7 @@
     return lax.ppermute(value, "core", [(0, 1), (1, 0)])
 
 
-def ctx_scan(local_state, backward):
+def ctx_scan(local_state, backward, hold=None):
     core = lax.axis_index("core")
     other = swap_cores(local_state)
     first = jnp.where(core == 0, local_state, other)
@@ -43,11 +43,13 @@
         below = below + arrived
         if distance * 2 < chips:
             window = window + arrived
+        if hold is not None and distance == 2:
+            window, below, hold = lax.optimization_barrier((window, below, hold))
         distance *= 2
     other_half = swap_cores(below)
     head0 = jnp.where(core == 0, below, other_half)
     head1 = jnp.where(core == 0, other_half, below)
-    return jnp.stack([head0, head1]) + within
+    return jnp.stack([head0, head1]) + within, hold
 
 
 def place_rows(w_block):
@@ -78,7 +80,7 @@
     return jnp.stack([even, odd], axis=1)
 
 
-def output_gradient(grad_out, w_out):
+def output_gradient(grad_out, placed):
     x_size, y_groups = lax.axis_size("x"), lax.axis_size("yhi")
     here = lax.axis_index("x")
     shifted = [grad_out] + [
@@ -86,7 +88,7 @@
         for shift in range(1, x_size)
     ]
     rows = jnp.roll(jnp.stack(shifted), here, axis=0)
-    columns = gather_columns(place_rows(w_out))
+    columns = gather_columns(placed)
     columns = columns.reshape((x_size, y_groups) + columns.shape[1:])
     tok_rows = grad_out.shape[0]
     partial = jnp.einsum(
@@ -103,11 +105,10 @@
     tok_rows = query.shape[0]
     feat_width = query.shape[1]
     head_count = feat_width // E
-    grad_z = output_gradient(grad_out, w_out)
+    placed = place_rows(w_out)
     query_heads = query.reshape(tok_rows, head_count, E)
     key_heads = key_feat.reshape(tok_rows, head_count, E)
     value_heads = value.reshape(tok_rows, head_count, E)
-    gradz_heads = grad_z.reshape(tok_rows, head_count, E)
     query_wide = query_heads.astype(jnp.float32)
     key_wide = key_heads.astype(jnp.float32)
     value_wide = value_heads.astype(jnp.float32)
@@ -120,7 +121,9 @@
     local_state = jnp.einsum(
         "shd,she->hde", key_heads, value_heads, preferred_element_type=jnp.float32
     )
-    state_in = ctx_scan(local_state, False)
+    state_in, placed = ctx_scan(local_state, False, placed)
+    grad_z = output_gradient(grad_out, placed)
+    gradz_heads = grad_z.reshape(tok_rows, head_count, E)
     attended = jnp.einsum("hts,she->the", weights, value_wide, precision=highest)
     attended = attended + jnp.einsum("thd,hde->the", query_wide, state_in, precision=highest)
     inv_rms = lax.rsqrt(jnp.mean(attended * attended, axis=-1, keepdims=True) + epsilon)
@@ -139,7 +142,7 @@
     local_adjoint = jnp.einsum(
         "thd,the->hde", query_heads, grad_att, preferred_element_type=jnp.float32
     )
-    adjoint = ctx_scan(local_adjoint, True)
+    adjoint, _ = ctx_scan(local_adjoint, True)
     grad_key = jnp.einsum("hts,thd->shd", grad_weights, query_wide, precision=highest)
     grad_key = grad_key + jnp.einsum("she,hde->shd", value_wide, adjoint, precision=highest)
     grad_value = jnp.einsum("hts,the->she", weights, grad_wide, precision=highest)

time: 145 us -> 155 us (1.069)
  the two profiles are of different devices: /device:TPU:1 before, /device:TPU:21 now
where the time goes in v8:
time: 155 us; the launch traced here: 154 us
  starting transfers between devices  95.1 us (61%)
  waiting for transfers between devices  39.7 us (26%)
  local copies, waits for them, and re-layouts  11.1 us (7%)
  matrix products  6.28 us (4%)
    ppermute x8, starting transfers between devices, ctx_scan(): arrived = lax.ppermute(window, CHIPS, pairs)  46.4 us
    ppermute x8, waiting for transfers between devices, ctx_scan(): arrived = lax.ppermute(window, CHIPS, pairs)  22.6 us
    ppermute x5, starting transfers between devices, swap_cores(): return lax.ppermute(value, 'core', [(0, 1), (1, 0)])  19.1 us
    all_to_all x1, waiting for transfers between devices, gather_columns(): mine = lax.all_to_all(spread, CHIPS, 0, 0, tiled=True)  14.7 us
    all_to_all x1, starting transfers between devices, gather_columns(): mine = lax.all_to_all(spread, CHIPS, 0, 0, tiled=True)  12.2 us
    ppermute x3, starting transfers between devices, output_gradient(): lax.ppermute(grad_out, 'x', [(i, (i - shift) % x_size) for i in range(x_s...  8.44 us
    unnamed x21, local copies, waits for them, and re-layouts  7.07 us
    all_to_all x1, starting transfers between devices, output_gradient(): parts = lax.all_to_all(partial, 'yhi', 0, 0, tiled=True)  5.11 us
  transfers between devices with their start and end apart: 19, of which 11 were waited for; matrix products, arithmetic and copies ran while one was open for 7% of the time, Pallas kernels for 0%

profile of v8, /device:TPU:21, one launch (start us, length us, event | category | flops | bytes accessed | tf_op | source)
XLA Modules:
  0.0 153.8 jit_solution(11705100389836589422)
XLA Ops:
  0.7 1.1 copy.114
  1.7 1.1 fusion.14
  2.8 2.6 %collective-permute-start = (f32[2,128,128]{2,1,0:T(8,128)S(1)}, f32[2,128,128]{2,1,0:T(8,128)S(1)}, u32[]{:S(2)}, u32[]{:S(2)}) collective-permute-start(f32[2,128,128]{2,1,0:T(8,128)S(1)} %fusion.14), channel_id=1, source_target_pairs={{0,16},{16,0},{1,17},{17,1},{2,18},{18,2},{3,19},{19,3},{4,20},{20... | collective-permute-start | bytes 393224 | tf_op jit(solution)/shard_map/ppermute | solution.py:19
  5.4 1.0 collective-permute-done
  6.4 4.0 %collective-permute-start.1 = (f32[128,128]{1,0:T(8,128)S(1)}, f32[128,128]{1,0:T(8,128)S(1)}, u32[]{:S(2)}, u32[]{:S(2)}) collective-permute-start(f32[128,128]{1,0:T(8,128)S(1)} %add_bitcast_fusion.1), channel_id=1, source_target_pairs={{0,32},{32,64},{64,96},{96,128},{128,160},{160,192},{192,224},{224... | collective-permute-start | bytes 196616 | tf_op jit(solution)/shard_map/ppermute | solution.py:42
  10.4 3.8 %collective-permute-start.3 = (bf16[256,128]{1,0:T(8,128)(2,1)}, bf16[256,128]{1,0:T(8,128)(2,1)S(1)}, u32[]{:S(2)}, u32[]{:S(2)}) collective-permute-start(bf16[256,128]{1,0:T(8,128)(2,1)} %param.9), channel_id=1, source_target_pairs={{1,32},{2,64},{3,96},{17,48},{18,80},{19,112},{32,1},{34,65},{35,9... | collective-permute-start | bytes 196616 | tf_op jit(solution)/shard_map/ppermute | solution.py:67
  14.2 6.6 %collective-permute-start.2 = (f32[128,128]{1,0:T(8,128)S(1)}, f32[128,128]{1,0:T(8,128)S(1)}, u32[]{:S(2)}, u32[]{:S(2)}) collective-permute-start(f32[128,128]{1,0:T(8,128)S(1)} %add.93), channel_id=1, source_target_pairs={{0,64},{32,96},{64,128},{96,160},{128,192},{160,224},{192,256},{22... | collective-permute-start | bytes 196616 | tf_op jit(solution)/shard_map/ppermute | solution.py:42
  20.8 1.3 collective-permute-done.2
  22.1 1.2 broadcast_in_dim.29
  23.3 12.2 %all-to-all-start = ((bf16[16,256,128]{2,1,0:T(8,128)(2,1)}), bf16[16,256,128]{2,1,0:T(8,128)(2,1)S(1)}, u32[]{:S(2)}, u32[]{:S(2)}) async-start(bf16[16,256,128]{2,1,0:T(8,128)(2,1)} %broadcast_in_dim.29), calls=%async_computation | async-start | bytes 2097152 | tf_op jit(solution)/shard_map/all_to_all | solution.py:75
  35.6 2.2 %collective-permute-start.8 = (bf16[256,256]{0,1:T(8,128)(2,1)S(1)}, bf16[256,256]{0,1:T(8,128)(2,1)S(1)}, u32[]{:S(2)}, u32[]{:S(2)}) collective-permute-start(bf16[256,256]{0,1:T(8,128)(2,1)S(1)} %copy.37), channel_id=1, source_target_pairs={{0,12},{4,0},{8,4},{12,8},{1,13},{5,1},{9,5},{13,9},{2,14},{6,2},{... | collective-permute-start | bytes 393224 | tf_op jit(solution)/shard_map/ppermute | solution.py:87
  37.8 4.4 %collective-permute-start.9 = (bf16[256,256]{0,1:T(8,128)(2,1)S(1)}, bf16[256,256]{0,1:T(8,128)(2,1)S(1)}, u32[]{:S(2)}, u32[]{:S(2)}) collective-permute-start(bf16[256,256]{0,1:T(8,128)(2,1)S(1)} %copy.37), channel_id=1, source_target_pairs={{0,8},{4,12},{8,0},{12,4},{1,9},{5,13},{9,1},{13,5},{2,10},{6,14},... | collective-permute-start | bytes 393224 | tf_op jit(solution)/shard_map/ppermute | solution.py:87
  42.2 1.9 %collective-permute-start.10 = (bf16[256,256]{0,1:T(8,128)(2,1)S(1)}, bf16[256,256]{0,1:T(8,128)(2,1)S(1)}, u32[]{:S(2)}, u32[]{:S(2)}) collective-permute-start(bf16[256,256]{0,1:T(8,128)(2,1)S(1)} %copy.37), channel_id=1, source_target_pairs={{0,4},{4,8},{8,12},{12,0},{1,5},{5,9},{9,13},{13,1},{2,6},{6,10},{... | collective-permute-start | bytes 393224 | tf_op jit(solution)/shard_map/ppermute | solution.py:87
  44.1 0.7 bitcast_dynamic-update-slice_fusion.6
  44.8 0.7 bitcast_dynamic-update-slice_fusion.4
  45.5 0.7 bitcast_dynamic-update-slice_fusion.2
  46.1 14.7 %all-to-all-done = bf16[16,256,128]{2,1,0:T(8,128)(2,1)S(1)} async-done(((bf16[16,256,128]{2,1,0:T(8,128)(2,1)}), bf16[16,256,128]{2,1,0:T(8,128)(2,1)S(1)}, u32[]{:S(2)}, u32[]{:S(2)}) %all-to-all-start) | async-done | bytes 1048608 | tf_op jit(solution)/shard_map/all_to_all | solution.py:75
  60.9 3.3 %collective-permute-start.7 = (bf16[16,256,128]{2,1,0:T(8,128)(2,1)S(1)}, bf16[16,256,128]{2,1,0:T(8,128)(2,1)S(1)}, u32[]{:S(2)}, u32[]{:S(2)}) collective-permute-start(bf16[16,256,128]{2,1,0:T(8,128)(2,1)S(1)} %all-to-all-done), channel_id=1, source_target_pairs={{0,16},{16,0},{1,17},{17,1},{2,18},{18,2},{3,19},{19,3},{4,20},{20... | collective-permute-start | bytes 3145736 | tf_op jit(solution)/shard_map/ppermute | solution.py:19
  64.2 0.7 bitcast_dynamic-update-slice_fusion
  64.8 0.7 bitcast_dynamic-update-slice_fusion.7
  65.5 0.7 bitcast_dynamic-update-slice_fusion.5
  66.2 0.7 bitcast_dynamic-update-slice_fusion.3
  66.8 0.7 bitcast_dynamic-update-slice_fusion.1
  67.5 1.1 constant_dynamic-slice_fusion
  68.7 1.7 %fusion.2 = f32[4,256,256]{1,2,0:T(8,128)} fusion(bf16[4,256,2,128,1]{1,3,2,4,0:T(8,128)(2,1)S(1)} %bitcast.143, bf16[4,4,1,256,128]{4,3,1,0,2:T(8,128)(2,1)S(1)} %bitcast.142, bf16[4,4,1,256,128]{4,3,1,0,2:T(8,128)(2,1)S(1)} %bitcast.141), kind=kOutput, calls=%fused_computation.3 | convolution fusion | flops 537919488 | bytes 3670016 | tf_op jit(solution)/shard_map/atrk,abrjk->btj/dot_general | solution.py:94
  70.4 5.1 %all-to-all-start.1 = ((f32[4,256,256]{1,2,0:T(8,128)}), f32[4,256,256]{1,2,0:T(8,128)S(1)}, u32[]{:S(2)}, u32[]{:S(2)}) async-start(f32[4,256,256]{1,2,0:T(8,128)} %fusion.2), calls=%async_computation.1 | async-start | bytes 2097152 | tf_op jit(solution)/shard_map/all_to_all | solution.py:100
  75.6 5.8 %collective-permute-start.4 = (f32[128,128]{1,0:T(8,128)S(1)}, f32[128,128]{1,0:T(8,128)S(1)}, u32[]{:S(2)}, u32[]{:S(2)}) collective-permute-start(f32[128,128]{1,0:T(8,128)S(1)} %get-tuple-element.7), channel_id=1, source_target_pairs={{0,128},{32,160},{64,192},{96,224},{128,256},{160,288},{192,320},{... | collective-permute-start | bytes 196616 | tf_op jit(solution)/shard_map/ppermute | solution.py:42
  81.4 1.3 collective-permute-done.4
  82.7 24.9 %collective-permute-start.5 = (f32[128,128]{1,0:T(8,128)S(1)}, f32[128,128]{1,0:T(8,128)S(1)}, u32[]{:S(2)}, u32[]{:S(2)}) collective-permute-start(f32[128,128]{1,0:T(8,128)S(1)} %add.98), channel_id=1, source_target_pairs={{0,256},{32,288},{64,320},{96,352},{128,384},{160,416},{192,448},{... | collective-permute-start | bytes 196616 | tf_op jit(solution)/shard_map/ppermute | solution.py:42
  107.9 1.1 collective-permute-done.5
  108.9 3.9 %collective-permute-start.6 = (f32[128,128]{1,0:T(8,128)S(1)}, f32[128,128]{1,0:T(8,128)S(1)}, u32[]{:S(2)}, u32[]{:S(2)}) collective-permute-start(f32[128,128]{1,0:T(8,128)S(1)} %add_add_fusion.1), channel_id=1, source_target_pairs={{0,16},{16,0},{1,17},{17,1},{2,18},{18,2},{3,19},{19,3},{4,20},{20... | collective-permute-start | bytes 196616 | tf_op jit(solution)/shard_map/ppermute | solution.py:19
  112.8 0.4 convolution_bitcast_fusion.2
  113.3 0.4 collective-permute-done.6
  114.5 2.3 %collective-permute-start.11 = (f32[2,128,128]{2,1,0:T(8,128)S(1)}, f32[2,128,128]{2,1,0:T(8,128)S(1)}, u32[]{:S(2)}, u32[]{:S(2)}) collective-permute-start(f32[2,128,128]{2,1,0:T(8,128)S(1)} %convolution_bitcast_fusion.6), channel_id=1, source_target_pairs={{0,16},{16,0},{1,17},{17,1},{2,18},{18,2},{3,19},{19,3},{4,20},{20... | collective-permute-start | bytes 393224 | tf_op jit(solution)/shard_map/ppermute | solution.py:19
  116.8 1.0 collective-permute-done.11
  117.8 1.3 collective-permute-start.12
  119.4 3.3 %collective-permute-done.12 = f32[128,128]{1,0:T(8,128)S(1)} collective-permute-done((f32[128,128]{1,0:T(8,128)S(1)}, f32[128,128]{1,0:T(8,128)S(1)}, u32[]{:S(2)}, u32[]{:S(2)}) %collective-permute-start.12) | collective-permute-done | bytes 65568 | tf_op jit(solution)/shard_map/ppermute | solution.py:42
  122.8 1.3 collective-permute-start.13
  124.4 5.0 %collective-permute-done.13 = f32[128,128]{1,0:T(8,128)S(1)} collective-permute-done((f32[128,128]{1,0:T(8,128)S(1)}, f32[128,128]{1,0:T(8,128)S(1)}, u32[]{:S(2)}, u32[]{:S(2)}) %collective-permute-start.13) | collective-permute-done | bytes 65568 | tf_op jit(solution)/shard_map/ppermute | solution.py:42
  129.4 1.3 collective-permute-start.14
  131.1 7.4 %collective-permute-done.14 = f32[128,128]{1,0:T(8,128)S(1)} collective-permute-done((f32[128,128]{1,0:T(8,128)S(1)}, f32[128,128]{1,0:T(8,128)S(1)}, u32[]{:S(2)}, u32[]{:S(2)}) %collective-permute-start.14) | collective-permute-done | bytes 65568 | tf_op jit(solution)/shard_map/ppermute | solution.py:42
  138.4 1.3 collective-permute-start.15
  139.7 0.4 convolution_bitcast_fusion.1
  140.2 3.3 %collective-permute-done.15 = f32[128,128]{1,0:T(8,128)S(1)} collective-permute-done((f32[128,128]{1,0:T(8,128)S(1)}, f32[128,128]{1,0:T(8,128)S(1)}, u32[]{:S(2)}, u32[]{:S(2)}) %collective-permute-start.15) | collective-permute-done | bytes 65568 | tf_op jit(solution)/shard_map/ppermute | solution.py:42
  143.5 7.1 %collective-permute-start.16 = (f32[128,128]{1,0:T(8,128)S(1)}, f32[128,128]{1,0:T(8,128)S(1)}, u32[]{:S(2)}, u32[]{:S(2)}) collective-permute-start(f32[128,128]{1,0:T(8,128)S(1)} %add_add_fusion), channel_id=1, source_target_pairs={{0,16},{16,0},{1,17},{17,1},{2,18},{18,2},{3,19},{19,3},{4,20},{20... | collective-permute-start | bytes 196616 | tf_op jit(solution)/shard_map/ppermute | solution.py:19
  150.9 0.8 copy.52
  152.0 0.8 copy.54
  153.0 0.8 copy.53
  (48 shorter events, 3.3 us)
Async XLA Ops:
  0.6 107.0 %copy-start = (bf16[256,256]{1,0:T(8,128)(2,1)S(1)}, bf16[256,256]{1,0:T(8,128)(2,1)}, u32[]{:S(2)}) copy-start(bf16[256,256]{1,0:T(8,128)(2,1)} %param.5) | copy-start | bytes 393220
  0.6 20.1 %copy-start.4 = (bf16[256,128]{1,0:T(8,128)(2,1)S(1)}, bf16[256,128]{1,0:T(8,128)(2,1)}, u32[]{:S(2)}) copy-start(bf16[256,128]{1,0:T(8,128)(2,1)} %param.9) | copy-start | bytes 196612
  2.8 3.6 %collective-permute-start = (f32[2,128,128]{2,1,0:T(8,128)S(1)}, f32[2,128,128]{2,1,0:T(8,128)S(1)}, u32[]{:S(2)}, u32[]{:S(2)}) collective-permute-start(f32[2,128,128]{2,1,0:T(8,128)S(1)} %fusion.14), channel_id=1, source_target_pairs={{0,16},{16,0},{1,17},{17,1},{2,18},{18,2},{3,19},{19,3},{4,20},{20... | collective-permute-start | bytes 393224 | tf_op jit(solution)/shard_map/ppermute | solution.py:19
  6.4 7.8 %collective-permute-start.1 = (f32[128,128]{1,0:T(8,128)S(1)}, f32[128,128]{1,0:T(8,128)S(1)}, u32[]{:S(2)}, u32[]{:S(2)}) collective-permute-start(f32[128,128]{1,0:T(8,128)S(1)} %add_bitcast_fusion.1), channel_id=1, source_target_pairs={{0,32},{32,64},{64,96},{96,128},{128,160},{160,192},{192,224},{224... | collective-permute-start | bytes 196616 | tf_op jit(solution)/shard_map/ppermute | solution.py:42
  10.4 10.4 %collective-permute-start.3 = (bf16[256,128]{1,0:T(8,128)(2,1)}, bf16[256,128]{1,0:T(8,128)(2,1)S(1)}, u32[]{:S(2)}, u32[]{:S(2)}) collective-permute-start(bf16[256,128]{1,0:T(8,128)(2,1)} %param.9), channel_id=1, source_target_pairs={{1,32},{2,64},{3,96},{17,48},{18,80},{19,112},{32,1},{34,65},{35,9... | collective-permute-start | bytes 196616 | tf_op jit(solution)/shard_map/ppermute | solution.py:67
  14.2 7.9 %collective-permute-start.2 = (f32[128,128]{1,0:T(8,128)S(1)}, f32[128,128]{1,0:T(8,128)S(1)}, u32[]{:S(2)}, u32[]{:S(2)}) collective-permute-start(f32[128,128]{1,0:T(8,128)S(1)} %add.93), channel_id=1, source_target_pairs={{0,64},{32,96},{64,128},{96,160},{128,192},{160,224},{192,256},{22... | collective-permute-start | bytes 196616 | tf_op jit(solution)/shard_map/ppermute | solution.py:42
  23.3 12.2 %copy-start.3 = (bf16[256,256]{1,0:T(8,128)(2,1)S(1)}, bf16[256,256]{1,0:T(8,128)(2,1)}, u32[]{:S(2)}) copy-start(bf16[256,256]{1,0:T(8,128)(2,1)} %param.8) | copy-start | bytes 393220
  23.3 37.5 %all-to-all-start = ((bf16[16,256,128]{2,1,0:T(8,128)(2,1)}), bf16[16,256,128]{2,1,0:T(8,128)(2,1)S(1)}, u32[]{:S(2)}, u32[]{:S(2)}) async-start(bf16[16,256,128]{2,1,0:T(8,128)(2,1)} %broadcast_in_dim.29), calls=%async_computation | async-start | bytes 2097152 | tf_op jit(solution)/shard_map/all_to_all | solution.py:75
  35.6 9.2 %collective-permute-start.8 = (bf16[256,256]{0,1:T(8,128)(2,1)S(1)}, bf16[256,256]{0,1:T(8,128)(2,1)S(1)}, u32[]{:S(2)}, u32[]{:S(2)}) collective-permute-start(bf16[256,256]{0,1:T(8,128)(2,1)S(1)} %copy.37), channel_id=1, source_target_pairs={{0,12},{4,0},{8,4},{12,8},{1,13},{5,1},{9,5},{13,9},{2,14},{6,2},{... | collective-permute-start | bytes 393224 | tf_op jit(solution)/shard_map/ppermute | solution.py:87
  37.8 7.7 %collective-permute-start.9 = (bf16[256,256]{0,1:T(8,128)(2,1)S(1)}, bf16[256,256]{0,1:T(8,128)(2,1)S(1)}, u32[]{:S(2)}, u32[]{:S(2)}) collective-permute-start(bf16[256,256]{0,1:T(8,128)(2,1)S(1)} %copy.37), channel_id=1, source_target_pairs={{0,8},{4,12},{8,0},{12,4},{1,9},{5,13},{9,1},{13,5},{2,10},{6,14},... | collective-permute-start | bytes 393224 | tf_op jit(solution)/shard_map/ppermute | solution.py:87
  42.2 22.0 %collective-permute-start.10 = (bf16[256,256]{0,1:T(8,128)(2,1)S(1)}, bf16[256,256]{0,1:T(8,128)(2,1)S(1)}, u32[]{:S(2)}, u32[]{:S(2)}) collective-permute-start(bf16[256,256]{0,1:T(8,128)(2,1)S(1)} %copy.37), channel_id=1, source_target_pairs={{0,4},{4,8},{8,12},{12,0},{1,5},{5,9},{9,13},{13,1},{2,6},{6,10},{... | collective-permute-start | bytes 393224 | tf_op jit(solution)/shard_map/ppermute | solution.py:87
  60.9 7.7 %collective-permute-start.7 = (bf16[16,256,128]{2,1,0:T(8,128)(2,1)S(1)}, bf16[16,256,128]{2,1,0:T(8,128)(2,1)S(1)}, u32[]{:S(2)}, u32[]{:S(2)}) collective-permute-start(bf16[16,256,128]{2,1,0:T(8,128)(2,1)S(1)} %all-to-all-done), channel_id=1, source_target_pairs={{0,16},{16,0},{1,17},{17,1},{2,18},{18,2},{3,19},{19,3},{4,20},{20... | collective-permute-start | bytes 3145736 | tf_op jit(solution)/shard_map/ppermute | solution.py:19
  70.4 37.2 %copy-start.2 = (bf16[256,256]{1,0:T(8,128)(2,1)S(1)}, bf16[256,256]{1,0:T(8,128)(2,1)}, u32[]{:S(2)}) copy-start(bf16[256,256]{1,0:T(8,128)(2,1)} %param.6) | copy-start | bytes 393220
  70.4 43.6 %all-to-all-start.1 = ((f32[4,256,256]{1,2,0:T(8,128)}), f32[4,256,256]{1,2,0:T(8,128)S(1)}, u32[]{:S(2)}, u32[]{:S(2)}) async-start(f32[4,256,256]{1,2,0:T(8,128)} %fusion.2), calls=%async_computation.1 | async-start | bytes 2097152 | tf_op jit(solution)/shard_map/all_to_all | solution.py:100
  75.6 37.3 %copy-start.1 = (bf16[256,256]{1,0:T(8,128)(2,1)S(1)}, bf16[256,256]{1,0:T(8,128)(2,1)}, u32[]{:S(2)}) copy-start(bf16[256,256]{1,0:T(8,128)(2,1)} %param.7) | copy-start | bytes 393220
  75.6 7.2 %collective-permute-start.4 = (f32[128,128]{1,0:T(8,128)S(1)}, f32[128,128]{1,0:T(8,128)S(1)}, u32[]{:S(2)}, u32[]{:S(2)}) collective-permute-start(f32[128,128]{1,0:T(8,128)S(1)} %get-tuple-element.7), channel_id=1, source_target_pairs={{0,128},{32,160},{64,192},{96,224},{128,256},{160,288},{192,320},{... | collective-permute-start | bytes 196616 | tf_op jit(solution)/shard_map/ppermute | solution.py:42
  82.7 26.2 %collective-permute-start.5 = (f32[128,128]{1,0:T(8,128)S(1)}, f32[128,128]{1,0:T(8,128)S(1)}, u32[]{:S(2)}, u32[]{:S(2)}) collective-permute-start(f32[128,128]{1,0:T(8,128)S(1)} %add.98), channel_id=1, source_target_pairs={{0,256},{32,288},{64,320},{96,352},{128,384},{160,416},{192,448},{... | collective-permute-start | bytes 196616 | tf_op jit(solution)/shard_map/ppermute | solution.py:42
  108.9 4.8 %collective-permute-start.6 = (f32[128,128]{1,0:T(8,128)S(1)}, f32[128,128]{1,0:T(8,128)S(1)}, u32[]{:S(2)}, u32[]{:S(2)}) collective-permute-start(f32[128,128]{1,0:T(8,128)S(1)} %add_add_fusion.1), channel_id=1, source_target_pairs={{0,16},{16,0},{1,17},{17,1},{2,18},{18,2},{3,19},{19,3},{4,20},{20... | collective-permute-start | bytes 196616 | tf_op jit(solution)/shard_map/ppermute | solution.py:19
  114.5 3.2 %collective-permute-start.11 = (f32[2,128,128]{2,1,0:T(8,128)S(1)}, f32[2,128,128]{2,1,0:T(8,128)S(1)}, u32[]{:S(2)}, u32[]{:S(2)}) collective-permute-start(f32[2,128,128]{2,1,0:T(8,128)S(1)} %convolution_bitcast_fusion.6), channel_id=1, source_target_pairs={{0,16},{16,0},{1,17},{17,1},{2,18},{18,2},{3,19},{19,3},{4,20},{20... | collective-permute-start | bytes 393224 | tf_op jit(solution)/shard_map/ppermute | solution.py:19
  117.8 5.0 %collective-permute-start.12 = (f32[128,128]{1,0:T(8,128)S(1)}, f32[128,128]{1,0:T(8,128)S(1)}, u32[]{:S(2)}, u32[]{:S(2)}) collective-permute-start(f32[128,128]{1,0:T(8,128)S(1)} %add_bitcast_fusion), channel_id=1, source_target_pairs={{32,0},{64,32},{96,64},{128,96},{160,128},{192,160},{224,192},{256... | collective-permute-start | bytes 196616 | tf_op jit(solution)/shard_map/ppermute | solution.py:42
  122.8 6.6 %collective-permute-start.13 = (f32[128,128]{1,0:T(8,128)S(1)}, f32[128,128]{1,0:T(8,128)S(1)}, u32[]{:S(2)}, u32[]{:S(2)}) collective-permute-start(f32[128,128]{1,0:T(8,128)S(1)} %add.108), channel_id=1, source_target_pairs={{64,0},{96,32},{128,64},{160,96},{192,128},{224,160},{256,192},{28... | collective-permute-start | bytes 196616 | tf_op jit(solution)/shard_map/ppermute | solution.py:42
  129.4 9.0 %collective-permute-start.14 = (f32[128,128]{1,0:T(8,128)S(1)}, f32[128,128]{1,0:T(8,128)S(1)}, u32[]{:S(2)}, u32[]{:S(2)}) collective-permute-start(f32[128,128]{1,0:T(8,128)S(1)} %add.110), channel_id=1, source_target_pairs={{128,0},{160,32},{192,64},{224,96},{256,128},{288,160},{320,192},{... | collective-permute-start | bytes 196616 | tf_op jit(solution)/shard_map/ppermute | solution.py:42
  138.4 5.0 %collective-permute-start.15 = (f32[128,128]{1,0:T(8,128)S(1)}, f32[128,128]{1,0:T(8,128)S(1)}, u32[]{:S(2)}, u32[]{:S(2)}) collective-permute-start(f32[128,128]{1,0:T(8,128)S(1)} %add.112), channel_id=1, source_target_pairs={{256,0},{288,32},{320,64},{352,96},{384,128},{416,160},{448,192},{... | collective-permute-start | bytes 196616 | tf_op jit(solution)/shard_map/ppermute | solution.py:42
  143.5 8.2 %collective-permute-start.16 = (f32[128,128]{1,0:T(8,128)S(1)}, f32[128,128]{1,0:T(8,128)S(1)}, u32[]{:S(2)}, u32[]{:S(2)}) collective-permute-start(f32[128,128]{1,0:T(8,128)S(1)} %add_add_fusion), channel_id=1, source_target_pairs={{0,16},{16,0},{1,17},{17,1},{2,18},{18,2},{3,19},{19,3},{4,20},{20... | collective-permute-start | bytes 196616 | tf_op jit(solution)/shard_map/ppermute | solution.py:19

commit v9 on v4

--- a/solution.py
+++ b/solution.py
@@ -19,7 +19,7 @@
     return lax.ppermute(value, "core", [(0, 1), (1, 0)])
 
 
-def ctx_scan(local_state, backward):
+def ctx_scan(local_state, backward, hold=None):
     core = lax.axis_index("core")
     chips = lax.axis_size("ylo") * lax.axis_size("z")
     step = -1 if backward else 1
@@ -45,11 +45,13 @@
         below = below + arrived
         if distance * 2 < chips:
             window = window + arrived
+        if hold is not None and distance == 4:
+            window, below, hold = lax.optimization_barrier((window, below, hold))
         distance *= 2
     other_half = swap_cores(below)
     head0 = jnp.where(core == 0, below, other_half)
     head1 = jnp.where(core == 0, other_half, below)
-    return jnp.stack([head0, head1]) + within
+    return jnp.stack([head0, head1]) + within, hold
 
 
 def gather_columns(w_block):
@@ -68,7 +70,13 @@
     feat_width = query.shape[1]
     head_count = feat_width // E
     full_rows = lax.all_gather(grad_out, TP, axis=1, tiled=True)
-    columns = gather_columns(w_out)
+    key_heads = key_feat.reshape(tok_rows, head_count, E)
+    value_heads = value.reshape(tok_rows, head_count, E)
+    local_state = jnp.einsum(
+        "shd,she->hde", key_heads, value_heads, preferred_element_type=jnp.float32
+    )
+    state_in, w_held = ctx_scan(local_state, False, w_out)
+    columns = gather_columns(w_held)
     grad_z = jnp.einsum(
         "tqrk,qrjk->tj",
         full_rows.reshape(tok_rows, columns.shape[0], 2, columns.shape[3]),
@@ -88,10 +96,6 @@
     )[None]
     scores = jnp.einsum("thd,shd->hts", query_heads, key_heads, preferred_element_type=jnp.float32)
     weights = jnp.where(causal, scores, 0.0)
-    local_state = jnp.einsum(
-        "shd,she->hde", key_heads, value_heads, preferred_element_type=jnp.float32
-    )
-    state_in = ctx_scan(local_state, False)
     attended = jnp.einsum("hts,she->the", weights, value_wide, precision=highest)
     attended = attended + jnp.einsum("thd,hde->the", query_wide, state_in, precision=highest)
     inv_rms = lax.rsqrt(jnp.mean(attended * attended, axis=-1, keepdims=True) + epsilon)
@@ -110,7 +114,7 @@
     local_adjoint = jnp.einsum(
         "thd,the->hde", query_heads, grad_att, preferred_element_type=jnp.float32
     )
-    adjoint = ctx_scan(local_adjoint, True)
+    adjoint, _ = ctx_scan(local_adjoint, True)
     grad_key = jnp.einsum("hts,thd->shd", grad_weights, query_wide, precision=highest)
     grad_key = grad_key + jnp.einsum("she,hde->shd", value_wide, adjoint, precision=highest)
     grad_value = jnp.einsum("hts,the->she", weights, grad_wide, precision=highest)

time: 140 us -> 147 us (1.050)
  the two profiles are of different devices: /device:TPU:51 before, /device:TPU:1 now
where the time goes in v9:
time: 147 us; the launch traced here: 146 us
  starting transfers between devices  63.3 us (43%)
  waiting for transfers between devices  50.5 us (34%)
  between operations  14.5 us (10%)
  matrix products  9.2 us (6%)
  local copies, waits for them, and re-layouts  6.26 us (4%)
  other arithmetic  2.37 us (2%)
    ppermute x6, starting transfers between devices, ctx_scan(): arrived = lax.ppermute(window, CHIPS, pairs)  25.7 us
    ppermute x5, starting transfers between devices, swap_cores(): return lax.ppermute(value, 'core', [(0, 1), (1, 0)])  24.4 us
    all_to_all x1, waiting for transfers between devices, gather_columns(): mine = lax.all_to_all(spread, CHIPS, 0, 0, tiled=True)  22.2 us
    ppermute x6, waiting for transfers between devices, ctx_scan(): arrived = lax.ppermute(window, CHIPS, pairs)  20.6 us
    all_to_all x1, starting transfers between devices, gather_columns(): mine = lax.all_to_all(spread, CHIPS, 0, 0, tiled=True)  7.77 us
    unnamed x24, local copies, waits for them, and re-layouts  4 us
    ppermute x2, waiting for transfers between devices, ctx_scan(): lax.ppermute(cross_head, CTX, [(2 * q + c, 2 * t + 1 - c) for q, t in nea...  3.58 us
    all_gather x1, waiting for transfers between devices, local(): full_rows = lax.all_gather(grad_out, TP, axis=1, tiled=True)  3.27 us
  transfers between devices with their start and end apart: 17, of which 10 were waited for; matrix products, arithmetic and copies ran while one was open for 7% of the time, Pallas kernels for 0%

profile of v9, /device:TPU:1, one launch (start us, length us, event | category | flops | bytes accessed | tf_op | source)
XLA Modules:
  0.0 146.1 jit_solution(13364295548245145898)
XLA Ops:
  7.2 1.0 copy.106
  8.3 1.1 fusion.13
  9.4 8.7 %collective-permute-start = (f32[2,128,128]{2,1,0:T(8,128)S(1)}, f32[2,128,128]{2,1,0:T(8,128)S(1)}, u32[]{:S(2)}, u32[]{:S(2)}) collective-permute-start(f32[2,128,128]{2,1,0:T(8,128)S(1)} %fusion.13), channel_id=1, source_target_pairs={{0,16},{16,0},{1,17},{17,1},{2,18},{18,2},{3,19},{19,3},{4,20},{20... | collective-permute-start | bytes 393224 | tf_op jit(solution)/shard_map/ppermute | solution.py:19
  18.1 1.3 collective-permute-start.1
  19.4 1.5 %collective-permute-start.2 = (f32[128,128]{1,0:T(8,128)S(1)}, f32[128,128]{1,0:T(8,128)S(1)}, u32[]{:S(2)}, u32[]{:S(2)}) collective-permute-start(f32[128,128]{1,0:T(8,128)S(1)} %get-tuple-element.27), channel_id=1, source_target_pairs={{0,48},{16,32},{32,80},{48,64},{64,112},{80,96},{96,144},{112,128}... | collective-permute-start | bytes 196616 | tf_op jit(solution)/shard_map/ppermute | solution.py:31
  21.0 1.7 %copy.39 = bf16[256,256]{0,1:T(8,128)(2,1)} copy(bf16[256,256]{1,0:T(8,128)(2,1)} %param.8) | data formatting | bytes 262144 | tf_op args[3]
  22.8 7.0 %collective-permute-start.3 = (f32[128,128]{1,0:T(8,128)S(1)}, f32[128,128]{1,0:T(8,128)S(1)}, u32[]{:S(2)}, u32[]{:S(2)}) collective-permute-start(f32[128,128]{1,0:T(8,128)S(1)} %get-tuple-element.17), channel_id=1, source_target_pairs={{0,64},{32,96},{64,128},{96,160},{128,192},{160,224},{192,256},{22... | collective-permute-start | bytes 196616 | tf_op jit(solution)/shard_map/ppermute | solution.py:44
  29.8 1.3 collective-permute-done.3
  31.1 11.5 %collective-permute-start.4 = (f32[128,128]{1,0:T(8,128)S(1)}, f32[128,128]{1,0:T(8,128)S(1)}, u32[]{:S(2)}, u32[]{:S(2)}) collective-permute-start(f32[128,128]{1,0:T(8,128)S(1)} %add.99), channel_id=1, source_target_pairs={{0,128},{32,160},{64,192},{96,224},{128,256},{160,288},{192,320},{... | collective-permute-start | bytes 196616 | tf_op jit(solution)/shard_map/ppermute | solution.py:44
  42.6 1.3 collective-permute-done.4
  43.9 0.6 add_add_fusion.1
  44.6 1.2 broadcast_in_dim.29
  45.8 7.8 %all-to-all-start = ((bf16[16,256,128]{2,1,0:T(8,128)(2,1)}), bf16[16,256,128]{2,1,0:T(8,128)(2,1)S(1)}, u32[]{:S(2)}, u32[]{:S(2)}) async-start(bf16[16,256,128]{2,1,0:T(8,128)(2,1)} %broadcast_in_dim.29), calls=%async_computation | async-start | bytes 2097152 | tf_op jit(solution)/shard_map/all_to_all | solution.py:60
  53.6 3.3 %collective-permute-start.5 = (f32[128,128]{1,0:T(8,128)}, f32[128,128]{1,0:T(8,128)S(1)}, u32[]{:S(2)}, u32[]{:S(2)}) collective-permute-start(f32[128,128]{1,0:T(8,128)} %get-tuple-element.7), channel_id=1, source_target_pairs={{0,256},{32,288},{64,320},{96,352},{128,384},{160,416},{192,448},{... | collective-permute-start | bytes 196616 | tf_op jit(solution)/shard_map/ppermute | solution.py:44
  56.9 22.2 %all-to-all-done = bf16[16,256,128]{2,1,0:T(8,128)(2,1)S(1)} async-done(((bf16[16,256,128]{2,1,0:T(8,128)(2,1)}), bf16[16,256,128]{2,1,0:T(8,128)(2,1)S(1)}, u32[]{:S(2)}, u32[]{:S(2)}) %all-to-all-start) | async-done | bytes 1048608 | tf_op jit(solution)/shard_map/all_to_all | solution.py:60
  79.0 3.2 %collective-permute-start.7 = (bf16[16,256,128]{2,1,0:T(8,128)(2,1)S(1)}, bf16[16,256,128]{2,1,0:T(8,128)(2,1)S(1)}, u32[]{:S(2)}, u32[]{:S(2)}) collective-permute-start(bf16[16,256,128]{2,1,0:T(8,128)(2,1)S(1)} %all-to-all-done), channel_id=1, source_target_pairs={{0,16},{16,0},{1,17},{17,1},{2,18},{18,2},{3,19},{19,3},{4,20},{20... | collective-permute-start | bytes 3145736 | tf_op jit(solution)/shard_map/ppermute | solution.py:19
  82.3 0.2 convolution_select_fusion.1
  82.5 1.9 %collective-permute-start.6 = (f32[128,128]{1,0:T(8,128)S(1)}, f32[128,128]{1,0:T(8,128)S(1)}, u32[]{:S(2)}, u32[]{:S(2)}) collective-permute-start(f32[128,128]{1,0:T(8,128)S(1)} %add.103), channel_id=1, source_target_pairs={{0,16},{16,0},{1,17},{17,1},{2,18},{18,2},{3,19},{19,3},{4,20},{20... | collective-permute-start | bytes 196616 | tf_op jit(solution)/shard_map/ppermute | solution.py:19
  84.5 1.2 convolution_bitcast_fusion.2
  85.6 0.1 collective-permute-done.6
  85.7 1.3 multiply_reduce_fusion.1
  87.1 1.5 %select_bitcast_fusion.1 = (bf16[16,1,256,128]{3,2,1,0:T(8,128)(2,1)}, bf16[16,1,256,128]{3,2,1,0:T(8,128)(2,1)}) fusion(bf16[16,256,128]{2,1,0:T(8,128)(2,1)S(1)} %all-to-all-done, bf16[16,256,128]{2,1,0:T(8,128)(2,1)S(1)} %collective-permute-done.7, pred[]{:T(512)S(6)} %eq.4), kind=kLoop, calls=%fused_computation.20 | loop fusion | flops 1048576 | bytes 4194305 | tf_op jit(solution)/shard_map/stack | solution.py:65
  88.6 3.3 %all-gather.2.cloned.1.call-done = bf16[256,4096]{0,1:T(8,128)(2,1)} async-done(((bf16[256,256]{0,1:T(8,128)(2,1)}), bf16[256,4096]{0,1:T(8,128)(2,1)}) %all-gather.2.cloned.1.call-update) | async-done | bytes 2097168 | tf_op jit(solution)/shard_map/all_gather | solution.py:72
  91.8 2.9 %fusion = f32[256,256,1,1]{1,0,3,2:T(8,128)S(1)} fusion(bf16[256,16,2,128]{0,3,2,1:T(8,128)(2,1)} %bitcast.152, bf16[16,1,256,128]{3,2,1,0:T(8,128)(2,1)} %get-tuple-element.20, bf16[16,1,256,128]{3,2,1,0:T(8,128)(2,1)} %get-tuple-element.19), kind=kOutput, calls=%fused_computation | convolution fusion | flops 537919488 | bytes 4456448 | tf_op jit(solution)/shard_map/tqrk,qrjk->tj/dot_general | solution.py:80
  94.8 0.1 multiply_reduce_fusion
  94.9 0.2 fusion.18
  95.1 1.3 collective-permute-start.8
  96.4 1.3 collective-permute-start.9
  97.7 3.1 %collective-permute-start.10 = (f32[2,128,128]{2,1,0:T(8,128)S(1)}, f32[2,128,128]{2,1,0:T(8,128)S(1)}, u32[]{:S(2)}, u32[]{:S(2)}) collective-permute-start(f32[2,128,128]{2,1,0:T(8,128)S(1)} %bitcast.148), channel_id=1, source_target_pairs={{0,16},{16,0},{1,17},{17,1},{2,18},{18,2},{3,19},{19,3},{4,20},{20... | collective-permute-start | bytes 393224 | tf_op jit(solution)/shard_map/ppermute | solution.py:19
  100.9 0.4 fusion.43
  101.2 0.7 collective-permute-done.8
  102.0 3.6 %collective-permute-done.9 = f32[128,128]{1,0:T(8,128)S(1)} collective-permute-done((f32[128,128]{1,0:T(8,128)S(1)}, f32[128,128]{1,0:T(8,128)S(1)}, u32[]{:S(2)}, u32[]{:S(2)}) %collective-permute-start.9) | collective-permute-done | bytes 65568 | tf_op jit(solution)/shard_map/ppermute | solution.py:31
  105.6 1.3 collective-permute-start.11
  106.9 0.3 convolution_select_fusion
  107.2 4.5 %collective-permute-done.11 = f32[128,128]{1,0:T(8,128)S(1)} collective-permute-done((f32[128,128]{1,0:T(8,128)S(1)}, f32[128,128]{1,0:T(8,128)S(1)}, u32[]{:S(2)}, u32[]{:S(2)}) %collective-permute-start.11) | collective-permute-done | bytes 65568 | tf_op jit(solution)/shard_map/ppermute | solution.py:44
  111.7 1.3 collective-permute-start.12
  113.0 0.4 convolution_bitcast_fusion
  113.3 7.3 %collective-permute-done.12 = f32[128,128]{1,0:T(8,128)S(1)} collective-permute-done((f32[128,128]{1,0:T(8,128)S(1)}, f32[128,128]{1,0:T(8,128)S(1)}, u32[]{:S(2)}, u32[]{:S(2)}) %collective-permute-start.12) | collective-permute-done | bytes 65568 | tf_op jit(solution)/shard_map/ppermute | solution.py:44
  120.6 1.3 collective-permute-start.13
  121.9 0.4 convolution_bitcast_fusion.1
  122.3 6.3 %collective-permute-done.13 = f32[128,128]{1,0:T(8,128)S(1)} collective-permute-done((f32[128,128]{1,0:T(8,128)S(1)}, f32[128,128]{1,0:T(8,128)S(1)}, u32[]{:S(2)}, u32[]{:S(2)}) %collective-permute-start.13) | collective-permute-done | bytes 65568 | tf_op jit(solution)/shard_map/ppermute | solution.py:44
  128.6 7.4 %collective-permute-start.14 = (f32[128,128]{1,0:T(8,128)S(1)}, f32[128,128]{1,0:T(8,128)S(1)}, u32[]{:S(2)}, u32[]{:S(2)}) collective-permute-start(f32[128,128]{1,0:T(8,128)S(1)} %add_add_fusion), channel_id=1, source_target_pairs={{0,16},{16,0},{1,17},{17,1},{2,18},{18,2},{3,19},{19,3},{4,20},{20... | collective-permute-start | bytes 196616 | tf_op jit(solution)/shard_map/ppermute | solution.py:19
  136.1 0.3 fusion.7
  136.3 0.8 copy.53
  137.1 0.3 fusion.9
  137.4 0.8 copy.55
  138.2 0.3 fusion.8
  138.5 0.8 copy.54
  (44 shorter events, 0.4 us)
Async XLA Ops:
  7.2 75.1 %copy-start = (bf16[256,256]{1,0:T(8,128)(2,1)S(1)}, bf16[256,256]{1,0:T(8,128)(2,1)}, u32[]{:S(2)}) copy-start(bf16[256,256]{1,0:T(8,128)(2,1)} %param.5) | copy-start | bytes 393220
  7.2 37.4 %copy-start.9 = (bf16[256,128]{1,0:T(8,128)(2,1)S(1)}, bf16[256,128]{1,0:T(8,128)(2,1)}, u32[]{:S(2)}) copy-start(bf16[256,128]{1,0:T(8,128)(2,1)} %param.9) | copy-start | bytes 196612
  7.2 84.6 %all-gather.2.cloned.1.call-start = ((), (), s32[]{:S(2)}) async-start(), calls=%async_computation.1 | async-start | bytes 2228224 | tf_op jit(solution)/shard_map/all_gather | solution.py:72
  9.4 13.4 %collective-permute-start = (f32[2,128,128]{2,1,0:T(8,128)S(1)}, f32[2,128,128]{2,1,0:T(8,128)S(1)}, u32[]{:S(2)}, u32[]{:S(2)}) collective-permute-start(f32[2,128,128]{2,1,0:T(8,128)S(1)} %fusion.13), channel_id=1, source_target_pairs={{0,16},{16,0},{1,17},{17,1},{2,18},{18,2},{3,19},{19,3},{4,20},{20... | collective-permute-start | bytes 393224 | tf_op jit(solution)/shard_map/ppermute | solution.py:19
  18.1 4.6 %collective-permute-start.1 = (f32[128,128]{1,0:T(8,128)S(1)}, f32[128,128]{1,0:T(8,128)S(1)}, u32[]{:S(2)}, u32[]{:S(2)}) collective-permute-start(f32[128,128]{1,0:T(8,128)S(1)} %get-tuple-element.28), channel_id=1, source_target_pairs={{0,32},{32,64},{64,96},{96,128},{128,160},{160,192},{192,224},{224... | collective-permute-start | bytes 196616 | tf_op jit(solution)/shard_map/ppermute | solution.py:30
  19.4 3.3 %collective-permute-start.2 = (f32[128,128]{1,0:T(8,128)S(1)}, f32[128,128]{1,0:T(8,128)S(1)}, u32[]{:S(2)}, u32[]{:S(2)}) collective-permute-start(f32[128,128]{1,0:T(8,128)S(1)} %get-tuple-element.27), channel_id=1, source_target_pairs={{0,48},{16,32},{32,80},{48,64},{64,112},{80,96},{96,144},{112,128}... | collective-permute-start | bytes 196616 | tf_op jit(solution)/shard_map/ppermute | solution.py:31
  22.7 59.6 %copy-start.2 = (bf16[256,256]{1,0:T(8,128)(2,1)S(1)}, bf16[256,256]{1,0:T(8,128)(2,1)}, u32[]{:S(2)}) copy-start(bf16[256,256]{1,0:T(8,128)(2,1)} %param.6) | copy-start | bytes 393220
  22.8 8.3 %collective-permute-start.3 = (f32[128,128]{1,0:T(8,128)S(1)}, f32[128,128]{1,0:T(8,128)S(1)}, u32[]{:S(2)}, u32[]{:S(2)}) collective-permute-start(f32[128,128]{1,0:T(8,128)S(1)} %get-tuple-element.17), channel_id=1, source_target_pairs={{0,64},{32,96},{64,128},{96,160},{128,192},{160,224},{192,256},{22... | collective-permute-start | bytes 196616 | tf_op jit(solution)/shard_map/ppermute | solution.py:44
  31.1 12.8 %collective-permute-start.4 = (f32[128,128]{1,0:T(8,128)S(1)}, f32[128,128]{1,0:T(8,128)S(1)}, u32[]{:S(2)}, u32[]{:S(2)}) collective-permute-start(f32[128,128]{1,0:T(8,128)S(1)} %add.99), channel_id=1, source_target_pairs={{0,128},{32,160},{64,192},{96,224},{128,256},{160,288},{192,320},{... | collective-permute-start | bytes 196616 | tf_op jit(solution)/shard_map/ppermute | solution.py:44
  44.6 39.9 %copy-start.1 = (bf16[256,256]{1,0:T(8,128)(2,1)S(1)}, bf16[256,256]{1,0:T(8,128)(2,1)}, u32[]{:S(2)}) copy-start(bf16[256,256]{1,0:T(8,128)(2,1)} %param.7) | copy-start | bytes 393220
  45.8 33.3 %all-to-all-start = ((bf16[16,256,128]{2,1,0:T(8,128)(2,1)}), bf16[16,256,128]{2,1,0:T(8,128)(2,1)S(1)}, u32[]{:S(2)}, u32[]{:S(2)}) async-start(bf16[16,256,128]{2,1,0:T(8,128)(2,1)} %broadcast_in_dim.29), calls=%async_computation | async-start | bytes 2097152 | tf_op jit(solution)/shard_map/all_to_all | solution.py:60
  53.6 32.1 %copy-start.7 = (pred[256,256]{1,0:T(8,128)(4,1)}, pred[256,256]{1,0:T(8,128)(4,1)S(1)}, u32[]{:S(2)}) copy-start(pred[256,256]{1,0:T(8,128)(4,1)S(1)} %iota_compare_fusion) | copy-start | bytes 196612
  53.6 28.9 %collective-permute-start.5 = (f32[128,128]{1,0:T(8,128)}, f32[128,128]{1,0:T(8,128)S(1)}, u32[]{:S(2)}, u32[]{:S(2)}) collective-permute-start(f32[128,128]{1,0:T(8,128)} %get-tuple-element.7), channel_id=1, source_target_pairs={{0,256},{32,288},{64,320},{96,352},{128,384},{160,416},{192,448},{... | collective-permute-start | bytes 196616 | tf_op jit(solution)/shard_map/ppermute | solution.py:44
  79.0 8.0 %collective-permute-start.7 = (bf16[16,256,128]{2,1,0:T(8,128)(2,1)S(1)}, bf16[16,256,128]{2,1,0:T(8,128)(2,1)S(1)}, u32[]{:S(2)}, u32[]{:S(2)}) collective-permute-start(bf16[16,256,128]{2,1,0:T(8,128)(2,1)S(1)} %all-to-all-done), channel_id=1, source_target_pairs={{0,16},{16,0},{1,17},{17,1},{2,18},{18,2},{3,19},{19,3},{4,20},{20... | collective-permute-start | bytes 3145736 | tf_op jit(solution)/shard_map/ppermute | solution.py:19
  82.5 3.1 %collective-permute-start.6 = (f32[128,128]{1,0:T(8,128)S(1)}, f32[128,128]{1,0:T(8,128)S(1)}, u32[]{:S(2)}, u32[]{:S(2)}) collective-permute-start(f32[128,128]{1,0:T(8,128)S(1)} %add.103), channel_id=1, source_target_pairs={{0,16},{16,0},{1,17},{17,1},{2,18},{18,2},{3,19},{19,3},{4,20},{20... | collective-permute-start | bytes 196616 | tf_op jit(solution)/shard_map/ppermute | solution.py:19
  85.7 1.4 copy-start.3
  85.7 1.4 copy-start.5
  94.8 12.1 %copy-start.8 = (pred[256,256]{1,0:T(8,128)(4,1)S(1)}, pred[256,256]{1,0:T(8,128)(4,1)}, u32[]{:S(2)}) copy-start(pred[256,256]{1,0:T(8,128)(4,1)} %copy-done.7) | copy-start | bytes 196612
  95.1 6.8 %collective-permute-start.8 = (f32[128,128]{1,0:T(8,128)S(1)}, f32[128,128]{1,0:T(8,128)S(1)}, u32[]{:S(2)}, u32[]{:S(2)}) collective-permute-start(f32[128,128]{1,0:T(8,128)S(1)} %get-tuple-element.24), channel_id=1, source_target_pairs={{32,0},{64,32},{96,64},{128,96},{160,128},{192,160},{224,192},{256... | collective-permute-start | bytes 196616 | tf_op jit(solution)/shard_map/ppermute | solution.py:30
  96.4 9.1 %collective-permute-start.9 = (f32[128,128]{1,0:T(8,128)S(1)}, f32[128,128]{1,0:T(8,128)S(1)}, u32[]{:S(2)}, u32[]{:S(2)}) collective-permute-start(f32[128,128]{1,0:T(8,128)S(1)} %get-tuple-element.23), channel_id=1, source_target_pairs={{32,16},{48,0},{64,48},{80,32},{96,80},{112,64},{128,112},{144,96}... | collective-permute-start | bytes 196616 | tf_op jit(solution)/shard_map/ppermute | solution.py:31
  97.7 7.8 %collective-permute-start.10 = (f32[2,128,128]{2,1,0:T(8,128)S(1)}, f32[2,128,128]{2,1,0:T(8,128)S(1)}, u32[]{:S(2)}, u32[]{:S(2)}) collective-permute-start(f32[2,128,128]{2,1,0:T(8,128)S(1)} %bitcast.148), channel_id=1, source_target_pairs={{0,16},{16,0},{1,17},{17,1},{2,18},{18,2},{3,19},{19,3},{4,20},{20... | collective-permute-start | bytes 393224 | tf_op jit(solution)/shard_map/ppermute | solution.py:19
  101.2 34.8 %copy-start.4 = (f32[1,128,128]{2,1,0:T(8,128)S(1)}, f32[1,128,128]{2,1,0:T(8,128)}, u32[]{:S(2)}) copy-start(f32[1,128,128]{2,1,0:T(8,128)} %copy-done.3) | copy-start | bytes 196612
  101.2 34.8 %copy-start.6 = (f32[1,128,128]{2,1,0:T(8,128)S(1)}, f32[1,128,128]{2,1,0:T(8,128)}, u32[]{:S(2)}) copy-start(f32[1,128,128]{2,1,0:T(8,128)} %copy-done.5) | copy-start | bytes 196612
  105.6 6.1 %collective-permute-start.11 = (f32[128,128]{1,0:T(8,128)S(1)}, f32[128,128]{1,0:T(8,128)S(1)}, u32[]{:S(2)}, u32[]{:S(2)}) collective-permute-start(f32[128,128]{1,0:T(8,128)S(1)} %get-tuple-element.15), channel_id=1, source_target_pairs={{64,0},{96,32},{128,64},{160,96},{192,128},{224,160},{256,192},{28... | collective-permute-start | bytes 196616 | tf_op jit(solution)/shard_map/ppermute | solution.py:44
  111.7 8.9 %collective-permute-start.12 = (f32[128,128]{1,0:T(8,128)S(1)}, f32[128,128]{1,0:T(8,128)S(1)}, u32[]{:S(2)}, u32[]{:S(2)}) collective-permute-start(f32[128,128]{1,0:T(8,128)S(1)} %add.113), channel_id=1, source_target_pairs={{128,0},{160,32},{192,64},{224,96},{256,128},{288,160},{320,192},{... | collective-permute-start | bytes 196616 | tf_op jit(solution)/shard_map/ppermute | solution.py:44
  120.6 8.0 %collective-permute-start.13 = (f32[128,128]{1,0:T(8,128)S(1)}, f32[128,128]{1,0:T(8,128)S(1)}, u32[]{:S(2)}, u32[]{:S(2)}) collective-permute-start(f32[128,128]{1,0:T(8,128)S(1)} %add.115), channel_id=1, source_target_pairs={{256,0},{288,32},{320,64},{352,96},{384,128},{416,160},{448,192},{... | collective-permute-start | bytes 196616 | tf_op jit(solution)/shard_map/ppermute | solution.py:44
  128.6 8.5 %collective-permute-start.14 = (f32[128,128]{1,0:T(8,128)S(1)}, f32[128,128]{1,0:T(8,128)S(1)}, u32[]{:S(2)}, u32[]{:S(2)}) collective-permute-start(f32[128,128]{1,0:T(8,128)S(1)} %add_add_fusion), channel_id=1, source_target_pairs={{0,16},{16,0},{1,17},{17,1},{2,18},{18,2},{3,19},{19,3},{4,20},{20... | collective-permute-start | bytes 196616 | tf_op jit(solution)/shard_map/ppermute | solution.py:19
Sparse Core Ops, SparseCore 0:
  22.8 68.9 all-gather.1

commit v10 on v2

--- a/solution.py
+++ b/solution.py
@@ -67,16 +67,9 @@
     head_count = feat_width // E
     full_rows = lax.all_gather(grad_out, TP, axis=1, tiled=True)
     columns = gather_columns(w_out)
-    grad_z = jnp.einsum(
-        "tqrk,qrjk->tj",
-        full_rows.reshape(tok_rows, columns.shape[0], 2, columns.shape[3]),
-        columns,
-        preferred_element_type=jnp.float32,
-    )
     query_heads = query.reshape(tok_rows, head_count, E)
     key_heads = key_feat.reshape(tok_rows, head_count, E)
     value_heads = value.reshape(tok_rows, head_count, E)
-    gradz_heads = grad_z.reshape(tok_rows, head_count, E)
     query_wide = query_heads.astype(jnp.float32)
     key_wide = key_heads.astype(jnp.float32)
     value_wide = value_heads.astype(jnp.float32)
@@ -89,7 +82,15 @@
     local_state = jnp.einsum(
         "shd,she->hde", key_heads, value_heads, preferred_element_type=jnp.float32
     )
+    columns, local_state = lax.optimization_barrier((columns, local_state))
     state_in = ctx_scan(local_state, False)
+    grad_z = jnp.einsum(
+        "tqrk,qrjk->tj",
+        full_rows.reshape(tok_rows, columns.shape[0], 2, columns.shape[3]),
+        columns,
+        preferred_element_type=jnp.float32,
+    )
+    gradz_heads = grad_z.reshape(tok_rows, head_count, E)
     attended = jnp.einsum("hts,she->the", weights, value_wide, precision=highest)
     attended = attended + jnp.einsum("thd,hde->the", query_wide, state_in, precision=highest)
     inv_rms = lax.rsqrt(jnp.mean(attended * attended, axis=-1, keepdims=True) + epsilon)

time: 139 us -> 153 us (1.10)
  waiting for transfers between devices: 36.5 us -> 54.5 us
  starting transfers between devices: 68 us -> 66.3 us
    all_to_all x1, waiting for transfers between devices: 0.01 us -> 24.6 us  [gather_columns(): mine = lax.all_to_all(spread, CHIPS, 0, 0, tiled=True)]
    ppermute x8, waiting for transfers between devices: 34.2 us -> 25.9 us  [ctx_scan(): arrived = lax.ppermute(window, CHIPS, pairs)]
    ppermute x8, starting transfers between devices: 33.5 us -> 30.3 us  [ctx_scan(): arrived = lax.ppermute(window, CHIPS, pairs)]
    ppermute x5, waiting for transfers between devices: 2.2 us -> 3.96 us  [swap_cores(): return lax.ppermute(value, 'core', [(0, 1), (1, 0)])]
    unnamed x22 -> x24, local copies, waits for them, and re-layouts: 4.09 us -> 3.7 us
  transfers between devices with their start and end apart: 15 -> 15, of which waited for: 9 -> 12; matrix products, arithmetic and copies ran while one was open for 8% -> 5% of each run, Pallas kernels for 0% -> 0%
where the time goes in v10:
time: 153 us; the launch traced here: 151 us
  starting transfers between devices  66.3 us (43%)
  waiting for transfers between devices  54.5 us (36%)
  between operations  14.5 us (9%)
  matrix products  7.64 us (5%)
  local copies, waits for them, and re-layouts  5.88 us (4%)
  other arithmetic  2.08 us (1%)
    ppermute x8, starting transfers between devices, ctx_scan(): arrived = lax.ppermute(window, CHIPS, pairs)  30.3 us
    ppermute x8, waiting for transfers between devices, ctx_scan(): arrived = lax.ppermute(window, CHIPS, pairs)  25.9 us
    all_to_all x1, waiting for transfers between devices, gather_columns(): mine = lax.all_to_all(spread, CHIPS, 0, 0, tiled=True)  24.6 us
    ppermute x5, starting transfers between devices, swap_cores(): return lax.ppermute(value, 'core', [(0, 1), (1, 0)])  24 us
    all_to_all x1, starting transfers between devices, gather_columns(): mine = lax.all_to_all(spread, CHIPS, 0, 0, tiled=True)  12 us
    ppermute x5, waiting for transfers between devices, swap_cores(): return lax.ppermute(value, 'core', [(0, 1), (1, 0)])  3.96 us
    unnamed x24, local copies, waits for them, and re-layouts  3.7 us
  transfers between devices with their start and end apart: 15, of which 12 were waited for; matrix products, arithmetic and copies ran while one was open for 5% of the time, Pallas kernels for 0%

profile of v10, /device:TPU:1, one launch (start us, length us, event | category | flops | bytes accessed | tf_op | source)
XLA Modules:
  0.0 150.9 jit_solution(5762260998620704833)
XLA Ops:
  7.2 2.1 %broadcast_in_dim.29 = bf16[16,256,128]{2,1,0:T(8,128)(2,1)} broadcast(bf16[256,128]{1,0:T(8,128)(2,1)} %param.9), dimensions={1,2} | broadcast | bytes 1114112 | tf_op jit(solution)/shard_map/broadcast_in_dim | solution.py:55
  9.3 12.0 %all-to-all-start = ((bf16[16,256,128]{2,1,0:T(8,128)(2,1)}), bf16[16,256,128]{2,1,0:T(8,128)(2,1)S(1)}, u32[]{:S(2)}, u32[]{:S(2)}) async-start(bf16[16,256,128]{2,1,0:T(8,128)(2,1)} %broadcast_in_dim.29), calls=%async_computation | async-start | bytes 2097152 | tf_op jit(solution)/shard_map/all_to_all | solution.py:56
  21.3 0.8 copy.37
  22.1 24.6 %all-to-all-done = bf16[16,256,128]{2,1,0:T(8,128)(2,1)S(1)} async-done(((bf16[16,256,128]{2,1,0:T(8,128)(2,1)}), bf16[16,256,128]{2,1,0:T(8,128)(2,1)S(1)}, u32[]{:S(2)}, u32[]{:S(2)}) %all-to-all-start) | async-done | bytes 1048608 | tf_op jit(solution)/shard_map/all_to_all | solution.py:56
  46.7 3.2 %collective-permute-start = (bf16[16,256,128]{2,1,0:T(8,128)(2,1)S(1)}, bf16[16,256,128]{2,1,0:T(8,128)(2,1)S(1)}, u32[]{:S(2)}, u32[]{:S(2)}) collective-permute-start(bf16[16,256,128]{2,1,0:T(8,128)(2,1)S(1)} %all-to-all-done), channel_id=1, source_target_pairs={{0,16},{16,0},{1,17},{17,1},{2,18},{18,2},{3,19},{19,3},{4,20},{20... | collective-permute-start | bytes 3145736 | tf_op jit(solution)/shard_map/ppermute | solution.py:19
  50.0 0.2 fusion.9
  50.2 2.0 %collective-permute-done = bf16[16,256,128]{2,1,0:T(8,128)(2,1)S(1)} collective-permute-done((bf16[16,256,128]{2,1,0:T(8,128)(2,1)S(1)}, bf16[16,256,128]{2,1,0:T(8,128)(2,1)S(1)}, u32[]{:S(2)}, u32[]{:S(2)}) %collective-permute-start) | collective-permute-done | bytes 1048608 | tf_op jit(solution)/shard_map/ppermute | solution.py:19
  52.3 0.2 pad_maximum_fusion
  52.5 2.3 %collective-permute-start.1 = (f32[2,128,128]{2,1,0:T(8,128)S(1)}, f32[2,128,128]{2,1,0:T(8,128)S(1)}, u32[]{:S(2)}, u32[]{:S(2)}) collective-permute-start(f32[2,128,128]{2,1,0:T(8,128)S(1)} %fusion.9), channel_id=1, source_target_pairs={{0,16},{16,0},{1,17},{17,1},{2,18},{18,2},{3,19},{19,3},{4,20},{20... | collective-permute-start | bytes 393224 | tf_op jit(solution)/shard_map/ppermute | solution.py:19
  54.8 1.0 collective-permute-done.1
  55.8 5.2 %collective-permute-start.2 = (f32[128,128]{1,0:T(8,128)S(1)}, f32[128,128]{1,0:T(8,128)S(1)}, u32[]{:S(2)}, u32[]{:S(2)}) collective-permute-start(f32[128,128]{1,0:T(8,128)S(1)} %add_bitcast_fusion.1), channel_id=1, source_target_pairs={{0,32},{32,64},{64,96},{96,128},{128,160},{160,192},{192,224},{224... | collective-permute-start | bytes 196616 | tf_op jit(solution)/shard_map/ppermute | solution.py:42
  61.0 1.3 collective-permute-done.2
  62.4 3.8 %collective-permute-start.3 = (f32[128,128]{1,0:T(8,128)S(1)}, f32[128,128]{1,0:T(8,128)S(1)}, u32[]{:S(2)}, u32[]{:S(2)}) collective-permute-start(f32[128,128]{1,0:T(8,128)S(1)} %add.79), channel_id=1, source_target_pairs={{0,64},{32,96},{64,128},{96,160},{128,192},{160,224},{192,256},{22... | collective-permute-start | bytes 196616 | tf_op jit(solution)/shard_map/ppermute | solution.py:42
  66.1 1.3 collective-permute-done.3
  67.5 7.7 %collective-permute-start.4 = (f32[128,128]{1,0:T(8,128)S(1)}, f32[128,128]{1,0:T(8,128)S(1)}, u32[]{:S(2)}, u32[]{:S(2)}) collective-permute-start(f32[128,128]{1,0:T(8,128)S(1)} %add.81), channel_id=1, source_target_pairs={{0,128},{32,160},{64,192},{96,224},{128,256},{160,288},{192,320},{... | collective-permute-start | bytes 196616 | tf_op jit(solution)/shard_map/ppermute | solution.py:42
  75.2 1.3 collective-permute-done.4
  76.5 8.3 %collective-permute-start.5 = (f32[128,128]{1,0:T(8,128)S(1)}, f32[128,128]{1,0:T(8,128)S(1)}, u32[]{:S(2)}, u32[]{:S(2)}) collective-permute-start(f32[128,128]{1,0:T(8,128)S(1)} %add.83), channel_id=1, source_target_pairs={{0,256},{32,288},{64,320},{96,352},{128,384},{160,416},{192,448},{... | collective-permute-start | bytes 196616 | tf_op jit(solution)/shard_map/ppermute | solution.py:42
  84.8 0.2 convolution_select_fusion.1
  85.1 2.9 %collective-permute-done.5 = f32[128,128]{1,0:T(8,128)S(1)} collective-permute-done((f32[128,128]{1,0:T(8,128)S(1)}, f32[128,128]{1,0:T(8,128)S(1)}, u32[]{:S(2)}, u32[]{:S(2)}) %collective-permute-start.5) | collective-permute-done | bytes 65568 | tf_op jit(solution)/shard_map/ppermute | solution.py:42
  88.0 0.6 add_add_fusion.1
  88.6 10.0 %collective-permute-start.6 = (f32[128,128]{1,0:T(8,128)}, f32[128,128]{1,0:T(8,128)S(1)}, u32[]{:S(2)}, u32[]{:S(2)}) collective-permute-start(f32[128,128]{1,0:T(8,128)} %add_add_fusion.1), channel_id=1, source_target_pairs={{0,16},{16,0},{1,17},{17,1},{2,18},{18,2},{3,19},{19,3},{4,20},{20... | collective-permute-start | bytes 196616 | tf_op jit(solution)/shard_map/ppermute | solution.py:19
  98.7 1.2 convolution_bitcast_fusion.2
  99.8 0.9 select_bitcast_fusion.5
  100.7 0.6 copy-done.3
  101.3 1.3 multiply_reduce_fusion.1
  102.7 2.3 %fusion.35 = f32[256,256,1,1]{1,0,3,2:T(8,128)S(1)} fusion(bf16[16,2,256,128]{3,2,1,0:T(8,128)(2,1)S(1)} %pad_maximum_fusion, bf16[256,16,2,128]{0,3,2,1:T(8,128)(2,1)} %bitcast.128), kind=kOutput, calls=%fused_computation.64 | convolution fusion | flops 536870912 | bytes 4456448 | tf_op jit(solution)/shard_map/tqrk,qrjk->tj/dot_general | solution.py:87
  105.1 0.2 convolution_bitcast_fusion.6
  105.4 2.2 %collective-permute-start.7 = (f32[2,128,128]{2,1,0:T(8,128)S(1)}, f32[2,128,128]{2,1,0:T(8,128)S(1)}, u32[]{:S(2)}, u32[]{:S(2)}) collective-permute-start(f32[2,128,128]{2,1,0:T(8,128)S(1)} %convolution_bitcast_fusion.6), channel_id=1, source_target_pairs={{0,16},{16,0},{1,17},{17,1},{2,18},{18,2},{3,19},{19,3},{4,20},{20... | collective-permute-start | bytes 393224 | tf_op jit(solution)/shard_map/ppermute | solution.py:19
  107.6 1.0 collective-permute-done.7
  108.6 1.4 collective-permute-start.8
  110.1 0.3 convolution_select_fusion
  110.4 4.2 %collective-permute-done.8 = f32[128,128]{1,0:T(8,128)S(1)} collective-permute-done((f32[128,128]{1,0:T(8,128)S(1)}, f32[128,128]{1,0:T(8,128)S(1)}, u32[]{:S(2)}, u32[]{:S(2)}) %collective-permute-start.8) | collective-permute-done | bytes 65568 | tf_op jit(solution)/shard_map/ppermute | solution.py:42
  114.5 1.3 collective-permute-start.9
  115.8 0.4 convolution_bitcast_fusion.1
  116.3 4.2 %collective-permute-done.9 = f32[128,128]{1,0:T(8,128)S(1)} collective-permute-done((f32[128,128]{1,0:T(8,128)S(1)}, f32[128,128]{1,0:T(8,128)S(1)}, u32[]{:S(2)}, u32[]{:S(2)}) %collective-permute-start.9) | collective-permute-done | bytes 65568 | tf_op jit(solution)/shard_map/ppermute | solution.py:42
  120.5 1.3 collective-permute-start.10
  121.8 0.4 convolution_bitcast_fusion
  122.1 7.4 %collective-permute-done.10 = f32[128,128]{1,0:T(8,128)S(1)} collective-permute-done((f32[128,128]{1,0:T(8,128)S(1)}, f32[128,128]{1,0:T(8,128)S(1)}, u32[]{:S(2)}, u32[]{:S(2)}) %collective-permute-start.10) | collective-permute-done | bytes 65568 | tf_op jit(solution)/shard_map/ppermute | solution.py:42
  129.5 1.3 collective-permute-start.11
  130.8 0.4 fusion.36
  131.2 3.4 %collective-permute-done.11 = f32[128,128]{1,0:T(8,128)S(1)} collective-permute-done((f32[128,128]{1,0:T(8,128)S(1)}, f32[128,128]{1,0:T(8,128)S(1)}, u32[]{:S(2)}, u32[]{:S(2)}) %collective-permute-start.11) | collective-permute-done | bytes 65568 | tf_op jit(solution)/shard_map/ppermute | solution.py:42
  134.5 6.3 %collective-permute-start.12 = (f32[128,128]{1,0:T(8,128)S(1)}, f32[128,128]{1,0:T(8,128)S(1)}, u32[]{:S(2)}, u32[]{:S(2)}) collective-permute-start(f32[128,128]{1,0:T(8,128)S(1)} %add_add_fusion), channel_id=1, source_target_pairs={{0,16},{16,0},{1,17},{17,1},{2,18},{18,2},{3,19},{19,3},{4,20},{20... | collective-permute-start | bytes 196616 | tf_op jit(solution)/shard_map/ppermute | solution.py:19
  140.8 0.3 fusion.3
  141.1 0.8 copy.49
  141.9 0.3 fusion.4
  142.2 0.8 copy.50
  142.9 0.3 fusion.5
  143.3 0.8 copy.51
  (41 shorter events, 0.6 us)
Async XLA Ops:
  7.2 77.7 %copy-start = (bf16[256,256]{1,0:T(8,128)(2,1)S(1)}, bf16[256,256]{1,0:T(8,128)(2,1)}, u32[]{:S(2)}) copy-start(bf16[256,256]{1,0:T(8,128)(2,1)} %param.5) | copy-start | bytes 393220
  7.2 14.1 %copy-start.9 = (bf16[256,256]{1,0:T(8,128)(2,1)S(1)}, bf16[256,256]{1,0:T(8,128)(2,1)}, u32[]{:S(2)}) copy-start(bf16[256,256]{1,0:T(8,128)(2,1)} %param.8) | copy-start | bytes 393220
  7.2 42.7 %copy-start.2 = (bf16[256,256]{1,0:T(8,128)(2,1)S(1)}, bf16[256,256]{1,0:T(8,128)(2,1)}, u32[]{:S(2)}) copy-start(bf16[256,256]{1,0:T(8,128)(2,1)} %param.6) | copy-start | bytes 393220
  7.2 42.8 %copy-start.1 = (bf16[256,256]{1,0:T(8,128)(2,1)S(1)}, bf16[256,256]{1,0:T(8,128)(2,1)}, u32[]{:S(2)}) copy-start(bf16[256,256]{1,0:T(8,128)(2,1)} %param.7) | copy-start | bytes 393220
  9.3 37.4 %all-to-all-start = ((bf16[16,256,128]{2,1,0:T(8,128)(2,1)}), bf16[16,256,128]{2,1,0:T(8,128)(2,1)S(1)}, u32[]{:S(2)}, u32[]{:S(2)}) async-start(bf16[16,256,128]{2,1,0:T(8,128)(2,1)} %broadcast_in_dim.29), calls=%async_computation | async-start | bytes 2097152 | tf_op jit(solution)/shard_map/all_to_all | solution.py:56
  21.3 81.4 %all-gather.2.cloned.1.call-start = ((), (), s32[]{:S(2)}) async-start(), calls=%async_computation.1 | async-start | bytes 2228224 | tf_op jit(solution)/shard_map/all_gather | solution.py:68
  46.7 5.5 %collective-permute-start = (bf16[16,256,128]{2,1,0:T(8,128)(2,1)S(1)}, bf16[16,256,128]{2,1,0:T(8,128)(2,1)S(1)}, u32[]{:S(2)}, u32[]{:S(2)}) collective-permute-start(bf16[16,256,128]{2,1,0:T(8,128)(2,1)S(1)} %all-to-all-done), channel_id=1, source_target_pairs={{0,16},{16,0},{1,17},{17,1},{2,18},{18,2},{3,19},{19,3},{4,20},{20... | collective-permute-start | bytes 3145736 | tf_op jit(solution)/shard_map/ppermute | solution.py:19
  52.5 3.3 %collective-permute-start.1 = (f32[2,128,128]{2,1,0:T(8,128)S(1)}, f32[2,128,128]{2,1,0:T(8,128)S(1)}, u32[]{:S(2)}, u32[]{:S(2)}) collective-permute-start(f32[2,128,128]{2,1,0:T(8,128)S(1)} %fusion.9), channel_id=1, source_target_pairs={{0,16},{16,0},{1,17},{17,1},{2,18},{18,2},{3,19},{19,3},{4,20},{20... | collective-permute-start | bytes 393224 | tf_op jit(solution)/shard_map/ppermute | solution.py:19
  55.8 6.6 %collective-permute-start.2 = (f32[128,128]{1,0:T(8,128)S(1)}, f32[128,128]{1,0:T(8,128)S(1)}, u32[]{:S(2)}, u32[]{:S(2)}) collective-permute-start(f32[128,128]{1,0:T(8,128)S(1)} %add_bitcast_fusion.1), channel_id=1, source_target_pairs={{0,32},{32,64},{64,96},{96,128},{128,160},{160,192},{192,224},{224... | collective-permute-start | bytes 196616 | tf_op jit(solution)/shard_map/ppermute | solution.py:42
  62.4 5.1 %collective-permute-start.3 = (f32[128,128]{1,0:T(8,128)S(1)}, f32[128,128]{1,0:T(8,128)S(1)}, u32[]{:S(2)}, u32[]{:S(2)}) collective-permute-start(f32[128,128]{1,0:T(8,128)S(1)} %add.79), channel_id=1, source_target_pairs={{0,64},{32,96},{64,128},{96,160},{128,192},{160,224},{192,256},{22... | collective-permute-start | bytes 196616 | tf_op jit(solution)/shard_map/ppermute | solution.py:42
  67.5 9.0 %collective-permute-start.4 = (f32[128,128]{1,0:T(8,128)S(1)}, f32[128,128]{1,0:T(8,128)S(1)}, u32[]{:S(2)}, u32[]{:S(2)}) collective-permute-start(f32[128,128]{1,0:T(8,128)S(1)} %add.81), channel_id=1, source_target_pairs={{0,128},{32,160},{64,192},{96,224},{128,256},{160,288},{192,320},{... | collective-permute-start | bytes 196616 | tf_op jit(solution)/shard_map/ppermute | solution.py:42
  75.2 25.5 %copy-start.7 = (pred[256,256]{1,0:T(8,128)(4,1)}, pred[256,256]{1,0:T(8,128)(4,1)S(1)}, u32[]{:S(2)}) copy-start(pred[256,256]{1,0:T(8,128)(4,1)S(1)} %iota_compare_fusion) | copy-start | bytes 196612
  76.5 11.5 %collective-permute-start.5 = (f32[128,128]{1,0:T(8,128)S(1)}, f32[128,128]{1,0:T(8,128)S(1)}, u32[]{:S(2)}, u32[]{:S(2)}) collective-permute-start(f32[128,128]{1,0:T(8,128)S(1)} %add.83), channel_id=1, source_target_pairs={{0,256},{32,288},{64,320},{96,352},{128,384},{160,416},{192,448},{... | collective-permute-start | bytes 196616 | tf_op jit(solution)/shard_map/ppermute | solution.py:42
  88.6 11.2 %collective-permute-start.6 = (f32[128,128]{1,0:T(8,128)}, f32[128,128]{1,0:T(8,128)S(1)}, u32[]{:S(2)}, u32[]{:S(2)}) collective-permute-start(f32[128,128]{1,0:T(8,128)} %add_add_fusion.1), channel_id=1, source_target_pairs={{0,16},{16,0},{1,17},{17,1},{2,18},{18,2},{3,19},{19,3},{4,20},{20... | collective-permute-start | bytes 196616 | tf_op jit(solution)/shard_map/ppermute | solution.py:19
  100.7 0.6 copy-start.3
  100.7 1.9 %copy-start.5 = (f32[1,128,128]{2,1,0:T(8,128)}, f32[1,128,128]{2,1,0:T(8,128)S(1)}, u32[]{:S(2)}) copy-start(f32[1,128,128]{2,1,0:T(8,128)S(1)} %get-tuple-element.18) | copy-start | bytes 196612
  102.7 7.4 %copy-start.8 = (pred[256,256]{1,0:T(8,128)(4,1)S(1)}, pred[256,256]{1,0:T(8,128)(4,1)}, u32[]{:S(2)}) copy-start(pred[256,256]{1,0:T(8,128)(4,1)} %copy-done.7) | copy-start | bytes 196612
  105.4 3.2 %collective-permute-start.7 = (f32[2,128,128]{2,1,0:T(8,128)S(1)}, f32[2,128,128]{2,1,0:T(8,128)S(1)}, u32[]{:S(2)}, u32[]{:S(2)}) collective-permute-start(f32[2,128,128]{2,1,0:T(8,128)S(1)} %convolution_bitcast_fusion.6), channel_id=1, source_target_pairs={{0,16},{16,0},{1,17},{17,1},{2,18},{18,2},{3,19},{19,3},{4,20},{20... | collective-permute-start | bytes 393224 | tf_op jit(solution)/shard_map/ppermute | solution.py:19
  108.6 32.2 %copy-start.4 = (f32[1,128,128]{2,1,0:T(8,128)S(1)}, f32[1,128,128]{2,1,0:T(8,128)}, u32[]{:S(2)}) copy-start(f32[1,128,128]{2,1,0:T(8,128)} %copy-done.3) | copy-start | bytes 196612
  108.6 32.2 %copy-start.6 = (f32[1,128,128]{2,1,0:T(8,128)S(1)}, f32[1,128,128]{2,1,0:T(8,128)}, u32[]{:S(2)}) copy-start(f32[1,128,128]{2,1,0:T(8,128)} %copy-done.5) | copy-start | bytes 196612
  108.6 5.9 %collective-permute-start.8 = (f32[128,128]{1,0:T(8,128)S(1)}, f32[128,128]{1,0:T(8,128)S(1)}, u32[]{:S(2)}, u32[]{:S(2)}) collective-permute-start(f32[128,128]{1,0:T(8,128)S(1)} %add_bitcast_fusion), channel_id=1, source_target_pairs={{32,0},{64,32},{96,64},{128,96},{160,128},{192,160},{224,192},{256... | collective-permute-start | bytes 196616 | tf_op jit(solution)/shard_map/ppermute | solution.py:42
  114.5 5.9 %collective-permute-start.9 = (f32[128,128]{1,0:T(8,128)S(1)}, f32[128,128]{1,0:T(8,128)S(1)}, u32[]{:S(2)}, u32[]{:S(2)}) collective-permute-start(f32[128,128]{1,0:T(8,128)S(1)} %add.91), channel_id=1, source_target_pairs={{64,0},{96,32},{128,64},{160,96},{192,128},{224,160},{256,192},{28... | collective-permute-start | bytes 196616 | tf_op jit(solution)/shard_map/ppermute | solution.py:42
  120.5 9.0 %collective-permute-start.10 = (f32[128,128]{1,0:T(8,128)S(1)}, f32[128,128]{1,0:T(8,128)S(1)}, u32[]{:S(2)}, u32[]{:S(2)}) collective-permute-start(f32[128,128]{1,0:T(8,128)S(1)} %add.93), channel_id=1, source_target_pairs={{128,0},{160,32},{192,64},{224,96},{256,128},{288,160},{320,192},{... | collective-permute-start | bytes 196616 | tf_op jit(solution)/shard_map/ppermute | solution.py:42
  129.5 5.0 %collective-permute-start.11 = (f32[128,128]{1,0:T(8,128)S(1)}, f32[128,128]{1,0:T(8,128)S(1)}, u32[]{:S(2)}, u32[]{:S(2)}) collective-permute-start(f32[128,128]{1,0:T(8,128)S(1)} %add.95), channel_id=1, source_target_pairs={{256,0},{288,32},{320,64},{352,96},{384,128},{416,160},{448,192},{... | collective-permute-start | bytes 196616 | tf_op jit(solution)/shard_map/ppermute | solution.py:42
  134.5 7.3 %collective-permute-start.12 = (f32[128,128]{1,0:T(8,128)S(1)}, f32[128,128]{1,0:T(8,128)S(1)}, u32[]{:S(2)}, u32[]{:S(2)}) collective-permute-start(f32[128,128]{1,0:T(8,128)S(1)} %add_add_fusion), channel_id=1, source_target_pairs={{0,16},{16,0},{1,17},{17,1},{2,18},{18,2},{3,19},{19,3},{4,20},{20... | collective-permute-start | bytes 196616 | tf_op jit(solution)/shard_map/ppermute | solution.py:19
Sparse Core Ops, SparseCore 0:
  25.7 64.7 all-gather.1

commit v11 on v4

--- a/solution.py
+++ b/solution.py
@@ -20,6 +20,37 @@
 
 
 def ctx_scan(local_state, backward):
+    core = lax.axis_index("core")
+    other = swap_cores(local_state)
+    first = jnp.where(core == 0, local_state, other)
+    second = jnp.where(core == 0, other, local_state)
+    chip_total = first + second
+    if backward:
+        within = jnp.where(core == 0, other, jnp.zeros_like(other))
+    else:
+        within = jnp.where(core == 1, other, jnp.zeros_like(other))
+    half = lax.dynamic_index_in_dim(chip_total, core, 0, keepdims=False)
+    chips = lax.axis_size("ylo") * lax.axis_size("z")
+    window = half
+    below = jnp.zeros_like(half)
+    distance = 1
+    while distance < chips:
+        if backward:
+            pairs = [(q, q - distance) for q in range(distance, chips)]
+        else:
+            pairs = [(q, q + distance) for q in range(chips - distance)]
+        arrived = lax.ppermute(window, CHIPS, pairs)
+        below = below + arrived
+        if distance * 2 < chips:
+            window = window + arrived
+        distance *= 2
+    other_half = swap_cores(below)
+    head0 = jnp.where(core == 0, below, other_half)
+    head1 = jnp.where(core == 0, other_half, below)
+    return jnp.stack([head0, head1]) + within
+
+
+def merged_scan(local_state, backward):
     core = lax.axis_index("core")
     chips = lax.axis_size("ylo") * lax.axis_size("z")
     step = -1 if backward else 1
@@ -110,7 +141,7 @@
     local_adjoint = jnp.einsum(
         "thd,the->hde", query_heads, grad_att, preferred_element_type=jnp.float32
     )
-    adjoint = ctx_scan(local_adjoint, True)
+    adjoint = merged_scan(local_adjoint, True)
     grad_key = jnp.einsum("hts,thd->shd", grad_weights, query_wide, precision=highest)
     grad_key = grad_key + jnp.einsum("she,hde->shd", value_wide, adjoint, precision=highest)
     grad_value = jnp.einsum("hts,the->she", weights, grad_wide, precision=highest)

time: 140 us -> 139 us (level)
  the two profiles are of different devices: /device:TPU:51 before, /device:TPU:1 now
where the time goes in v11:
time: 139 us; the launch traced here: 137 us
  starting transfers between devices  66.9 us (48%)
  waiting for transfers between devices  38.2 us (27%)
  between operations  14.5 us (10%)
  matrix products  8.29 us (6%)
  local copies, waits for them, and re-layouts  6.24 us (4%)
  other arithmetic  3.19 us (2%)
    ppermute x4, starting transfers between devices, ctx_scan(): arrived = lax.ppermute(window, CHIPS, pairs)  28.2 us
    ppermute x5, starting transfers between devices, swap_cores(): return lax.ppermute(value, 'core', [(0, 1), (1, 0)])  20.2 us
    ppermute x3, waiting for transfers between devices, merged_scan(): arrived = lax.ppermute(window, CHIPS, pairs)  19 us
    ppermute x4, waiting for transfers between devices, ctx_scan(): arrived = lax.ppermute(window, CHIPS, pairs)  14.3 us
    all_to_all x1, starting transfers between devices, gather_columns(): mine = lax.all_to_all(spread, CHIPS, 0, 0, tiled=True)  12 us
    unnamed x22, local copies, waits for them, and re-layouts  4.09 us
    ppermute x3, starting transfers between devices, merged_scan(): arrived = lax.ppermute(window, CHIPS, pairs)  3.88 us
    dot_general x1, matrix products, local(): jnp.einsum('tqrk,qrjk->tj', full_rows.reshape(tok_rows, columns.shape[0],...  2.94 us
  transfers between devices with their start and end apart: 16, of which 9 were waited for; matrix products, arithmetic and copies ran while one was open for 8% of the time, Pallas kernels for 0%

profile of v11, /device:TPU:1, one launch (start us, length us, event | category | flops | bytes accessed | tf_op | source)
XLA Modules:
  0.0 137.3 jit_solution(7680403325589515261)
XLA Ops:
  7.2 0.0 all-gather.2.cloned.1.call-start
  7.2 1.8 %copy.39 = bf16[256,256]{0,1:T(8,128)(2,1)} copy(bf16[256,256]{1,0:T(8,128)(2,1)} %param.8) | data formatting | bytes 262144 | tf_op args[3]
  9.0 2.0 %broadcast_in_dim.29 = bf16[16,256,128]{2,1,0:T(8,128)(2,1)} broadcast(bf16[256,128]{1,0:T(8,128)(2,1)} %param.9), dimensions={1,2} | broadcast | bytes 1114112 | tf_op jit(solution)/shard_map/broadcast_in_dim | solution.py:88
  11.1 12.0 %all-to-all-start = ((bf16[16,256,128]{2,1,0:T(8,128)(2,1)}), bf16[16,256,128]{2,1,0:T(8,128)(2,1)S(1)}, u32[]{:S(2)}, u32[]{:S(2)}) async-start(bf16[16,256,128]{2,1,0:T(8,128)(2,1)} %broadcast_in_dim.29), calls=%async_computation | async-start | bytes 2097152 | tf_op jit(solution)/shard_map/all_to_all | solution.py:89
  23.1 0.1 copy.106
  23.2 0.2 fusion.13
  23.3 2.9 %collective-permute-start = (f32[2,128,128]{2,1,0:T(8,128)S(1)}, f32[2,128,128]{2,1,0:T(8,128)S(1)}, u32[]{:S(2)}, u32[]{:S(2)}) collective-permute-start(f32[2,128,128]{2,1,0:T(8,128)S(1)} %fusion.13), channel_id=1, source_target_pairs={{0,16},{16,0},{1,17},{17,1},{2,18},{18,2},{3,19},{19,3},{4,20},{20... | collective-permute-start | bytes 393224 | tf_op jit(solution)/shard_map/ppermute | solution.py:19
  26.2 1.0 collective-permute-done
  27.2 3.5 %collective-permute-start.1 = (f32[128,128]{1,0:T(8,128)S(1)}, f32[128,128]{1,0:T(8,128)S(1)}, u32[]{:S(2)}, u32[]{:S(2)}) collective-permute-start(f32[128,128]{1,0:T(8,128)S(1)} %add_bitcast_fusion), channel_id=1, source_target_pairs={{0,32},{32,64},{64,96},{96,128},{128,160},{160,192},{192,224},{224... | collective-permute-start | bytes 196616 | tf_op jit(solution)/shard_map/ppermute | solution.py:42
  30.8 11.7 %collective-permute-done.1 = f32[128,128]{1,0:T(8,128)S(1)} collective-permute-done((f32[128,128]{1,0:T(8,128)S(1)}, f32[128,128]{1,0:T(8,128)S(1)}, u32[]{:S(2)}, u32[]{:S(2)}) %collective-permute-start.1) | collective-permute-done | bytes 65568 | tf_op jit(solution)/shard_map/ppermute | solution.py:42
  42.5 9.3 %collective-permute-start.2 = (f32[128,128]{1,0:T(8,128)S(1)}, f32[128,128]{1,0:T(8,128)S(1)}, u32[]{:S(2)}, u32[]{:S(2)}) collective-permute-start(f32[128,128]{1,0:T(8,128)S(1)} %add.89), channel_id=1, source_target_pairs={{0,64},{32,96},{64,128},{96,160},{128,192},{160,224},{192,256},{22... | collective-permute-start | bytes 196616 | tf_op jit(solution)/shard_map/ppermute | solution.py:42
  51.8 1.3 collective-permute-done.2
  53.1 10.8 %collective-permute-start.3 = (f32[128,128]{1,0:T(8,128)S(1)}, f32[128,128]{1,0:T(8,128)S(1)}, u32[]{:S(2)}, u32[]{:S(2)}) collective-permute-start(f32[128,128]{1,0:T(8,128)S(1)} %add.91), channel_id=1, source_target_pairs={{0,128},{32,160},{64,192},{96,224},{128,256},{160,288},{192,320},{... | collective-permute-start | bytes 196616 | tf_op jit(solution)/shard_map/ppermute | solution.py:42
  64.0 1.3 collective-permute-done.3
  65.2 0.6 add.93
  65.9 4.6 %collective-permute-start.4 = (f32[128,128]{1,0:T(8,128)}, f32[128,128]{1,0:T(8,128)}, u32[]{:S(2)}, u32[]{:S(2)}) collective-permute-start(f32[128,128]{1,0:T(8,128)} %add.93), channel_id=1, source_target_pairs={{0,256},{32,288},{64,320},{96,352},{128,384},{160,416},{192,448},{... | collective-permute-start | bytes 196616 | tf_op jit(solution)/shard_map/ppermute | solution.py:42
  70.4 0.2 convolution_select_fusion.1
  70.7 8.1 %collective-permute-start.6 = (bf16[16,256,128]{2,1,0:T(8,128)(2,1)S(1)}, bf16[16,256,128]{2,1,0:T(8,128)(2,1)S(1)}, u32[]{:S(2)}, u32[]{:S(2)}) collective-permute-start(bf16[16,256,128]{2,1,0:T(8,128)(2,1)S(1)} %all-to-all-done), channel_id=1, source_target_pairs={{0,16},{16,0},{1,17},{17,1},{2,18},{18,2},{3,19},{19,3},{4,20},{20... | collective-permute-start | bytes 3145736 | tf_op jit(solution)/shard_map/ppermute | solution.py:19
  78.8 0.9 add_add_fusion.1
  79.7 2.8 %collective-permute-start.5 = (f32[128,128]{1,0:T(8,128)S(1)}, f32[128,128]{1,0:T(8,128)S(1)}, u32[]{:S(2)}, u32[]{:S(2)}) collective-permute-start(f32[128,128]{1,0:T(8,128)S(1)} %add_add_fusion.1), channel_id=1, source_target_pairs={{0,16},{16,0},{1,17},{17,1},{2,18},{18,2},{3,19},{19,3},{4,20},{20... | collective-permute-start | bytes 196616 | tf_op jit(solution)/shard_map/ppermute | solution.py:19
  82.5 1.2 convolution_bitcast_fusion.2
  83.7 1.3 multiply_reduce_fusion.1
  85.0 1.4 %select_bitcast_fusion.1 = (bf16[16,1,256,128]{3,2,1,0:T(8,128)(2,1)}, bf16[16,1,256,128]{3,2,1,0:T(8,128)(2,1)}) fusion(bf16[16,256,128]{2,1,0:T(8,128)(2,1)S(1)} %all-to-all-done, bf16[16,256,128]{2,1,0:T(8,128)(2,1)S(1)} %collective-permute-done.6, pred[]{:T(512)S(6)} %eq.4), kind=kLoop, calls=%fused_computation.20 | loop fusion | flops 1048576 | bytes 4194305 | tf_op jit(solution)/shard_map/stack | solution.py:94
  86.5 2.9 %fusion = f32[256,256,1,1]{1,0,3,2:T(8,128)S(1)} fusion(bf16[256,16,2,128]{0,3,2,1:T(8,128)(2,1)} %bitcast.144, bf16[16,1,256,128]{3,2,1,0:T(8,128)(2,1)} %get-tuple-element.12, bf16[16,1,256,128]{3,2,1,0:T(8,128)(2,1)} %get-tuple-element.11), kind=kOutput, calls=%fused_computation | convolution fusion | flops 537919488 | bytes 4456448 | tf_op jit(solution)/shard_map/tqrk,qrjk->tj/dot_general | solution.py:103
  89.5 0.1 multiply_reduce_fusion
  89.6 0.2 fusion.18
  89.8 1.3 collective-permute-start.7
  91.1 1.3 collective-permute-start.8
  92.4 2.0 %collective-permute-start.9 = (f32[2,128,128]{2,1,0:T(8,128)S(1)}, f32[2,128,128]{2,1,0:T(8,128)S(1)}, u32[]{:S(2)}, u32[]{:S(2)}) collective-permute-start(f32[2,128,128]{2,1,0:T(8,128)S(1)} %bitcast.140), channel_id=1, source_target_pairs={{0,16},{16,0},{1,17},{17,1},{2,18},{18,2},{3,19},{19,3},{4,20},{20... | collective-permute-start | bytes 393224 | tf_op jit(solution)/shard_map/ppermute | solution.py:19
  94.4 0.3 fusion.42
  94.8 1.6 %collective-permute-done.7 = f32[128,128]{1,0:T(8,128)S(1)} collective-permute-done((f32[128,128]{1,0:T(8,128)S(1)}, f32[128,128]{1,0:T(8,128)S(1)}, u32[]{:S(2)}, u32[]{:S(2)}) %collective-permute-start.7) | collective-permute-done | bytes 65568 | tf_op jit(solution)/shard_map/ppermute | solution.py:61
  96.4 2.2 %collective-permute-done.8 = f32[128,128]{1,0:T(8,128)S(1)} collective-permute-done((f32[128,128]{1,0:T(8,128)S(1)}, f32[128,128]{1,0:T(8,128)S(1)}, u32[]{:S(2)}, u32[]{:S(2)}) %collective-permute-start.8) | collective-permute-done | bytes 65568 | tf_op jit(solution)/shard_map/ppermute | solution.py:62
  98.7 1.3 collective-permute-start.10
  100.0 0.3 convolution_select_fusion
  100.3 5.8 %collective-permute-done.10 = f32[128,128]{1,0:T(8,128)S(1)} collective-permute-done((f32[128,128]{1,0:T(8,128)S(1)}, f32[128,128]{1,0:T(8,128)S(1)}, u32[]{:S(2)}, u32[]{:S(2)}) %collective-permute-start.10) | collective-permute-done | bytes 65568 | tf_op jit(solution)/shard_map/ppermute | solution.py:75
  106.1 1.3 collective-permute-start.11
  107.4 0.4 convolution_bitcast_fusion
  107.8 8.3 %collective-permute-done.11 = f32[128,128]{1,0:T(8,128)S(1)} collective-permute-done((f32[128,128]{1,0:T(8,128)S(1)}, f32[128,128]{1,0:T(8,128)S(1)}, u32[]{:S(2)}, u32[]{:S(2)}) %collective-permute-start.11) | collective-permute-done | bytes 65568 | tf_op jit(solution)/shard_map/ppermute | solution.py:75
  116.1 1.3 collective-permute-start.12
  117.4 0.4 convolution_bitcast_fusion.1
  117.9 4.8 %collective-permute-done.12 = f32[128,128]{1,0:T(8,128)S(1)} collective-permute-done((f32[128,128]{1,0:T(8,128)S(1)}, f32[128,128]{1,0:T(8,128)S(1)}, u32[]{:S(2)}, u32[]{:S(2)}) %collective-permute-start.12) | collective-permute-done | bytes 65568 | tf_op jit(solution)/shard_map/ppermute | solution.py:75
  122.7 4.5 %collective-permute-start.13 = (f32[128,128]{1,0:T(8,128)S(1)}, f32[128,128]{1,0:T(8,128)S(1)}, u32[]{:S(2)}, u32[]{:S(2)}) collective-permute-start(f32[128,128]{1,0:T(8,128)S(1)} %add_add_fusion), channel_id=1, source_target_pairs={{0,16},{16,0},{1,17},{17,1},{2,18},{18,2},{3,19},{19,3},{4,20},{20... | collective-permute-start | bytes 196616 | tf_op jit(solution)/shard_map/ppermute | solution.py:19
  127.3 0.3 fusion.7
  127.5 0.8 copy.53
  128.3 0.3 fusion.9
  128.6 0.8 copy.55
  129.4 0.3 fusion.8
  129.7 0.8 copy.54
  (40 shorter events, 0.3 us)
Async XLA Ops:
  7.2 63.3 %copy-start = (bf16[256,256]{1,0:T(8,128)(2,1)S(1)}, bf16[256,256]{1,0:T(8,128)(2,1)}, u32[]{:S(2)}) copy-start(bf16[256,256]{1,0:T(8,128)(2,1)} %param.5) | copy-start | bytes 393220
  7.2 15.9 %copy-start.2 = (bf16[256,256]{1,0:T(8,128)(2,1)S(1)}, bf16[256,256]{1,0:T(8,128)(2,1)}, u32[]{:S(2)}) copy-start(bf16[256,256]{1,0:T(8,128)(2,1)} %param.6) | copy-start | bytes 393220
  7.2 16.0 %copy-start.1 = (bf16[256,256]{1,0:T(8,128)(2,1)S(1)}, bf16[256,256]{1,0:T(8,128)(2,1)}, u32[]{:S(2)}) copy-start(bf16[256,256]{1,0:T(8,128)(2,1)} %param.7) | copy-start | bytes 393220
  7.2 79.3 %all-gather.2.cloned.1.call-start = ((), (), s32[]{:S(2)}) async-start(), calls=%async_computation.1 | async-start | bytes 2228224 | tf_op jit(solution)/shard_map/all_gather | solution.py:101
  11.1 59.6 %all-to-all-start = ((bf16[16,256,128]{2,1,0:T(8,128)(2,1)}), bf16[16,256,128]{2,1,0:T(8,128)(2,1)S(1)}, u32[]{:S(2)}, u32[]{:S(2)}) async-start(bf16[16,256,128]{2,1,0:T(8,128)(2,1)} %broadcast_in_dim.29), calls=%async_computation | async-start | bytes 2097152 | tf_op jit(solution)/shard_map/all_to_all | solution.py:89
  23.3 3.8 %collective-permute-start = (f32[2,128,128]{2,1,0:T(8,128)S(1)}, f32[2,128,128]{2,1,0:T(8,128)S(1)}, u32[]{:S(2)}, u32[]{:S(2)}) collective-permute-start(f32[2,128,128]{2,1,0:T(8,128)S(1)} %fusion.13), channel_id=1, source_target_pairs={{0,16},{16,0},{1,17},{17,1},{2,18},{18,2},{3,19},{19,3},{4,20},{20... | collective-permute-start | bytes 393224 | tf_op jit(solution)/shard_map/ppermute | solution.py:19
  27.2 15.3 %collective-permute-start.1 = (f32[128,128]{1,0:T(8,128)S(1)}, f32[128,128]{1,0:T(8,128)S(1)}, u32[]{:S(2)}, u32[]{:S(2)}) collective-permute-start(f32[128,128]{1,0:T(8,128)S(1)} %add_bitcast_fusion), channel_id=1, source_target_pairs={{0,32},{32,64},{64,96},{96,128},{128,160},{160,192},{192,224},{224... | collective-permute-start | bytes 196616 | tf_op jit(solution)/shard_map/ppermute | solution.py:42
  42.5 10.6 %collective-permute-start.2 = (f32[128,128]{1,0:T(8,128)S(1)}, f32[128,128]{1,0:T(8,128)S(1)}, u32[]{:S(2)}, u32[]{:S(2)}) collective-permute-start(f32[128,128]{1,0:T(8,128)S(1)} %add.89), channel_id=1, source_target_pairs={{0,64},{32,96},{64,128},{96,160},{128,192},{160,224},{192,256},{22... | collective-permute-start | bytes 196616 | tf_op jit(solution)/shard_map/ppermute | solution.py:42
  53.1 12.1 %collective-permute-start.3 = (f32[128,128]{1,0:T(8,128)S(1)}, f32[128,128]{1,0:T(8,128)S(1)}, u32[]{:S(2)}, u32[]{:S(2)}) collective-permute-start(f32[128,128]{1,0:T(8,128)S(1)} %add.91), channel_id=1, source_target_pairs={{0,128},{32,160},{64,192},{96,224},{128,256},{160,288},{192,320},{... | collective-permute-start | bytes 196616 | tf_op jit(solution)/shard_map/ppermute | solution.py:42
  63.9 6.7 %copy-start.7 = (pred[256,256]{1,0:T(8,128)(4,1)}, pred[256,256]{1,0:T(8,128)(4,1)S(1)}, u32[]{:S(2)}) copy-start(pred[256,256]{1,0:T(8,128)(4,1)S(1)} %iota_compare_fusion) | copy-start | bytes 196612
  65.9 12.9 %collective-permute-start.4 = (f32[128,128]{1,0:T(8,128)}, f32[128,128]{1,0:T(8,128)}, u32[]{:S(2)}, u32[]{:S(2)}) collective-permute-start(f32[128,128]{1,0:T(8,128)} %add.93), channel_id=1, source_target_pairs={{0,256},{32,288},{64,320},{96,352},{128,384},{160,416},{192,448},{... | collective-permute-start | bytes 196616 | tf_op jit(solution)/shard_map/ppermute | solution.py:42
  70.7 14.4 %collective-permute-start.6 = (bf16[16,256,128]{2,1,0:T(8,128)(2,1)S(1)}, bf16[16,256,128]{2,1,0:T(8,128)(2,1)S(1)}, u32[]{:S(2)}, u32[]{:S(2)}) collective-permute-start(bf16[16,256,128]{2,1,0:T(8,128)(2,1)S(1)} %all-to-all-done), channel_id=1, source_target_pairs={{0,16},{16,0},{1,17},{17,1},{2,18},{18,2},{3,19},{19,3},{4,20},{20... | collective-permute-start | bytes 3145736 | tf_op jit(solution)/shard_map/ppermute | solution.py:19
  79.7 3.9 %collective-permute-start.5 = (f32[128,128]{1,0:T(8,128)S(1)}, f32[128,128]{1,0:T(8,128)S(1)}, u32[]{:S(2)}, u32[]{:S(2)}) collective-permute-start(f32[128,128]{1,0:T(8,128)S(1)} %add_add_fusion.1), channel_id=1, source_target_pairs={{0,16},{16,0},{1,17},{17,1},{2,18},{18,2},{3,19},{19,3},{4,20},{20... | collective-permute-start | bytes 196616 | tf_op jit(solution)/shard_map/ppermute | solution.py:19
  83.6 1.4 copy-start.3
  83.6 1.4 %copy-start.5 = (f32[1,128,128]{2,1,0:T(8,128)}, f32[1,128,128]{2,1,0:T(8,128)S(1)}, u32[]{:S(2)}) copy-start(f32[1,128,128]{2,1,0:T(8,128)S(1)} %get-tuple-element.18) | copy-start | bytes 196612
  89.4 10.6 %copy-start.8 = (pred[256,256]{1,0:T(8,128)(4,1)S(1)}, pred[256,256]{1,0:T(8,128)(4,1)}, u32[]{:S(2)}) copy-start(pred[256,256]{1,0:T(8,128)(4,1)} %copy-done.7) | copy-start | bytes 196612
  89.8 6.6 %collective-permute-start.7 = (f32[128,128]{1,0:T(8,128)S(1)}, f32[128,128]{1,0:T(8,128)S(1)}, u32[]{:S(2)}, u32[]{:S(2)}) collective-permute-start(f32[128,128]{1,0:T(8,128)S(1)} %get-tuple-element.16), channel_id=1, source_target_pairs={{32,0},{64,32},{96,64},{128,96},{160,128},{192,160},{224,192},{256... | collective-permute-start | bytes 196616 | tf_op jit(solution)/shard_map/ppermute | solution.py:61
  91.1 7.6 %collective-permute-start.8 = (f32[128,128]{1,0:T(8,128)S(1)}, f32[128,128]{1,0:T(8,128)S(1)}, u32[]{:S(2)}, u32[]{:S(2)}) collective-permute-start(f32[128,128]{1,0:T(8,128)S(1)} %get-tuple-element.15), channel_id=1, source_target_pairs={{32,16},{48,0},{64,48},{80,32},{96,80},{112,64},{128,112},{144,96}... | collective-permute-start | bytes 196616 | tf_op jit(solution)/shard_map/ppermute | solution.py:62
  92.4 6.3 %collective-permute-start.9 = (f32[2,128,128]{2,1,0:T(8,128)S(1)}, f32[2,128,128]{2,1,0:T(8,128)S(1)}, u32[]{:S(2)}, u32[]{:S(2)}) collective-permute-start(f32[2,128,128]{2,1,0:T(8,128)S(1)} %bitcast.140), channel_id=1, source_target_pairs={{0,16},{16,0},{1,17},{17,1},{2,18},{18,2},{3,19},{19,3},{4,20},{20... | collective-permute-start | bytes 393224 | tf_op jit(solution)/shard_map/ppermute | solution.py:19
  94.8 32.5 %copy-start.4 = (f32[1,128,128]{2,1,0:T(8,128)S(1)}, f32[1,128,128]{2,1,0:T(8,128)}, u32[]{:S(2)}) copy-start(f32[1,128,128]{2,1,0:T(8,128)} %copy-done.3) | copy-start | bytes 196612
  94.8 32.5 %copy-start.6 = (f32[1,128,128]{2,1,0:T(8,128)S(1)}, f32[1,128,128]{2,1,0:T(8,128)}, u32[]{:S(2)}) copy-start(f32[1,128,128]{2,1,0:T(8,128)} %copy-done.5) | copy-start | bytes 196612
  98.7 7.4 %collective-permute-start.10 = (f32[128,128]{1,0:T(8,128)S(1)}, f32[128,128]{1,0:T(8,128)S(1)}, u32[]{:S(2)}, u32[]{:S(2)}) collective-permute-start(f32[128,128]{1,0:T(8,128)S(1)} %get-tuple-element.9), channel_id=1, source_target_pairs={{64,0},{96,32},{128,64},{160,96},{192,128},{224,160},{256,192},{28... | collective-permute-start | bytes 196616 | tf_op jit(solution)/shard_map/ppermute | solution.py:75
  106.1 10.0 %collective-permute-start.11 = (f32[128,128]{1,0:T(8,128)S(1)}, f32[128,128]{1,0:T(8,128)S(1)}, u32[]{:S(2)}, u32[]{:S(2)}) collective-permute-start(f32[128,128]{1,0:T(8,128)S(1)} %add.105), channel_id=1, source_target_pairs={{128,0},{160,32},{192,64},{224,96},{256,128},{288,160},{320,192},{... | collective-permute-start | bytes 196616 | tf_op jit(solution)/shard_map/ppermute | solution.py:75
  116.1 6.6 %collective-permute-start.12 = (f32[128,128]{1,0:T(8,128)S(1)}, f32[128,128]{1,0:T(8,128)S(1)}, u32[]{:S(2)}, u32[]{:S(2)}) collective-permute-start(f32[128,128]{1,0:T(8,128)S(1)} %add.107), channel_id=1, source_target_pairs={{256,0},{288,32},{320,64},{352,96},{384,128},{416,160},{448,192},{... | collective-permute-start | bytes 196616 | tf_op jit(solution)/shard_map/ppermute | solution.py:75
  122.7 5.6 %collective-permute-start.13 = (f32[128,128]{1,0:T(8,128)S(1)}, f32[128,128]{1,0:T(8,128)S(1)}, u32[]{:S(2)}, u32[]{:S(2)}) collective-permute-start(f32[128,128]{1,0:T(8,128)S(1)} %add_add_fusion), channel_id=1, source_target_pairs={{0,16},{16,0},{1,17},{17,1},{2,18},{18,2},{3,19},{19,3},{4,20},{20... | collective-permute-start | bytes 196616 | tf_op jit(solution)/shard_map/ppermute | solution.py:19
Sparse Core Ops, SparseCore 0:
  11.6 69.3 all-gather.1

commit v12 on v2

--- a/solution.py
+++ b/solution.py
@@ -1,6 +1,7 @@
 import jax
 import jax.numpy as jnp
 from jax import lax
+from jax.experimental.layout import Layout, with_layout_constraint
 from jax.sharding import Mesh
 from jax.sharding import PartitionSpec as P
 
@@ -113,10 +114,10 @@
     grad_key = grad_key + jnp.einsum("she,hde->shd", value_wide, adjoint, precision=highest)
     grad_value = jnp.einsum("hts,the->she", weights, grad_wide, precision=highest)
     grad_value = grad_value + jnp.einsum("shd,hde->she", key_wide, adjoint, precision=highest)
-    return (
-        grad_query.reshape(tok_rows, feat_width).astype(jnp.bfloat16),
-        grad_key.reshape(tok_rows, feat_width).astype(jnp.bfloat16),
-        grad_value.reshape(tok_rows, feat_width).astype(jnp.bfloat16),
+    row_major = Layout(major_to_minor=(0, 1))
+    return tuple(
+        with_layout_constraint(out.reshape(tok_rows, feat_width), row_major).astype(jnp.bfloat16)
+        for out in (grad_query, grad_key, grad_value)
     )
 
 

time: 139 us -> 136 us (0.978)
  other arithmetic: 3.19 us -> 1.72 us
    unnamed x22 -> x23, local copies, waits for them, and re-layouts: 4.09 us -> 1.82 us
  transfers between devices with their start and end apart: 15 -> 15, of which waited for: 9 -> 10; matrix products, arithmetic and copies ran while one was open for 8% -> 6% of each run, Pallas kernels for 0% -> 0%
where the time goes in v12:
time: 136 us; the launch traced here: 135 us
  starting transfers between devices  68.5 us (50%)
  waiting for transfers between devices  36.7 us (27%)
  between operations  14.5 us (11%)
  matrix products  8.18 us (6%)
  local copies, waits for them, and re-layouts  5.27 us (4%)
  other arithmetic  1.72 us (1%)
    ppermute x8, waiting for transfers between devices, ctx_scan(): arrived = lax.ppermute(window, CHIPS, pairs)  34 us
    ppermute x8, starting transfers between devices, ctx_scan(): arrived = lax.ppermute(window, CHIPS, pairs)  32.9 us
    ppermute x5, starting transfers between devices, swap_cores(): return lax.ppermute(value, 'core', [(0, 1), (1, 0)])  23.6 us
    all_to_all x1, starting transfers between devices, gather_columns(): mine = lax.all_to_all(spread, CHIPS, 0, 0, tiled=True)  12 us
    dot_general x1, matrix products, local(): jnp.einsum('tqrk,qrjk->tj', full_rows.reshape(tok_rows, columns.shape[0],...  2.94 us
  transfers between devices with their start and end apart: 15, of which 10 were waited for; matrix products, arithmetic and copies ran while one was open for 6% of the time, Pallas kernels for 0%

profile of v12, /device:TPU:1, one launch (start us, length us, event | category | flops | bytes accessed | tf_op | source)
XLA Modules:
  0.0 134.8 jit_solution(11939104616418007108)
XLA Ops:
  7.2 0.0 copy-start
  7.2 0.0 all-gather.2.cloned.1.call-start
  7.2 1.8 %copy.39 = bf16[256,256]{0,1:T(8,128)(2,1)} copy(bf16[256,256]{1,0:T(8,128)(2,1)} %param.8) | data formatting | bytes 262144 | tf_op args[3]
  9.0 0.0 all-gather.2.cloned.1.call-update
  9.0 2.0 %broadcast_in_dim.29 = bf16[16,256,128]{2,1,0:T(8,128)(2,1)} broadcast(bf16[256,128]{1,0:T(8,128)(2,1)} %param.9), dimensions={1,2} | broadcast | bytes 1114112 | tf_op jit(solution)/shard_map/broadcast_in_dim | solution.py:56
  11.1 12.0 %all-to-all-start = ((bf16[16,256,128]{2,1,0:T(8,128)(2,1)}), bf16[16,256,128]{2,1,0:T(8,128)(2,1)S(1)}, u32[]{:S(2)}, u32[]{:S(2)}) async-start(bf16[16,256,128]{2,1,0:T(8,128)(2,1)} %broadcast_in_dim.29), calls=%async_computation | async-start | bytes 2097152 | tf_op jit(solution)/shard_map/all_to_all | solution.py:57
  23.1 0.2 fusion.13
  23.3 2.9 %collective-permute-start = (f32[2,128,128]{2,1,0:T(8,128)S(1)}, f32[2,128,128]{2,1,0:T(8,128)S(1)}, u32[]{:S(2)}, u32[]{:S(2)}) collective-permute-start(f32[2,128,128]{2,1,0:T(8,128)S(1)} %fusion.13), channel_id=1, source_target_pairs={{0,16},{16,0},{1,17},{17,1},{2,18},{18,2},{3,19},{19,3},{4,20},{20... | collective-permute-start | bytes 393224 | tf_op jit(solution)/shard_map/ppermute | solution.py:20
  26.2 1.0 collective-permute-done
  27.1 3.5 %collective-permute-start.1 = (f32[128,128]{1,0:T(8,128)S(1)}, f32[128,128]{1,0:T(8,128)S(1)}, u32[]{:S(2)}, u32[]{:S(2)}) collective-permute-start(f32[128,128]{1,0:T(8,128)S(1)} %add_bitcast_fusion.1), channel_id=1, source_target_pairs={{0,32},{32,64},{64,96},{96,128},{128,160},{160,192},{192,224},{224... | collective-permute-start | bytes 196616 | tf_op jit(solution)/shard_map/ppermute | solution.py:43
  30.7 11.8 %collective-permute-done.1 = f32[128,128]{1,0:T(8,128)S(1)} collective-permute-done((f32[128,128]{1,0:T(8,128)S(1)}, f32[128,128]{1,0:T(8,128)S(1)}, u32[]{:S(2)}, u32[]{:S(2)}) %collective-permute-start.1) | collective-permute-done | bytes 65568 | tf_op jit(solution)/shard_map/ppermute | solution.py:43
  42.5 9.3 %collective-permute-start.2 = (f32[128,128]{1,0:T(8,128)S(1)}, f32[128,128]{1,0:T(8,128)S(1)}, u32[]{:S(2)}, u32[]{:S(2)}) collective-permute-start(f32[128,128]{1,0:T(8,128)S(1)} %add.81), channel_id=1, source_target_pairs={{0,64},{32,96},{64,128},{96,160},{128,192},{160,224},{192,256},{22... | collective-permute-start | bytes 196616 | tf_op jit(solution)/shard_map/ppermute | solution.py:43
  51.8 1.3 collective-permute-done.2
  53.1 10.8 %collective-permute-start.3 = (f32[128,128]{1,0:T(8,128)S(1)}, f32[128,128]{1,0:T(8,128)S(1)}, u32[]{:S(2)}, u32[]{:S(2)}) collective-permute-start(f32[128,128]{1,0:T(8,128)S(1)} %add.83), channel_id=1, source_target_pairs={{0,128},{32,160},{64,192},{96,224},{128,256},{160,288},{192,320},{... | collective-permute-start | bytes 196616 | tf_op jit(solution)/shard_map/ppermute | solution.py:43
  63.9 0.0 copy-start.9
  64.0 1.3 collective-permute-done.3
  65.2 4.0 %collective-permute-start.4 = (f32[128,128]{1,0:T(8,128)S(1)}, f32[128,128]{1,0:T(8,128)S(1)}, u32[]{:S(2)}, u32[]{:S(2)}) collective-permute-start(f32[128,128]{1,0:T(8,128)S(1)} %add.85), channel_id=1, source_target_pairs={{0,256},{32,288},{64,320},{96,352},{128,384},{160,416},{192,448},{... | collective-permute-start | bytes 196616 | tf_op jit(solution)/shard_map/ppermute | solution.py:43
  69.2 0.2 convolution_select_fusion.1
  69.5 8.1 %collective-permute-start.6 = (bf16[16,256,128]{2,1,0:T(8,128)(2,1)S(1)}, bf16[16,256,128]{2,1,0:T(8,128)(2,1)S(1)}, u32[]{:S(2)}, u32[]{:S(2)}) collective-permute-start(bf16[16,256,128]{2,1,0:T(8,128)(2,1)S(1)} %all-to-all-done), channel_id=1, source_target_pairs={{0,16},{16,0},{1,17},{17,1},{2,18},{18,2},{3,19},{19,3},{4,20},{20... | collective-permute-start | bytes 3145736 | tf_op jit(solution)/shard_map/ppermute | solution.py:20
  77.6 3.9 %collective-permute-start.5 = (f32[128,128]{1,0:T(8,128)S(1)}, f32[128,128]{1,0:T(8,128)S(1)}, u32[]{:S(2)}, u32[]{:S(2)}) collective-permute-start(f32[128,128]{1,0:T(8,128)S(1)} %add_add_fusion.1), channel_id=1, source_target_pairs={{0,16},{16,0},{1,17},{17,1},{2,18},{18,2},{3,19},{19,3},{4,20},{20... | collective-permute-start | bytes 196616 | tf_op jit(solution)/shard_map/ppermute | solution.py:20
  81.5 0.4 convolution_bitcast_fusion.2
  82.0 0.4 collective-permute-done.5
  82.4 1.3 multiply_reduce_fusion.1
  83.8 1.4 %select_bitcast_fusion.1 = (bf16[16,1,256,128]{3,2,1,0:T(8,128)(2,1)}, bf16[16,1,256,128]{3,2,1,0:T(8,128)(2,1)}) fusion(bf16[16,256,128]{2,1,0:T(8,128)(2,1)S(1)} %all-to-all-done, bf16[16,256,128]{2,1,0:T(8,128)(2,1)S(1)} %collective-permute-done.6, pred[]{:T(512)S(6)} %eq.4), kind=kLoop, calls=%fused_computation.21 | loop fusion | flops 1048576 | bytes 4194305 | tf_op jit(solution)/shard_map/stack | solution.py:62
  85.2 2.9 %fusion = f32[256,256,1,1]{1,0,3,2:T(8,128)S(1)} fusion(bf16[256,16,2,128]{0,3,2,1:T(8,128)(2,1)} %bitcast.144, bf16[16,1,256,128]{3,2,1,0:T(8,128)(2,1)} %get-tuple-element.4, bf16[16,1,256,128]{3,2,1,0:T(8,128)(2,1)} %get-tuple-element.3), kind=kOutput, calls=%fused_computation | convolution fusion | flops 537919488 | bytes 4456448 | tf_op jit(solution)/shard_map/tqrk,qrjk->tj/dot_general | solution.py:71
  88.2 0.0 copy-start.10
  88.2 0.1 multiply_reduce_fusion
  88.3 0.2 convolution_bitcast_fusion.6
  88.5 1.9 %collective-permute-start.7 = (f32[2,128,128]{2,1,0:T(8,128)S(1)}, f32[2,128,128]{2,1,0:T(8,128)S(1)}, u32[]{:S(2)}, u32[]{:S(2)}) collective-permute-start(f32[2,128,128]{2,1,0:T(8,128)S(1)} %convolution_bitcast_fusion.6), channel_id=1, source_target_pairs={{0,16},{16,0},{1,17},{17,1},{2,18},{18,2},{3,19},{19,3},{4,20},{20... | collective-permute-start | bytes 393224 | tf_op jit(solution)/shard_map/ppermute | solution.py:20
  90.4 1.3 collective-permute-done.7
  91.8 1.4 %collective-permute-start.8 = (f32[128,128]{1,0:T(8,128)S(1)}, f32[128,128]{1,0:T(8,128)S(1)}, u32[]{:S(2)}, u32[]{:S(2)}) collective-permute-start(f32[128,128]{1,0:T(8,128)S(1)} %add_bitcast_fusion), channel_id=1, source_target_pairs={{32,0},{64,32},{96,64},{128,96},{160,128},{192,160},{224,192},{256... | collective-permute-start | bytes 196616 | tf_op jit(solution)/shard_map/ppermute | solution.py:43
  93.2 0.7 fusion.44
  93.9 4.1 %collective-permute-done.8 = f32[128,128]{1,0:T(8,128)S(1)} collective-permute-done((f32[128,128]{1,0:T(8,128)S(1)}, f32[128,128]{1,0:T(8,128)S(1)}, u32[]{:S(2)}, u32[]{:S(2)}) %collective-permute-start.8) | collective-permute-done | bytes 65568 | tf_op jit(solution)/shard_map/ppermute | solution.py:43
  98.0 1.3 collective-permute-start.9
  99.3 0.3 convolution_select_fusion
  99.6 4.5 %collective-permute-done.9 = f32[128,128]{1,0:T(8,128)S(1)} collective-permute-done((f32[128,128]{1,0:T(8,128)S(1)}, f32[128,128]{1,0:T(8,128)S(1)}, u32[]{:S(2)}, u32[]{:S(2)}) %collective-permute-start.9) | collective-permute-done | bytes 65568 | tf_op jit(solution)/shard_map/ppermute | solution.py:43
  104.1 1.3 collective-permute-start.10
  105.4 0.7 convolution_bitcast_fusion
  106.1 7.0 %collective-permute-done.10 = f32[128,128]{1,0:T(8,128)S(1)} collective-permute-done((f32[128,128]{1,0:T(8,128)S(1)}, f32[128,128]{1,0:T(8,128)S(1)}, u32[]{:S(2)}, u32[]{:S(2)}) %collective-permute-start.10) | collective-permute-done | bytes 65568 | tf_op jit(solution)/shard_map/ppermute | solution.py:43
  113.1 1.3 collective-permute-start.11
  114.4 0.4 convolution_bitcast_fusion.1
  114.7 4.0 %collective-permute-done.11 = f32[128,128]{1,0:T(8,128)S(1)} collective-permute-done((f32[128,128]{1,0:T(8,128)S(1)}, f32[128,128]{1,0:T(8,128)S(1)}, u32[]{:S(2)}, u32[]{:S(2)}) %collective-permute-start.11) | collective-permute-done | bytes 65568 | tf_op jit(solution)/shard_map/ppermute | solution.py:43
  118.8 6.8 %collective-permute-start.12 = (f32[128,128]{1,0:T(8,128)S(1)}, f32[128,128]{1,0:T(8,128)S(1)}, u32[]{:S(2)}, u32[]{:S(2)}) collective-permute-start(f32[128,128]{1,0:T(8,128)S(1)} %add_add_fusion), channel_id=1, source_target_pairs={{0,16},{16,0},{1,17},{17,1},{2,18},{18,2},{3,19},{19,3},{4,20},{20... | collective-permute-start | bytes 196616 | tf_op jit(solution)/shard_map/ppermute | solution.py:20
  125.6 0.3 fusion.8
  126.0 0.7 copy.124
  126.7 0.3 fusion.6
  126.9 0.3 fusion.4
  127.2 0.7 bitcast_convert_fusion
  (40 shorter events, 0.3 us)
Async XLA Ops:
  7.2 62.1 %copy-start = (bf16[256,256]{1,0:T(8,128)(2,1)S(1)}, bf16[256,256]{1,0:T(8,128)(2,1)}, u32[]{:S(2)}) copy-start(bf16[256,256]{1,0:T(8,128)(2,1)} %param.5) | copy-start | bytes 393220
  7.2 15.9 %copy-start.2 = (bf16[256,256]{1,0:T(8,128)(2,1)S(1)}, bf16[256,256]{1,0:T(8,128)(2,1)}, u32[]{:S(2)}) copy-start(bf16[256,256]{1,0:T(8,128)(2,1)} %param.6) | copy-start | bytes 393220
  7.2 15.9 %copy-start.1 = (bf16[256,256]{1,0:T(8,128)(2,1)S(1)}, bf16[256,256]{1,0:T(8,128)(2,1)}, u32[]{:S(2)}) copy-start(bf16[256,256]{1,0:T(8,128)(2,1)} %param.7) | copy-start | bytes 393220
  7.2 78.0 %all-gather.2.cloned.1.call-start = ((), (), s32[]{:S(2)}) async-start(), calls=%async_computation.1 | async-start | bytes 2228224 | tf_op jit(solution)/shard_map/all_gather | solution.py:69
  11.1 58.4 %all-to-all-start = ((bf16[16,256,128]{2,1,0:T(8,128)(2,1)}), bf16[16,256,128]{2,1,0:T(8,128)(2,1)S(1)}, u32[]{:S(2)}, u32[]{:S(2)}) async-start(bf16[16,256,128]{2,1,0:T(8,128)(2,1)} %broadcast_in_dim.29), calls=%async_computation | async-start | bytes 2097152 | tf_op jit(solution)/shard_map/all_to_all | solution.py:57
  23.3 3.8 %collective-permute-start = (f32[2,128,128]{2,1,0:T(8,128)S(1)}, f32[2,128,128]{2,1,0:T(8,128)S(1)}, u32[]{:S(2)}, u32[]{:S(2)}) collective-permute-start(f32[2,128,128]{2,1,0:T(8,128)S(1)} %fusion.13), channel_id=1, source_target_pairs={{0,16},{16,0},{1,17},{17,1},{2,18},{18,2},{3,19},{19,3},{4,20},{20... | collective-permute-start | bytes 393224 | tf_op jit(solution)/shard_map/ppermute | solution.py:20
  27.1 38.1 %copy-start.3 = (f32[2,128,128]{2,1,0:T(8,128)}, f32[2,128,128]{2,1,0:T(8,128)S(1)}, u32[]{:S(2)}) copy-start(f32[2,128,128]{2,1,0:T(8,128)S(1)} %collective-permute-done) | copy-start | bytes 393220
  27.1 15.3 %collective-permute-start.1 = (f32[128,128]{1,0:T(8,128)S(1)}, f32[128,128]{1,0:T(8,128)S(1)}, u32[]{:S(2)}, u32[]{:S(2)}) collective-permute-start(f32[128,128]{1,0:T(8,128)S(1)} %add_bitcast_fusion.1), channel_id=1, source_target_pairs={{0,32},{32,64},{64,96},{96,128},{128,160},{160,192},{192,224},{224... | collective-permute-start | bytes 196616 | tf_op jit(solution)/shard_map/ppermute | solution.py:43
  42.5 10.6 %collective-permute-start.2 = (f32[128,128]{1,0:T(8,128)S(1)}, f32[128,128]{1,0:T(8,128)S(1)}, u32[]{:S(2)}, u32[]{:S(2)}) collective-permute-start(f32[128,128]{1,0:T(8,128)S(1)} %add.81), channel_id=1, source_target_pairs={{0,64},{32,96},{64,128},{96,160},{128,192},{160,224},{192,256},{22... | collective-permute-start | bytes 196616 | tf_op jit(solution)/shard_map/ppermute | solution.py:43
  53.1 12.1 %collective-permute-start.3 = (f32[128,128]{1,0:T(8,128)S(1)}, f32[128,128]{1,0:T(8,128)S(1)}, u32[]{:S(2)}, u32[]{:S(2)}) collective-permute-start(f32[128,128]{1,0:T(8,128)S(1)} %add.83), channel_id=1, source_target_pairs={{0,128},{32,160},{64,192},{96,224},{128,256},{160,288},{192,320},{... | collective-permute-start | bytes 196616 | tf_op jit(solution)/shard_map/ppermute | solution.py:43
  63.9 5.3 %copy-start.9 = (pred[256,256]{1,0:T(8,128)(4,1)}, pred[256,256]{1,0:T(8,128)(4,1)S(1)}, u32[]{:S(2)}) copy-start(pred[256,256]{1,0:T(8,128)(4,1)S(1)} %iota_compare_fusion) | copy-start | bytes 196612
  65.2 12.3 %collective-permute-start.4 = (f32[128,128]{1,0:T(8,128)S(1)}, f32[128,128]{1,0:T(8,128)S(1)}, u32[]{:S(2)}, u32[]{:S(2)}) collective-permute-start(f32[128,128]{1,0:T(8,128)S(1)} %add.85), channel_id=1, source_target_pairs={{0,256},{32,288},{64,320},{96,352},{128,384},{160,416},{192,448},{... | collective-permute-start | bytes 196616 | tf_op jit(solution)/shard_map/ppermute | solution.py:43
  69.5 14.3 %collective-permute-start.6 = (bf16[16,256,128]{2,1,0:T(8,128)(2,1)S(1)}, bf16[16,256,128]{2,1,0:T(8,128)(2,1)S(1)}, u32[]{:S(2)}, u32[]{:S(2)}) collective-permute-start(bf16[16,256,128]{2,1,0:T(8,128)(2,1)S(1)} %all-to-all-done), channel_id=1, source_target_pairs={{0,16},{16,0},{1,17},{17,1},{2,18},{18,2},{3,19},{19,3},{4,20},{20... | collective-permute-start | bytes 3145736 | tf_op jit(solution)/shard_map/ppermute | solution.py:20
  77.6 4.8 %collective-permute-start.5 = (f32[128,128]{1,0:T(8,128)S(1)}, f32[128,128]{1,0:T(8,128)S(1)}, u32[]{:S(2)}, u32[]{:S(2)}) collective-permute-start(f32[128,128]{1,0:T(8,128)S(1)} %add_add_fusion.1), channel_id=1, source_target_pairs={{0,16},{16,0},{1,17},{17,1},{2,18},{18,2},{3,19},{19,3},{4,20},{20... | collective-permute-start | bytes 196616 | tf_op jit(solution)/shard_map/ppermute | solution.py:20
  82.4 1.3 copy-start.5
  82.4 1.3 copy-start.7
  88.2 11.2 %copy-start.10 = (pred[256,256]{1,0:T(8,128)(4,1)S(1)}, pred[256,256]{1,0:T(8,128)(4,1)}, u32[]{:S(2)}) copy-start(pred[256,256]{1,0:T(8,128)(4,1)} %copy-done.9) | copy-start | bytes 196612
  88.5 3.2 %collective-permute-start.7 = (f32[2,128,128]{2,1,0:T(8,128)S(1)}, f32[2,128,128]{2,1,0:T(8,128)S(1)}, u32[]{:S(2)}, u32[]{:S(2)}) collective-permute-start(f32[2,128,128]{2,1,0:T(8,128)S(1)} %convolution_bitcast_fusion.6), channel_id=1, source_target_pairs={{0,16},{16,0},{1,17},{17,1},{2,18},{18,2},{3,19},{19,3},{4,20},{20... | collective-permute-start | bytes 393224 | tf_op jit(solution)/shard_map/ppermute | solution.py:20
  91.8 33.8 %copy-start.4 = (f32[2,128,128]{2,1,0:T(8,128)S(1)}, f32[2,128,128]{2,1,0:T(8,128)}, u32[]{:S(2)}) copy-start(f32[2,128,128]{2,1,0:T(8,128)} %copy-done.3) | copy-start | bytes 393220
  91.8 33.8 %copy-start.6 = (f32[1,128,128]{2,1,0:T(8,128)S(1)}, f32[1,128,128]{2,1,0:T(8,128)}, u32[]{:S(2)}) copy-start(f32[1,128,128]{2,1,0:T(8,128)} %copy-done.5) | copy-start | bytes 196612
  91.8 33.8 %copy-start.8 = (f32[1,128,128]{2,1,0:T(8,128)S(1)}, f32[1,128,128]{2,1,0:T(8,128)}, u32[]{:S(2)}) copy-start(f32[1,128,128]{2,1,0:T(8,128)} %copy-done.7) | copy-start | bytes 196612
  91.8 6.2 %collective-permute-start.8 = (f32[128,128]{1,0:T(8,128)S(1)}, f32[128,128]{1,0:T(8,128)S(1)}, u32[]{:S(2)}, u32[]{:S(2)}) collective-permute-start(f32[128,128]{1,0:T(8,128)S(1)} %add_bitcast_fusion), channel_id=1, source_target_pairs={{32,0},{64,32},{96,64},{128,96},{160,128},{192,160},{224,192},{256... | collective-permute-start | bytes 196616 | tf_op jit(solution)/shard_map/ppermute | solution.py:43
  98.0 6.1 %collective-permute-start.9 = (f32[128,128]{1,0:T(8,128)S(1)}, f32[128,128]{1,0:T(8,128)S(1)}, u32[]{:S(2)}, u32[]{:S(2)}) collective-permute-start(f32[128,128]{1,0:T(8,128)S(1)} %add.93), channel_id=1, source_target_pairs={{64,0},{96,32},{128,64},{160,96},{192,128},{224,160},{256,192},{28... | collective-permute-start | bytes 196616 | tf_op jit(solution)/shard_map/ppermute | solution.py:43
  104.1 8.9 %collective-permute-start.10 = (f32[128,128]{1,0:T(8,128)S(1)}, f32[128,128]{1,0:T(8,128)S(1)}, u32[]{:S(2)}, u32[]{:S(2)}) collective-permute-start(f32[128,128]{1,0:T(8,128)S(1)} %add.95), channel_id=1, source_target_pairs={{128,0},{160,32},{192,64},{224,96},{256,128},{288,160},{320,192},{... | collective-permute-start | bytes 196616 | tf_op jit(solution)/shard_map/ppermute | solution.py:43
  113.1 5.7 %collective-permute-start.11 = (f32[128,128]{1,0:T(8,128)S(1)}, f32[128,128]{1,0:T(8,128)S(1)}, u32[]{:S(2)}, u32[]{:S(2)}) collective-permute-start(f32[128,128]{1,0:T(8,128)S(1)} %add.97), channel_id=1, source_target_pairs={{256,0},{288,32},{320,64},{352,96},{384,128},{416,160},{448,192},{... | collective-permute-start | bytes 196616 | tf_op jit(solution)/shard_map/ppermute | solution.py:43
  118.8 7.9 %collective-permute-start.12 = (f32[128,128]{1,0:T(8,128)S(1)}, f32[128,128]{1,0:T(8,128)S(1)}, u32[]{:S(2)}, u32[]{:S(2)}) collective-permute-start(f32[128,128]{1,0:T(8,128)S(1)} %add_add_fusion), channel_id=1, source_target_pairs={{0,16},{16,0},{1,17},{17,1},{2,18},{18,2},{3,19},{19,3},{4,20},{20... | collective-permute-start | bytes 196616 | tf_op jit(solution)/shard_map/ppermute | solution.py:20
Sparse Core Ops, SparseCore 0:
  11.6 69.5 all-gather.1

commit v13 on v12

--- a/solution.py
+++ b/solution.py
@@ -66,11 +66,11 @@
     tok_rows = query.shape[0]
     feat_width = query.shape[1]
     head_count = feat_width // E
-    full_rows = lax.all_gather(grad_out, TP, axis=1, tiled=True)
+    full_rows = lax.all_gather(grad_out, TP, axis=0)
     columns = gather_columns(w_out)
     grad_z = jnp.einsum(
-        "tqrk,qrjk->tj",
-        full_rows.reshape(tok_rows, columns.shape[0], 2, columns.shape[3]),
+        "qtrk,qrjk->tj",
+        full_rows.reshape(columns.shape[0], tok_rows, 2, columns.shape[3]),
         columns,
         preferred_element_type=jnp.float32,
     )

time: 136 us -> 141 us (1.037)
  local copies, waits for them, and re-layouts: 5.27 us -> 7.63 us
  other arithmetic: 1.72 us -> 3.27 us
    reshape x0 -> x1, local copies, waits for them, and re-layouts: none -> 4.13 us  [local(): full_rows.reshape(columns.shape[0], tok_rows, 2, columns.shape[3])]
    unnamed x23 -> x26, local copies, waits for them, and re-layouts: 1.82 us -> 0.07 us
  transfers between devices with their start and end apart: 15 -> 15, of which waited for: 10 -> 10; matrix products, arithmetic and copies ran while one was open for 6% -> 7% of each run, Pallas kernels for 0% -> 0%
where the time goes in v13:
time: 141 us; the launch traced here: 139 us
  starting transfers between devices  68.2 us (48%)
  waiting for transfers between devices  37.9 us (27%)
  between operations  14.5 us (10%)
  local copies, waits for them, and re-layouts  7.63 us (5%)
  matrix products  7.57 us (5%)
  other arithmetic  3.27 us (2%)
    ppermute x8, waiting for transfers between devices, ctx_scan(): arrived = lax.ppermute(window, CHIPS, pairs)  34.3 us
    ppermute x8, starting transfers between devices, ctx_scan(): arrived = lax.ppermute(window, CHIPS, pairs)  32.4 us
    ppermute x5, starting transfers between devices, swap_cores(): return lax.ppermute(value, 'core', [(0, 1), (1, 0)])  23.9 us
    all_to_all x1, starting transfers between devices, gather_columns(): mine = lax.all_to_all(spread, CHIPS, 0, 0, tiled=True)  12 us
    reshape x1, local copies, waits for them, and re-layouts, local(): full_rows.reshape(columns.shape[0], tok_rows, 2, columns.shape[3])  4.13 us
    ppermute x5, waiting for transfers between devices, swap_cores(): return lax.ppermute(value, 'core', [(0, 1), (1, 0)])  2.91 us
  transfers between devices with their start and end apart: 15, of which 10 were waited for; matrix products, arithmetic and copies ran while one was open for 7% of the time, Pallas kernels for 0%

profile of v13, /device:TPU:1, one launch (start us, length us, event | category | flops | bytes accessed | tf_op | source)
XLA Modules:
  0.0 139.1 jit_solution(1443163871407045562)
XLA Ops:
  7.2 0.0 all-gather.3.cloned.1.call-start
  7.2 0.7 all-gather.3.cloned.1.call-update
  7.9 2.0 %broadcast_in_dim.29 = bf16[16,256,128]{2,1,0:T(8,128)(2,1)} broadcast(bf16[256,128]{1,0:T(8,128)(2,1)} %param.9), dimensions={1,2} | broadcast | bytes 1114112 | tf_op jit(solution)/shard_map/broadcast_in_dim | solution.py:56
  10.0 12.0 %all-to-all-start = ((bf16[16,256,128]{2,1,0:T(8,128)(2,1)}), bf16[16,256,128]{2,1,0:T(8,128)(2,1)S(1)}, u32[]{:S(2)}, u32[]{:S(2)}) async-start(bf16[16,256,128]{2,1,0:T(8,128)(2,1)} %broadcast_in_dim.29), calls=%async_computation | async-start | bytes 2097152 | tf_op jit(solution)/shard_map/all_to_all | solution.py:57
  22.0 0.2 fusion.14
  22.2 2.9 %collective-permute-start = (f32[2,128,128]{2,1,0:T(8,128)S(1)}, f32[2,128,128]{2,1,0:T(8,128)S(1)}, u32[]{:S(2)}, u32[]{:S(2)}) collective-permute-start(f32[2,128,128]{2,1,0:T(8,128)S(1)} %fusion.14), channel_id=1, source_target_pairs={{0,16},{16,0},{1,17},{17,1},{2,18},{18,2},{3,19},{19,3},{4,20},{20... | collective-permute-start | bytes 393224 | tf_op jit(solution)/shard_map/ppermute | solution.py:20
  25.1 1.0 collective-permute-done
  26.0 3.5 %collective-permute-start.1 = (f32[128,128]{1,0:T(8,128)S(1)}, f32[128,128]{1,0:T(8,128)S(1)}, u32[]{:S(2)}, u32[]{:S(2)}) collective-permute-start(f32[128,128]{1,0:T(8,128)S(1)} %add_bitcast_fusion.1), channel_id=1, source_target_pairs={{0,32},{32,64},{64,96},{96,128},{128,160},{160,192},{192,224},{224... | collective-permute-start | bytes 196616 | tf_op jit(solution)/shard_map/ppermute | solution.py:43
  29.6 12.4 %collective-permute-done.1 = f32[128,128]{1,0:T(8,128)S(1)} collective-permute-done((f32[128,128]{1,0:T(8,128)S(1)}, f32[128,128]{1,0:T(8,128)S(1)}, u32[]{:S(2)}, u32[]{:S(2)}) %collective-permute-start.1) | collective-permute-done | bytes 65568 | tf_op jit(solution)/shard_map/ppermute | solution.py:43
  42.0 9.2 %collective-permute-start.2 = (f32[128,128]{1,0:T(8,128)S(1)}, f32[128,128]{1,0:T(8,128)S(1)}, u32[]{:S(2)}, u32[]{:S(2)}) collective-permute-start(f32[128,128]{1,0:T(8,128)S(1)} %add.81), channel_id=1, source_target_pairs={{0,64},{32,96},{64,128},{96,160},{128,192},{160,224},{192,256},{22... | collective-permute-start | bytes 196616 | tf_op jit(solution)/shard_map/ppermute | solution.py:43
  51.2 1.3 collective-permute-done.2
  52.5 9.3 %collective-permute-start.3 = (f32[128,128]{1,0:T(8,128)S(1)}, f32[128,128]{1,0:T(8,128)S(1)}, u32[]{:S(2)}, u32[]{:S(2)}) collective-permute-start(f32[128,128]{1,0:T(8,128)S(1)} %add.83), channel_id=1, source_target_pairs={{0,128},{32,160},{64,192},{96,224},{128,256},{160,288},{192,320},{... | collective-permute-start | bytes 196616 | tf_op jit(solution)/shard_map/ppermute | solution.py:43
  61.8 1.3 collective-permute-done.3
  63.1 5.1 %collective-permute-start.4 = (f32[128,128]{1,0:T(8,128)S(1)}, f32[128,128]{1,0:T(8,128)S(1)}, u32[]{:S(2)}, u32[]{:S(2)}) collective-permute-start(f32[128,128]{1,0:T(8,128)S(1)} %add.85), channel_id=1, source_target_pairs={{0,256},{32,288},{64,320},{96,352},{128,384},{160,416},{192,448},{... | collective-permute-start | bytes 196616 | tf_op jit(solution)/shard_map/ppermute | solution.py:43
  68.2 0.2 convolution_select_fusion.1
  68.5 8.7 %collective-permute-start.6 = (bf16[16,256,128]{2,1,0:T(8,128)(2,1)S(1)}, bf16[16,256,128]{2,1,0:T(8,128)(2,1)S(1)}, u32[]{:S(2)}, u32[]{:S(2)}) collective-permute-start(bf16[16,256,128]{2,1,0:T(8,128)(2,1)S(1)} %all-to-all-done), channel_id=1, source_target_pairs={{0,16},{16,0},{1,17},{17,1},{2,18},{18,2},{3,19},{19,3},{4,20},{20... | collective-permute-start | bytes 3145736 | tf_op jit(solution)/shard_map/ppermute | solution.py:20
  77.1 0.6 add_add_fusion.1
  77.8 3.6 %collective-permute-start.5 = (f32[128,128]{1,0:T(8,128)}, f32[128,128]{1,0:T(8,128)S(1)}, u32[]{:S(2)}, u32[]{:S(2)}) collective-permute-start(f32[128,128]{1,0:T(8,128)} %add_add_fusion.1), channel_id=1, source_target_pairs={{0,16},{16,0},{1,17},{17,1},{2,18},{18,2},{3,19},{19,3},{4,20},{20... | collective-permute-start | bytes 196616 | tf_op jit(solution)/shard_map/ppermute | solution.py:20
  81.4 0.4 convolution_bitcast_fusion.2
  81.9 0.6 collective-permute-done.5
  82.5 0.8 select_bitcast_fusion.5
  83.4 1.3 multiply_reduce_fusion.1
  84.7 1.5 %select_bitcast_fusion.1 = (bf16[16,1,256,128]{3,2,1,0:T(8,128)(2,1)}, bf16[16,1,256,128]{3,2,1,0:T(8,128)(2,1)}) fusion(bf16[16,256,128]{2,1,0:T(8,128)(2,1)S(1)} %all-to-all-done, bf16[16,256,128]{2,1,0:T(8,128)(2,1)S(1)} %collective-permute-done.6, pred[]{:T(512)S(6)} %eq.4), kind=kLoop, calls=%fused_computation.22 | loop fusion | flops 1048576 | bytes 4194305 | tf_op jit(solution)/shard_map/stack | solution.py:62
  86.2 4.1 %reshape.61 = bf16[16,256,2,128]{3,2,1,0:T(2,128)(2,1)} reshape(bf16[4096,256]{1,0:T(8,128)(2,1)} %all-gather.3.cloned.1.call-done) | data formatting | bytes 4194304 | tf_op jit(solution)/shard_map/reshape | solution.py:73
  90.4 2.3 %fusion = f32[256,256,1,1]{1,0,3,2:T(8,128)S(1)} fusion(bf16[16,1,256,128]{3,2,1,0:T(8,128)(2,1)S(1)} %copy-done.4, bf16[16,1,256,128]{3,2,1,0:T(8,128)(2,1)S(1)} %copy-done.3, bf16[16,256,2,128]{3,2,1,0:T(2,128)(2,1)} %reshape.61), kind=kOutput, calls=%fused_computation | convolution fusion | flops 537919488 | bytes 4456448 | tf_op jit(solution)/shard_map/qtrk,qrjk->tj/dot_general | solution.py:71
  92.7 0.1 multiply_reduce_fusion
  92.8 0.1 multiply_convert_fusion
  92.9 0.2 convolution_bitcast_fusion.6
  93.1 1.9 %collective-permute-start.7 = (f32[2,128,128]{2,1,0:T(8,128)S(1)}, f32[2,128,128]{2,1,0:T(8,128)S(1)}, u32[]{:S(2)}, u32[]{:S(2)}) collective-permute-start(f32[2,128,128]{2,1,0:T(8,128)S(1)} %convolution_bitcast_fusion.6), channel_id=1, source_target_pairs={{0,16},{16,0},{1,17},{17,1},{2,18},{18,2},{3,19},{19,3},{4,20},{20... | collective-permute-start | bytes 393224 | tf_op jit(solution)/shard_map/ppermute | solution.py:20
  95.0 1.3 collective-permute-done.7
  96.4 1.4 %collective-permute-start.8 = (f32[128,128]{1,0:T(8,128)S(1)}, f32[128,128]{1,0:T(8,128)S(1)}, u32[]{:S(2)}, u32[]{:S(2)}) collective-permute-start(f32[128,128]{1,0:T(8,128)S(1)} %add_bitcast_fusion), channel_id=1, source_target_pairs={{32,0},{64,32},{96,64},{128,96},{160,128},{192,160},{224,192},{256... | collective-permute-start | bytes 196616 | tf_op jit(solution)/shard_map/ppermute | solution.py:43
  97.8 0.7 fusion.45
  98.5 3.9 %collective-permute-done.8 = f32[128,128]{1,0:T(8,128)S(1)} collective-permute-done((f32[128,128]{1,0:T(8,128)S(1)}, f32[128,128]{1,0:T(8,128)S(1)}, u32[]{:S(2)}, u32[]{:S(2)}) %collective-permute-start.8) | collective-permute-done | bytes 65568 | tf_op jit(solution)/shard_map/ppermute | solution.py:43
  102.4 1.3 collective-permute-start.9
  103.7 0.3 convolution_select_fusion
  104.0 5.1 %collective-permute-done.9 = f32[128,128]{1,0:T(8,128)S(1)} collective-permute-done((f32[128,128]{1,0:T(8,128)S(1)}, f32[128,128]{1,0:T(8,128)S(1)}, u32[]{:S(2)}, u32[]{:S(2)}) %collective-permute-start.9) | collective-permute-done | bytes 65568 | tf_op jit(solution)/shard_map/ppermute | solution.py:43
  109.1 1.3 collective-permute-start.10
  110.4 0.4 convolution_bitcast_fusion.1
  110.8 7.2 %collective-permute-done.10 = f32[128,128]{1,0:T(8,128)S(1)} collective-permute-done((f32[128,128]{1,0:T(8,128)S(1)}, f32[128,128]{1,0:T(8,128)S(1)}, u32[]{:S(2)}, u32[]{:S(2)}) %collective-permute-start.10) | collective-permute-done | bytes 65568 | tf_op jit(solution)/shard_map/ppermute | solution.py:43
  118.0 1.3 collective-permute-start.11
  119.3 0.6 convolution_bitcast_fusion
  120.0 3.1 %collective-permute-done.11 = f32[128,128]{1,0:T(8,128)S(1)} collective-permute-done((f32[128,128]{1,0:T(8,128)S(1)}, f32[128,128]{1,0:T(8,128)S(1)}, u32[]{:S(2)}, u32[]{:S(2)}) %collective-permute-start.11) | collective-permute-done | bytes 65568 | tf_op jit(solution)/shard_map/ppermute | solution.py:43
  123.1 6.8 %collective-permute-start.12 = (f32[128,128]{1,0:T(8,128)S(1)}, f32[128,128]{1,0:T(8,128)S(1)}, u32[]{:S(2)}, u32[]{:S(2)}) collective-permute-start(f32[128,128]{1,0:T(8,128)S(1)} %add_add_fusion), channel_id=1, source_target_pairs={{0,16},{16,0},{1,17},{17,1},{2,18},{18,2},{3,19},{19,3},{4,20},{20... | collective-permute-start | bytes 196616 | tf_op jit(solution)/shard_map/ppermute | solution.py:20
  129.9 0.3 fusion.9
  130.2 0.7 copy.127
  130.9 0.3 fusion.5
  131.2 0.3 fusion.7
  131.5 0.7 bitcast_convert_fusion
  (44 shorter events, 0.2 us)
Async XLA Ops:
  7.2 61.0 %copy-start = (bf16[256,256]{1,0:T(8,128)(2,1)S(1)}, bf16[256,256]{1,0:T(8,128)(2,1)}, u32[]{:S(2)}) copy-start(bf16[256,256]{1,0:T(8,128)(2,1)} %param.5) | copy-start | bytes 393220
  7.2 14.8 %copy-start.1 = (bf16[256,256]{1,0:T(8,128)(2,1)S(1)}, bf16[256,256]{1,0:T(8,128)(2,1)}, u32[]{:S(2)}) copy-start(bf16[256,256]{1,0:T(8,128)(2,1)} %param.6) | copy-start | bytes 393220
  7.2 14.8 %copy-start.2 = (bf16[256,256]{1,0:T(8,128)(2,1)S(1)}, bf16[256,256]{1,0:T(8,128)(2,1)}, u32[]{:S(2)}) copy-start(bf16[256,256]{1,0:T(8,128)(2,1)} %param.7) | copy-start | bytes 393220
  7.2 79.0 %all-gather.3.cloned.1.call-start = ((), (), s32[]{:S(2)}) async-start(), calls=%async_computation.1 | async-start | bytes 2228224 | tf_op jit(solution)/shard_map/all_gather | solution.py:69
  10.0 58.5 %all-to-all-start = ((bf16[16,256,128]{2,1,0:T(8,128)(2,1)}), bf16[16,256,128]{2,1,0:T(8,128)(2,1)S(1)}, u32[]{:S(2)}, u32[]{:S(2)}) async-start(bf16[16,256,128]{2,1,0:T(8,128)(2,1)} %broadcast_in_dim.29), calls=%async_computation | async-start | bytes 2097152 | tf_op jit(solution)/shard_map/all_to_all | solution.py:57
  22.2 3.8 %collective-permute-start = (f32[2,128,128]{2,1,0:T(8,128)S(1)}, f32[2,128,128]{2,1,0:T(8,128)S(1)}, u32[]{:S(2)}, u32[]{:S(2)}) collective-permute-start(f32[2,128,128]{2,1,0:T(8,128)S(1)} %fusion.14), channel_id=1, source_target_pairs={{0,16},{16,0},{1,17},{17,1},{2,18},{18,2},{3,19},{19,3},{4,20},{20... | collective-permute-start | bytes 393224 | tf_op jit(solution)/shard_map/ppermute | solution.py:20
  26.0 37.1 %copy-start.5 = (f32[2,128,128]{2,1,0:T(8,128)}, f32[2,128,128]{2,1,0:T(8,128)S(1)}, u32[]{:S(2)}) copy-start(f32[2,128,128]{2,1,0:T(8,128)S(1)} %collective-permute-done) | copy-start | bytes 393220
  26.0 16.0 %collective-permute-start.1 = (f32[128,128]{1,0:T(8,128)S(1)}, f32[128,128]{1,0:T(8,128)S(1)}, u32[]{:S(2)}, u32[]{:S(2)}) collective-permute-start(f32[128,128]{1,0:T(8,128)S(1)} %add_bitcast_fusion.1), channel_id=1, source_target_pairs={{0,32},{32,64},{64,96},{96,128},{128,160},{160,192},{192,224},{224... | collective-permute-start | bytes 196616 | tf_op jit(solution)/shard_map/ppermute | solution.py:43
  42.0 10.5 %collective-permute-start.2 = (f32[128,128]{1,0:T(8,128)S(1)}, f32[128,128]{1,0:T(8,128)S(1)}, u32[]{:S(2)}, u32[]{:S(2)}) collective-permute-start(f32[128,128]{1,0:T(8,128)S(1)} %add.81), channel_id=1, source_target_pairs={{0,64},{32,96},{64,128},{96,160},{128,192},{160,224},{192,256},{22... | collective-permute-start | bytes 196616 | tf_op jit(solution)/shard_map/ppermute | solution.py:43
  52.5 10.6 %collective-permute-start.3 = (f32[128,128]{1,0:T(8,128)S(1)}, f32[128,128]{1,0:T(8,128)S(1)}, u32[]{:S(2)}, u32[]{:S(2)}) collective-permute-start(f32[128,128]{1,0:T(8,128)S(1)} %add.83), channel_id=1, source_target_pairs={{0,128},{32,160},{64,192},{96,224},{128,256},{160,288},{192,320},{... | collective-permute-start | bytes 196616 | tf_op jit(solution)/shard_map/ppermute | solution.py:43
  61.8 21.6 %copy-start.11 = (pred[256,256]{1,0:T(8,128)(4,1)}, pred[256,256]{1,0:T(8,128)(4,1)S(1)}, u32[]{:S(2)}) copy-start(pred[256,256]{1,0:T(8,128)(4,1)S(1)} %iota_compare_fusion) | copy-start | bytes 196612
  63.1 14.0 %collective-permute-start.4 = (f32[128,128]{1,0:T(8,128)S(1)}, f32[128,128]{1,0:T(8,128)S(1)}, u32[]{:S(2)}, u32[]{:S(2)}) collective-permute-start(f32[128,128]{1,0:T(8,128)S(1)} %add.85), channel_id=1, source_target_pairs={{0,256},{32,288},{64,320},{96,352},{128,384},{160,416},{192,448},{... | collective-permute-start | bytes 196616 | tf_op jit(solution)/shard_map/ppermute | solution.py:43
  68.5 16.3 %collective-permute-start.6 = (bf16[16,256,128]{2,1,0:T(8,128)(2,1)S(1)}, bf16[16,256,128]{2,1,0:T(8,128)(2,1)S(1)}, u32[]{:S(2)}, u32[]{:S(2)}) collective-permute-start(bf16[16,256,128]{2,1,0:T(8,128)(2,1)S(1)} %all-to-all-done), channel_id=1, source_target_pairs={{0,16},{16,0},{1,17},{17,1},{2,18},{18,2},{3,19},{19,3},{4,20},{20... | collective-permute-start | bytes 3145736 | tf_op jit(solution)/shard_map/ppermute | solution.py:20
  77.8 4.7 %collective-permute-start.5 = (f32[128,128]{1,0:T(8,128)}, f32[128,128]{1,0:T(8,128)S(1)}, u32[]{:S(2)}, u32[]{:S(2)}) collective-permute-start(f32[128,128]{1,0:T(8,128)} %add_add_fusion.1), channel_id=1, source_target_pairs={{0,16},{16,0},{1,17},{17,1},{2,18},{18,2},{3,19},{19,3},{4,20},{20... | collective-permute-start | bytes 196616 | tf_op jit(solution)/shard_map/ppermute | solution.py:20
  83.4 1.3 copy-start.7
  83.4 1.3 copy-start.9
  86.2 4.1 %copy-start.3 = (bf16[16,1,256,128]{3,2,1,0:T(8,128)(2,1)S(1)}, bf16[16,1,256,128]{3,2,1,0:T(8,128)(2,1)}, u32[]{:S(2)}) copy-start(bf16[16,1,256,128]{3,2,1,0:T(8,128)(2,1)} %get-tuple-element.3) | copy-start | bytes 3145732
  86.2 4.1 %copy-start.4 = (bf16[16,1,256,128]{3,2,1,0:T(8,128)(2,1)S(1)}, bf16[16,1,256,128]{3,2,1,0:T(8,128)(2,1)}, u32[]{:S(2)}) copy-start(bf16[16,1,256,128]{3,2,1,0:T(8,128)(2,1)} %get-tuple-element.4) | copy-start | bytes 3145732
  92.7 11.0 %copy-start.12 = (pred[256,256]{1,0:T(8,128)(4,1)S(1)}, pred[256,256]{1,0:T(8,128)(4,1)}, u32[]{:S(2)}) copy-start(pred[256,256]{1,0:T(8,128)(4,1)} %copy-done.11) | copy-start | bytes 196612
  93.1 3.2 %collective-permute-start.7 = (f32[2,128,128]{2,1,0:T(8,128)S(1)}, f32[2,128,128]{2,1,0:T(8,128)S(1)}, u32[]{:S(2)}, u32[]{:S(2)}) collective-permute-start(f32[2,128,128]{2,1,0:T(8,128)S(1)} %convolution_bitcast_fusion.6), channel_id=1, source_target_pairs={{0,16},{16,0},{1,17},{17,1},{2,18},{18,2},{3,19},{19,3},{4,20},{20... | collective-permute-start | bytes 393224 | tf_op jit(solution)/shard_map/ppermute | solution.py:20
  96.3 33.5 %copy-start.6 = (f32[2,128,128]{2,1,0:T(8,128)S(1)}, f32[2,128,128]{2,1,0:T(8,128)}, u32[]{:S(2)}) copy-start(f32[2,128,128]{2,1,0:T(8,128)} %copy-done.5) | copy-start | bytes 393220
  96.3 33.5 %copy-start.8 = (f32[1,128,128]{2,1,0:T(8,128)S(1)}, f32[1,128,128]{2,1,0:T(8,128)}, u32[]{:S(2)}) copy-start(f32[1,128,128]{2,1,0:T(8,128)} %copy-done.7) | copy-start | bytes 196612
  96.4 33.5 %copy-start.10 = (f32[1,128,128]{2,1,0:T(8,128)S(1)}, f32[1,128,128]{2,1,0:T(8,128)}, u32[]{:S(2)}) copy-start(f32[1,128,128]{2,1,0:T(8,128)} %copy-done.9) | copy-start | bytes 196612
  96.4 6.0 %collective-permute-start.8 = (f32[128,128]{1,0:T(8,128)S(1)}, f32[128,128]{1,0:T(8,128)S(1)}, u32[]{:S(2)}, u32[]{:S(2)}) collective-permute-start(f32[128,128]{1,0:T(8,128)S(1)} %add_bitcast_fusion), channel_id=1, source_target_pairs={{32,0},{64,32},{96,64},{128,96},{160,128},{192,160},{224,192},{256... | collective-permute-start | bytes 196616 | tf_op jit(solution)/shard_map/ppermute | solution.py:43
  102.4 6.7 %collective-permute-start.9 = (f32[128,128]{1,0:T(8,128)S(1)}, f32[128,128]{1,0:T(8,128)S(1)}, u32[]{:S(2)}, u32[]{:S(2)}) collective-permute-start(f32[128,128]{1,0:T(8,128)S(1)} %add.93), channel_id=1, source_target_pairs={{64,0},{96,32},{128,64},{160,96},{192,128},{224,160},{256,192},{28... | collective-permute-start | bytes 196616 | tf_op jit(solution)/shard_map/ppermute | solution.py:43
  109.1 8.9 %collective-permute-start.10 = (f32[128,128]{1,0:T(8,128)S(1)}, f32[128,128]{1,0:T(8,128)S(1)}, u32[]{:S(2)}, u32[]{:S(2)}) collective-permute-start(f32[128,128]{1,0:T(8,128)S(1)} %add.95), channel_id=1, source_target_pairs={{128,0},{160,32},{192,64},{224,96},{256,128},{288,160},{320,192},{... | collective-permute-start | bytes 196616 | tf_op jit(solution)/shard_map/ppermute | solution.py:43
  118.0 5.0 %collective-permute-start.11 = (f32[128,128]{1,0:T(8,128)S(1)}, f32[128,128]{1,0:T(8,128)S(1)}, u32[]{:S(2)}, u32[]{:S(2)}) collective-permute-start(f32[128,128]{1,0:T(8,128)S(1)} %add.97), channel_id=1, source_target_pairs={{256,0},{288,32},{320,64},{352,96},{384,128},{416,160},{448,192},{... | collective-permute-start | bytes 196616 | tf_op jit(solution)/shard_map/ppermute | solution.py:43
  123.1 7.8 %collective-permute-start.12 = (f32[128,128]{1,0:T(8,128)S(1)}, f32[128,128]{1,0:T(8,128)S(1)}, u32[]{:S(2)}, u32[]{:S(2)}) collective-permute-start(f32[128,128]{1,0:T(8,128)S(1)} %add_add_fusion), channel_id=1, source_target_pairs={{0,16},{16,0},{1,17},{17,1},{2,18},{18,2},{3,19},{19,3},{4,20},{20... | collective-permute-start | bytes 196616 | tf_op jit(solution)/shard_map/ppermute | solution.py:20
Sparse Core Ops, SparseCore 0:
  11.0 69.8 all-gather.2

commit v14 on v11

--- a/solution.py
+++ b/solution.py
@@ -1,6 +1,7 @@
 import jax
 import jax.numpy as jnp
 from jax import lax
+from jax.experimental.layout import Layout, with_layout_constraint
 from jax.sharding import Mesh
 from jax.sharding import PartitionSpec as P
 
@@ -146,10 +147,10 @@
     grad_key = grad_key + jnp.einsum("she,hde->shd", value_wide, adjoint, precision=highest)
     grad_value = jnp.einsum("hts,the->she", weights, grad_wide, precision=highest)
     grad_value = grad_value + jnp.einsum("shd,hde->she", key_wide, adjoint, precision=highest)
-    return (
-        grad_query.reshape(tok_rows, feat_width).astype(jnp.bfloat16),
-        grad_key.reshape(tok_rows, feat_width).astype(jnp.bfloat16),
-        grad_value.reshape(tok_rows, feat_width).astype(jnp.bfloat16),
+    row_major = Layout(major_to_minor=(0, 1))
+    return tuple(
+        with_layout_constraint(out.reshape(tok_rows, feat_width), row_major).astype(jnp.bfloat16)
+        for out in (grad_query, grad_key, grad_value)
     )
 
 

time: 139 us -> 137 us (0.986); the launches traced: 137 us -> 137 us
  other arithmetic: 3.19 us -> 1.72 us
    unnamed x22 -> x23, local copies, waits for them, and re-layouts: 4.09 us -> 1.82 us
    ppermute x3, waiting for transfers between devices: 19 us -> 21 us  [merged_scan(): arrived = lax.ppermute(window, CHIPS, pairs)]
  transfers between devices with their start and end apart: 16 -> 16, of which waited for: 9 -> 10; matrix products, arithmetic and copies ran while one was open for 8% -> 6% of each run, Pallas kernels for 0% -> 0%
where the time goes in v14:
time: 137 us
  starting transfers between devices  67.7 us (49%)
  waiting for transfers between devices  39.3 us (29%)
  between operations  14.5 us (11%)
  matrix products  8.18 us (6%)
  local copies, waits for them, and re-layouts  5.29 us (4%)
  other arithmetic  1.72 us (1%)
    ppermute x4, starting transfers between devices, ctx_scan(): arrived = lax.ppermute(window, CHIPS, pairs)  27.6 us
    ppermute x5, starting transfers between devices, swap_cores(): return lax.ppermute(value, 'core', [(0, 1), (1, 0)])  21.6 us
    ppermute x3, waiting for transfers between devices, merged_scan(): arrived = lax.ppermute(window, CHIPS, pairs)  21 us
    ppermute x4, waiting for transfers between devices, ctx_scan(): arrived = lax.ppermute(window, CHIPS, pairs)  14.3 us
    all_to_all x1, starting transfers between devices, gather_columns(): mine = lax.all_to_all(spread, CHIPS, 0, 0, tiled=True)  12 us
    ppermute x3, starting transfers between devices, merged_scan(): arrived = lax.ppermute(window, CHIPS, pairs)  3.88 us
    dot_general x1, matrix products, local(): jnp.einsum('tqrk,qrjk->tj', full_rows.reshape(tok_rows, columns.shape[0],...  2.94 us
  transfers between devices with their start and end apart: 16, of which 10 were waited for; matrix products, arithmetic and copies ran while one was open for 6% of the time, Pallas kernels for 0%

profile of v14, /device:TPU:1, one launch (start us, length us, event | category | flops | bytes accessed | tf_op | source)
XLA Modules:
  0.0 136.7 jit_solution(11063888398832650806)
XLA Ops:
  7.2 0.0 copy-start
  7.2 0.0 all-gather.2.cloned.1.call-start
  7.2 1.8 %copy.41 = bf16[256,256]{0,1:T(8,128)(2,1)} copy(bf16[256,256]{1,0:T(8,128)(2,1)} %param.8) | data formatting | bytes 262144 | tf_op args[3]
  9.0 0.0 all-gather.2.cloned.1.call-update
  9.0 2.0 %broadcast_in_dim.29 = bf16[16,256,128]{2,1,0:T(8,128)(2,1)} broadcast(bf16[256,128]{1,0:T(8,128)(2,1)} %param.9), dimensions={1,2} | broadcast | bytes 1114112 | tf_op jit(solution)/shard_map/broadcast_in_dim | solution.py:89
  11.1 12.0 %all-to-all-start = ((bf16[16,256,128]{2,1,0:T(8,128)(2,1)}), bf16[16,256,128]{2,1,0:T(8,128)(2,1)S(1)}, u32[]{:S(2)}, u32[]{:S(2)}) async-start(bf16[16,256,128]{2,1,0:T(8,128)(2,1)} %broadcast_in_dim.29), calls=%async_computation | async-start | bytes 2097152 | tf_op jit(solution)/shard_map/all_to_all | solution.py:90
  23.1 0.2 fusion.13
  23.3 2.9 %collective-permute-start = (f32[2,128,128]{2,1,0:T(8,128)S(1)}, f32[2,128,128]{2,1,0:T(8,128)S(1)}, u32[]{:S(2)}, u32[]{:S(2)}) collective-permute-start(f32[2,128,128]{2,1,0:T(8,128)S(1)} %fusion.13), channel_id=1, source_target_pairs={{0,16},{16,0},{1,17},{17,1},{2,18},{18,2},{3,19},{19,3},{4,20},{20... | collective-permute-start | bytes 393224 | tf_op jit(solution)/shard_map/ppermute | solution.py:20
  26.2 1.0 collective-permute-done
  27.2 3.5 %collective-permute-start.1 = (f32[128,128]{1,0:T(8,128)S(1)}, f32[128,128]{1,0:T(8,128)S(1)}, u32[]{:S(2)}, u32[]{:S(2)}) collective-permute-start(f32[128,128]{1,0:T(8,128)S(1)} %add_bitcast_fusion), channel_id=1, source_target_pairs={{0,32},{32,64},{64,96},{96,128},{128,160},{160,192},{192,224},{224... | collective-permute-start | bytes 196616 | tf_op jit(solution)/shard_map/ppermute | solution.py:43
  30.7 11.8 %collective-permute-done.1 = f32[128,128]{1,0:T(8,128)S(1)} collective-permute-done((f32[128,128]{1,0:T(8,128)S(1)}, f32[128,128]{1,0:T(8,128)S(1)}, u32[]{:S(2)}, u32[]{:S(2)}) %collective-permute-start.1) | collective-permute-done | bytes 65568 | tf_op jit(solution)/shard_map/ppermute | solution.py:43
  42.5 9.3 %collective-permute-start.2 = (f32[128,128]{1,0:T(8,128)S(1)}, f32[128,128]{1,0:T(8,128)S(1)}, u32[]{:S(2)}, u32[]{:S(2)}) collective-permute-start(f32[128,128]{1,0:T(8,128)S(1)} %add.91), channel_id=1, source_target_pairs={{0,64},{32,96},{64,128},{96,160},{128,192},{160,224},{192,256},{22... | collective-permute-start | bytes 196616 | tf_op jit(solution)/shard_map/ppermute | solution.py:43
  51.8 1.3 collective-permute-done.2
  53.1 10.8 %collective-permute-start.3 = (f32[128,128]{1,0:T(8,128)S(1)}, f32[128,128]{1,0:T(8,128)S(1)}, u32[]{:S(2)}, u32[]{:S(2)}) collective-permute-start(f32[128,128]{1,0:T(8,128)S(1)} %add.93), channel_id=1, source_target_pairs={{0,128},{32,160},{64,192},{96,224},{128,256},{160,288},{192,320},{... | collective-permute-start | bytes 196616 | tf_op jit(solution)/shard_map/ppermute | solution.py:43
  63.9 0.0 copy-start.9
  64.0 1.3 collective-permute-done.3
  65.2 4.0 %collective-permute-start.4 = (f32[128,128]{1,0:T(8,128)S(1)}, f32[128,128]{1,0:T(8,128)S(1)}, u32[]{:S(2)}, u32[]{:S(2)}) collective-permute-start(f32[128,128]{1,0:T(8,128)S(1)} %add.95), channel_id=1, source_target_pairs={{0,256},{32,288},{64,320},{96,352},{128,384},{160,416},{192,448},{... | collective-permute-start | bytes 196616 | tf_op jit(solution)/shard_map/ppermute | solution.py:43
  69.2 0.2 convolution_select_fusion.1
  69.5 8.1 %collective-permute-start.6 = (bf16[16,256,128]{2,1,0:T(8,128)(2,1)S(1)}, bf16[16,256,128]{2,1,0:T(8,128)(2,1)S(1)}, u32[]{:S(2)}, u32[]{:S(2)}) collective-permute-start(bf16[16,256,128]{2,1,0:T(8,128)(2,1)S(1)} %all-to-all-done), channel_id=1, source_target_pairs={{0,16},{16,0},{1,17},{17,1},{2,18},{18,2},{3,19},{19,3},{4,20},{20... | collective-permute-start | bytes 3145736 | tf_op jit(solution)/shard_map/ppermute | solution.py:20
  77.6 3.9 %collective-permute-start.5 = (f32[128,128]{1,0:T(8,128)S(1)}, f32[128,128]{1,0:T(8,128)S(1)}, u32[]{:S(2)}, u32[]{:S(2)}) collective-permute-start(f32[128,128]{1,0:T(8,128)S(1)} %add_add_fusion.1), channel_id=1, source_target_pairs={{0,16},{16,0},{1,17},{17,1},{2,18},{18,2},{3,19},{19,3},{4,20},{20... | collective-permute-start | bytes 196616 | tf_op jit(solution)/shard_map/ppermute | solution.py:20
  81.5 0.4 convolution_bitcast_fusion.2
  81.9 0.4 collective-permute-done.5
  82.4 1.3 multiply_reduce_fusion.1
  83.7 1.5 %select_bitcast_fusion.1 = (bf16[16,1,256,128]{3,2,1,0:T(8,128)(2,1)}, bf16[16,1,256,128]{3,2,1,0:T(8,128)(2,1)}) fusion(bf16[16,256,128]{2,1,0:T(8,128)(2,1)S(1)} %all-to-all-done, bf16[16,256,128]{2,1,0:T(8,128)(2,1)S(1)} %collective-permute-done.6, pred[]{:T(512)S(6)} %eq.4), kind=kLoop, calls=%fused_computation.20 | loop fusion | flops 1048576 | bytes 4194305 | tf_op jit(solution)/shard_map/stack | solution.py:95
  85.2 2.9 %fusion = f32[256,256,1,1]{1,0,3,2:T(8,128)S(1)} fusion(bf16[256,16,2,128]{0,3,2,1:T(8,128)(2,1)} %bitcast.156, bf16[16,1,256,128]{3,2,1,0:T(8,128)(2,1)} %get-tuple-element.6, bf16[16,1,256,128]{3,2,1,0:T(8,128)(2,1)} %get-tuple-element.5), kind=kOutput, calls=%fused_computation | convolution fusion | flops 537919488 | bytes 4456448 | tf_op jit(solution)/shard_map/tqrk,qrjk->tj/dot_general | solution.py:104
  88.2 0.1 multiply_reduce_fusion
  88.3 0.2 fusion.19
  88.5 1.3 collective-permute-start.7
  89.8 1.3 collective-permute-start.8
  91.1 1.9 %collective-permute-start.9 = (f32[2,128,128]{2,1,0:T(8,128)S(1)}, f32[2,128,128]{2,1,0:T(8,128)S(1)}, u32[]{:S(2)}, u32[]{:S(2)}) collective-permute-start(f32[2,128,128]{2,1,0:T(8,128)S(1)} %bitcast.154), channel_id=1, source_target_pairs={{0,16},{16,0},{1,17},{17,1},{2,18},{18,2},{3,19},{19,3},{4,20},{20... | collective-permute-start | bytes 393224 | tf_op jit(solution)/shard_map/ppermute | solution.py:20
  93.0 0.7 fusion.46
  93.7 0.6 collective-permute-done.7
  94.3 1.9 %collective-permute-done.8 = f32[128,128]{1,0:T(8,128)S(1)} collective-permute-done((f32[128,128]{1,0:T(8,128)S(1)}, f32[128,128]{1,0:T(8,128)S(1)}, u32[]{:S(2)}, u32[]{:S(2)}) %collective-permute-start.8) | collective-permute-done | bytes 65568 | tf_op jit(solution)/shard_map/ppermute | solution.py:63
  96.3 1.3 collective-permute-start.10
  97.6 0.3 convolution_select_fusion
  97.9 5.6 %collective-permute-done.10 = f32[128,128]{1,0:T(8,128)S(1)} collective-permute-done((f32[128,128]{1,0:T(8,128)S(1)}, f32[128,128]{1,0:T(8,128)S(1)}, u32[]{:S(2)}, u32[]{:S(2)}) %collective-permute-start.10) | collective-permute-done | bytes 65568 | tf_op jit(solution)/shard_map/ppermute | solution.py:76
  103.5 1.3 collective-permute-start.11
  104.8 0.7 convolution_bitcast_fusion
  105.4 7.4 %collective-permute-done.11 = f32[128,128]{1,0:T(8,128)S(1)} collective-permute-done((f32[128,128]{1,0:T(8,128)S(1)}, f32[128,128]{1,0:T(8,128)S(1)}, u32[]{:S(2)}, u32[]{:S(2)}) %collective-permute-start.11) | collective-permute-done | bytes 65568 | tf_op jit(solution)/shard_map/ppermute | solution.py:76
  112.8 1.3 collective-permute-start.12
  114.1 0.4 convolution_bitcast_fusion.1
  114.5 8.1 %collective-permute-done.12 = f32[128,128]{1,0:T(8,128)S(1)} collective-permute-done((f32[128,128]{1,0:T(8,128)S(1)}, f32[128,128]{1,0:T(8,128)S(1)}, u32[]{:S(2)}, u32[]{:S(2)}) %collective-permute-start.12) | collective-permute-done | bytes 65568 | tf_op jit(solution)/shard_map/ppermute | solution.py:76
  122.6 4.9 %collective-permute-start.13 = (f32[128,128]{1,0:T(8,128)S(1)}, f32[128,128]{1,0:T(8,128)S(1)}, u32[]{:S(2)}, u32[]{:S(2)}) collective-permute-start(f32[128,128]{1,0:T(8,128)S(1)} %add_add_fusion), channel_id=1, source_target_pairs={{0,16},{16,0},{1,17},{17,1},{2,18},{18,2},{3,19},{19,3},{4,20},{20... | collective-permute-start | bytes 196616 | tf_op jit(solution)/shard_map/ppermute | solution.py:20
  127.5 0.3 fusion.8
  127.8 0.7 copy.128
  128.5 0.3 fusion.6
  128.8 0.3 fusion.4
  129.1 0.7 bitcast_convert_fusion
  (42 shorter events, 0.3 us)
Async XLA Ops:
  7.2 62.1 %copy-start = (bf16[256,256]{1,0:T(8,128)(2,1)S(1)}, bf16[256,256]{1,0:T(8,128)(2,1)}, u32[]{:S(2)}) copy-start(bf16[256,256]{1,0:T(8,128)(2,1)} %param.5) | copy-start | bytes 393220
  7.2 15.9 %copy-start.2 = (bf16[256,256]{1,0:T(8,128)(2,1)S(1)}, bf16[256,256]{1,0:T(8,128)(2,1)}, u32[]{:S(2)}) copy-start(bf16[256,256]{1,0:T(8,128)(2,1)} %param.6) | copy-start | bytes 393220
  7.2 15.9 %copy-start.1 = (bf16[256,256]{1,0:T(8,128)(2,1)S(1)}, bf16[256,256]{1,0:T(8,128)(2,1)}, u32[]{:S(2)}) copy-start(bf16[256,256]{1,0:T(8,128)(2,1)} %param.7) | copy-start | bytes 393220
  7.2 78.0 %all-gather.2.cloned.1.call-start = ((), (), s32[]{:S(2)}) async-start(), calls=%async_computation.1 | async-start | bytes 2228224 | tf_op jit(solution)/shard_map/all_gather | solution.py:102
  11.1 58.4 %all-to-all-start = ((bf16[16,256,128]{2,1,0:T(8,128)(2,1)}), bf16[16,256,128]{2,1,0:T(8,128)(2,1)S(1)}, u32[]{:S(2)}, u32[]{:S(2)}) async-start(bf16[16,256,128]{2,1,0:T(8,128)(2,1)} %broadcast_in_dim.29), calls=%async_computation | async-start | bytes 2097152 | tf_op jit(solution)/shard_map/all_to_all | solution.py:90
  23.3 3.8 %collective-permute-start = (f32[2,128,128]{2,1,0:T(8,128)S(1)}, f32[2,128,128]{2,1,0:T(8,128)S(1)}, u32[]{:S(2)}, u32[]{:S(2)}) collective-permute-start(f32[2,128,128]{2,1,0:T(8,128)S(1)} %fusion.13), channel_id=1, source_target_pairs={{0,16},{16,0},{1,17},{17,1},{2,18},{18,2},{3,19},{19,3},{4,20},{20... | collective-permute-start | bytes 393224 | tf_op jit(solution)/shard_map/ppermute | solution.py:20
  27.1 38.1 %copy-start.3 = (f32[2,128,128]{2,1,0:T(8,128)}, f32[2,128,128]{2,1,0:T(8,128)S(1)}, u32[]{:S(2)}) copy-start(f32[2,128,128]{2,1,0:T(8,128)S(1)} %collective-permute-done) | copy-start | bytes 393220
  27.2 15.3 %collective-permute-start.1 = (f32[128,128]{1,0:T(8,128)S(1)}, f32[128,128]{1,0:T(8,128)S(1)}, u32[]{:S(2)}, u32[]{:S(2)}) collective-permute-start(f32[128,128]{1,0:T(8,128)S(1)} %add_bitcast_fusion), channel_id=1, source_target_pairs={{0,32},{32,64},{64,96},{96,128},{128,160},{160,192},{192,224},{224... | collective-permute-start | bytes 196616 | tf_op jit(solution)/shard_map/ppermute | solution.py:43
  42.5 10.6 %collective-permute-start.2 = (f32[128,128]{1,0:T(8,128)S(1)}, f32[128,128]{1,0:T(8,128)S(1)}, u32[]{:S(2)}, u32[]{:S(2)}) collective-permute-start(f32[128,128]{1,0:T(8,128)S(1)} %add.91), channel_id=1, source_target_pairs={{0,64},{32,96},{64,128},{96,160},{128,192},{160,224},{192,256},{22... | collective-permute-start | bytes 196616 | tf_op jit(solution)/shard_map/ppermute | solution.py:43
  53.1 12.1 %collective-permute-start.3 = (f32[128,128]{1,0:T(8,128)S(1)}, f32[128,128]{1,0:T(8,128)S(1)}, u32[]{:S(2)}, u32[]{:S(2)}) collective-permute-start(f32[128,128]{1,0:T(8,128)S(1)} %add.93), channel_id=1, source_target_pairs={{0,128},{32,160},{64,192},{96,224},{128,256},{160,288},{192,320},{... | collective-permute-start | bytes 196616 | tf_op jit(solution)/shard_map/ppermute | solution.py:43
  63.9 5.3 %copy-start.9 = (pred[256,256]{1,0:T(8,128)(4,1)}, pred[256,256]{1,0:T(8,128)(4,1)S(1)}, u32[]{:S(2)}) copy-start(pred[256,256]{1,0:T(8,128)(4,1)S(1)} %iota_compare_fusion) | copy-start | bytes 196612
  65.2 12.3 %collective-permute-start.4 = (f32[128,128]{1,0:T(8,128)S(1)}, f32[128,128]{1,0:T(8,128)S(1)}, u32[]{:S(2)}, u32[]{:S(2)}) collective-permute-start(f32[128,128]{1,0:T(8,128)S(1)} %add.95), channel_id=1, source_target_pairs={{0,256},{32,288},{64,320},{96,352},{128,384},{160,416},{192,448},{... | collective-permute-start | bytes 196616 | tf_op jit(solution)/shard_map/ppermute | solution.py:43
  69.5 14.3 %collective-permute-start.6 = (bf16[16,256,128]{2,1,0:T(8,128)(2,1)S(1)}, bf16[16,256,128]{2,1,0:T(8,128)(2,1)S(1)}, u32[]{:S(2)}, u32[]{:S(2)}) collective-permute-start(bf16[16,256,128]{2,1,0:T(8,128)(2,1)S(1)} %all-to-all-done), channel_id=1, source_target_pairs={{0,16},{16,0},{1,17},{17,1},{2,18},{18,2},{3,19},{19,3},{4,20},{20... | collective-permute-start | bytes 3145736 | tf_op jit(solution)/shard_map/ppermute | solution.py:20
  77.6 4.8 %collective-permute-start.5 = (f32[128,128]{1,0:T(8,128)S(1)}, f32[128,128]{1,0:T(8,128)S(1)}, u32[]{:S(2)}, u32[]{:S(2)}) collective-permute-start(f32[128,128]{1,0:T(8,128)S(1)} %add_add_fusion.1), channel_id=1, source_target_pairs={{0,16},{16,0},{1,17},{17,1},{2,18},{18,2},{3,19},{19,3},{4,20},{20... | collective-permute-start | bytes 196616 | tf_op jit(solution)/shard_map/ppermute | solution.py:20
  82.4 1.3 copy-start.5
  82.4 1.3 copy-start.7
  88.1 9.4 %copy-start.10 = (pred[256,256]{1,0:T(8,128)(4,1)S(1)}, pred[256,256]{1,0:T(8,128)(4,1)}, u32[]{:S(2)}) copy-start(pred[256,256]{1,0:T(8,128)(4,1)} %copy-done.9) | copy-start | bytes 196612
  88.5 5.8 %collective-permute-start.7 = (f32[128,128]{1,0:T(8,128)S(1)}, f32[128,128]{1,0:T(8,128)S(1)}, u32[]{:S(2)}, u32[]{:S(2)}) collective-permute-start(f32[128,128]{1,0:T(8,128)S(1)} %get-tuple-element.10), channel_id=1, source_target_pairs={{32,0},{64,32},{96,64},{128,96},{160,128},{192,160},{224,192},{256... | collective-permute-start | bytes 196616 | tf_op jit(solution)/shard_map/ppermute | solution.py:62
  89.8 6.4 %collective-permute-start.8 = (f32[128,128]{1,0:T(8,128)S(1)}, f32[128,128]{1,0:T(8,128)S(1)}, u32[]{:S(2)}, u32[]{:S(2)}) collective-permute-start(f32[128,128]{1,0:T(8,128)S(1)} %get-tuple-element.9), channel_id=1, source_target_pairs={{32,16},{48,0},{64,48},{80,32},{96,80},{112,64},{128,112},{144,96}... | collective-permute-start | bytes 196616 | tf_op jit(solution)/shard_map/ppermute | solution.py:63
  91.1 5.1 %collective-permute-start.9 = (f32[2,128,128]{2,1,0:T(8,128)S(1)}, f32[2,128,128]{2,1,0:T(8,128)S(1)}, u32[]{:S(2)}, u32[]{:S(2)}) collective-permute-start(f32[2,128,128]{2,1,0:T(8,128)S(1)} %bitcast.154), channel_id=1, source_target_pairs={{0,16},{16,0},{1,17},{17,1},{2,18},{18,2},{3,19},{19,3},{4,20},{20... | collective-permute-start | bytes 393224 | tf_op jit(solution)/shard_map/ppermute | solution.py:20
  93.7 33.8 %copy-start.4 = (f32[2,128,128]{2,1,0:T(8,128)S(1)}, f32[2,128,128]{2,1,0:T(8,128)}, u32[]{:S(2)}) copy-start(f32[2,128,128]{2,1,0:T(8,128)} %copy-done.3) | copy-start | bytes 393220
  93.7 33.8 %copy-start.6 = (f32[1,128,128]{2,1,0:T(8,128)S(1)}, f32[1,128,128]{2,1,0:T(8,128)}, u32[]{:S(2)}) copy-start(f32[1,128,128]{2,1,0:T(8,128)} %copy-done.5) | copy-start | bytes 196612
  93.7 33.8 %copy-start.8 = (f32[1,128,128]{2,1,0:T(8,128)S(1)}, f32[1,128,128]{2,1,0:T(8,128)}, u32[]{:S(2)}) copy-start(f32[1,128,128]{2,1,0:T(8,128)} %copy-done.7) | copy-start | bytes 196612
  96.3 7.2 %collective-permute-start.10 = (f32[128,128]{1,0:T(8,128)S(1)}, f32[128,128]{1,0:T(8,128)S(1)}, u32[]{:S(2)}, u32[]{:S(2)}) collective-permute-start(f32[128,128]{1,0:T(8,128)S(1)} %get-tuple-element.3), channel_id=1, source_target_pairs={{64,0},{96,32},{128,64},{160,96},{192,128},{224,160},{256,192},{28... | collective-permute-start | bytes 196616 | tf_op jit(solution)/shard_map/ppermute | solution.py:76
  103.5 9.3 %collective-permute-start.11 = (f32[128,128]{1,0:T(8,128)S(1)}, f32[128,128]{1,0:T(8,128)S(1)}, u32[]{:S(2)}, u32[]{:S(2)}) collective-permute-start(f32[128,128]{1,0:T(8,128)S(1)} %add.107), channel_id=1, source_target_pairs={{128,0},{160,32},{192,64},{224,96},{256,128},{288,160},{320,192},{... | collective-permute-start | bytes 196616 | tf_op jit(solution)/shard_map/ppermute | solution.py:76
  112.8 9.7 %collective-permute-start.12 = (f32[128,128]{1,0:T(8,128)S(1)}, f32[128,128]{1,0:T(8,128)S(1)}, u32[]{:S(2)}, u32[]{:S(2)}) collective-permute-start(f32[128,128]{1,0:T(8,128)S(1)} %add.109), channel_id=1, source_target_pairs={{256,0},{288,32},{320,64},{352,96},{384,128},{416,160},{448,192},{... | collective-permute-start | bytes 196616 | tf_op jit(solution)/shard_map/ppermute | solution.py:76
  122.6 5.9 %collective-permute-start.13 = (f32[128,128]{1,0:T(8,128)S(1)}, f32[128,128]{1,0:T(8,128)S(1)}, u32[]{:S(2)}, u32[]{:S(2)}) collective-permute-start(f32[128,128]{1,0:T(8,128)S(1)} %add_add_fusion), channel_id=1, source_target_pairs={{0,16},{16,0},{1,17},{17,1},{2,18},{18,2},{3,19},{19,3},{4,20},{20... | collective-permute-start | bytes 196616 | tf_op jit(solution)/shard_map/ppermute | solution.py:20
Sparse Core Ops, SparseCore 0:
  11.6 69.5 all-gather.1
